TPU v7x, 256 devices: a whole 4x4x8 slice. The times are simulated.
256 devices in a mesh: dp: 8 (over x, core), expert: 16 (over y, z_hi), tensor: 2 (over z_lo).
Axes of the slice: x: 4, y: 4, z: 8 (z_hi: 4, z_lo: 2; z = z_hi * 2 + z_lo), core: 2. Of those that a mesh axis runs over, the one named last changes fastest.
Arguments:
- tokens: bfloat16 [1024, 7168], P(('dp', 'expert'), 'tensor'), may hold values from -6 to 6
- upstream: bfloat16 [1024, 7168], P(('dp', 'expert'), 'tensor'), may hold values from -3 to 3
- probs: bfloat16 [1024, 8], P(('dp', 'expert')), may hold values from 0.049804688 to 0.59765625
- routing: int32 [1024, 8], P(('dp', 'expert')), may hold values from 0 to 15, all different within a row; in each aligned block of 8 rows (0 to 7, 8 to 15, ...) at most 5 rows name the same one
- row_rollout: int32 [1024], P(('dp', 'expert')), may hold values from 0 to 255
- group_ids: int32 [256], replicated, may hold values from 0 to 31
- rewards: int32 [256], replicated, may hold values from 0 to 1
- w_gate: bfloat16 [16, 7168, 2048], P('expert', None, ('dp', 'tensor')), may hold values from -0.0625 to 0.0625
- w_up: bfloat16 [16, 7168, 2048], P('expert', None, ('dp', 'tensor')), may hold values from -0.0625 to 0.0625
- w_down: bfloat16 [16, 2048, 7168], P('expert', ('dp', 'tensor')), may hold values from -0.125 to 0.125
Outputs:
- input_grad: bfloat16 [1024, 7168], P(('dp', 'expert'), 'tensor')
- route_grad: bfloat16 [1024, 8], P(('dp', 'expert'))
- grad_gate: bfloat16 [16, 7168, 2048], P('expert', None, ('dp', 'tensor'))
- grad_up: bfloat16 [16, 7168, 2048], P('expert', None, ('dp', 'tensor'))
- grad_down: bfloat16 [16, 2048, 7168], P('expert', ('dp', 'tensor'))
Inputs may be any that keep to these rules, and one draw needn't show every extreme that they name: `routing`: each row names 8 different experts. Within each aligned block of 8 rows (the tokens of one index pair of dp and expert) no expert is named by more than 5 rows, a bound that some block reaches.
All inputs are finite; a program needn't handle non-finite values.
Results may differ from a plain program's by a relative error of at most 0.025.
Values may be sent and summed in bfloat16 or wider, within the bound.
No kernel may reach another device: no remote copies, remote signals or barrier semaphores. Data moves between devices by JAX's collectives and lax.ppermute only.
A program may use at most 128 MiB of HBM per device.

v0:
```python
import jax
import jax.numpy as jnp
from jax import lax
from jax.sharding import PartitionSpec as P


def advantages(row_rollout, group_ids, rewards):
    same_group = (group_ids[:, None] == group_ids[None, :]).astype(jnp.float32)
    reward_values = rewards.astype(jnp.float32)
    group_total = jnp.dot(same_group, reward_values, precision=lax.Precision.HIGHEST)
    group_count = jnp.sum(same_group, axis=1)
    per_rollout = reward_values - group_total / group_count
    member = (
        row_rollout[:, None] == jnp.arange(per_rollout.shape[0], dtype=jnp.int32)[None, :]
    ).astype(jnp.float32)
    return jnp.dot(member, per_rollout, precision=lax.Precision.HIGHEST)


def selection(routing, probs, experts, capacity):
    route_hits = (
        routing[:, :, None] == jnp.arange(experts, dtype=jnp.int32)[None, None, :]
    ).astype(jnp.float32)
    occupied = jnp.sum(route_hits, axis=1)
    weight = jnp.einsum("rke,rk->re", route_hits, probs.astype(jnp.float32))
    before = jnp.cumsum(occupied, axis=0) - occupied
    slot_index = jnp.arange(capacity, dtype=jnp.float32)
    chosen = occupied.T[:, None, :] * (before.T[:, None, :] == slot_index[None, :, None]).astype(
        jnp.float32
    )
    return (route_hits, weight, chosen)


def shards(tokens, upstream, probs, routing, row_rollout, group_ids, rewards, w_gate, w_up, w_down):
    experts = lax.axis_size("expert")
    dp_size = lax.axis_size("dp")
    tensor_size = lax.axis_size("tensor")
    group_rows, features = tokens.shape
    routes_per_row = routing.shape[1]
    capacity = min(group_rows, 5 * group_rows * routes_per_row // (4 * experts))
    hidden_width = w_gate.shape[2]
    slots = experts * capacity
    advantage = advantages(row_rollout, group_ids, rewards)
    cotangent = (advantage[:, None] * upstream.astype(jnp.float32)).astype(jnp.bfloat16)
    route_hits, weight, chosen = selection(routing, probs, experts, capacity)
    chosen_half = chosen.astype(jnp.bfloat16)
    packed_rows = jnp.einsum(
        "ecr,rf->ecf", chosen_half, tokens, preferred_element_type=jnp.float32
    ).astype(jnp.bfloat16)
    packed_upstream = jnp.einsum(
        "ecr,rf->ecf", chosen_half, cotangent, preferred_element_type=jnp.float32
    ).astype(jnp.bfloat16)
    packed_prob = jnp.einsum("ecr,re->ec", chosen, weight).astype(jnp.bfloat16)
    arrived = (
        lax.all_to_all(packed_rows, "expert", split_axis=0, concat_axis=0, tiled=True),
        lax.all_to_all(packed_upstream, "expert", split_axis=0, concat_axis=0, tiled=True),
        lax.all_to_all(packed_prob, "expert", split_axis=0, concat_axis=0, tiled=True),
    )
    gathered = (
        lax.all_gather(
            arrived[0].reshape(1, slots, features), ("dp", "tensor"), axis=0, tiled=True
        ),
        lax.all_gather(
            arrived[1].reshape(1, slots, features), ("dp", "tensor"), axis=0, tiled=True
        ),
        lax.all_gather(arrived[2].reshape(1, slots), ("dp", "tensor"), axis=0, tiled=True),
    )
    rows_in = gathered[0].reshape(dp_size, tensor_size, experts, capacity, features)
    rows_back = gathered[1].reshape(dp_size, tensor_size, experts, capacity, features)
    slot_prob = gathered[2].reshape(dp_size, tensor_size, experts, capacity)[:, 0]
    layout = "dtecf"
    weights_in = jnp.concatenate([w_gate[0], w_up[0]], axis=1).reshape(
        tensor_size, features, 2 * hidden_width
    )
    weights_out = w_down[0].reshape(hidden_width, tensor_size, features)
    both = jnp.einsum(
        layout + ",tfk->deck", rows_in, weights_in, preferred_element_type=jnp.float32
    )
    gate = both[..., :hidden_width]
    up_part = both[..., hidden_width:]
    back_hidden = jnp.einsum(
        layout + ",htf->dech", rows_back, weights_out, preferred_element_type=jnp.float32
    )
    sigmoid_gate = jax.nn.sigmoid(gate)
    active = gate * sigmoid_gate
    hidden = (active * up_part).astype(jnp.bfloat16)
    hidden_wide = lax.optimization_barrier(hidden).astype(jnp.float32)
    route_part = jnp.sum(hidden_wide * back_hidden, axis=-1)
    scale = slot_prob.astype(jnp.float32)[..., None]
    scaled = scale * back_hidden
    grad_gate_in = scaled * up_part * sigmoid_gate * (1.0 + gate * (1.0 - sigmoid_gate))
    grad_up_in = scaled * active
    grad_inner = jnp.concatenate([grad_gate_in, grad_up_in], axis=-1).astype(jnp.bfloat16)
    weighted = (scale * hidden_wide).astype(jnp.bfloat16)
    grad_down = jnp.einsum(
        "dech," + layout + "->htf", weighted, rows_back, preferred_element_type=jnp.float32
    )
    grad_down = grad_down.reshape(hidden_width, tensor_size * features).astype(jnp.bfloat16)
    grad_both = jnp.einsum(
        layout + ",deck->tfk", rows_in, grad_inner, preferred_element_type=jnp.float32
    )
    grad_both = grad_both.reshape(tensor_size * features, 2 * hidden_width)
    grad_gate = grad_both[:, :hidden_width].astype(jnp.bfloat16)
    grad_up = grad_both[:, hidden_width:].astype(jnp.bfloat16)
    route_total = lax.psum(route_part, ("dp", "tensor"))
    own_route = lax.dynamic_index_in_dim(route_total, lax.axis_index("dp"), 0, keepdims=False)
    first = jnp.int32(0) // slots
    needed = min(
        dp_size,
        (slots * lax.axis_size(("dp", "tensor")) // slots + tensor_size - 1) // tensor_size + 1,
    )
    lead = jnp.clip(first // tensor_size, 0, dp_size - needed)
    part = lax.dynamic_slice_in_dim(grad_inner, lead, needed, 0)
    product = jnp.einsum("deck,tfk->dtecf", part, weights_in, preferred_element_type=jnp.float32)
    product = product.reshape(needed * tensor_size * slots, features)
    own_rows = lax.psum_scatter(
        product.astype(jnp.bfloat16), ("dp", "tensor"), scatter_dimension=0, tiled=True
    ).astype(jnp.float32)
    home = (
        lax.all_to_all(
            own_rows.reshape(experts, capacity, features).astype(jnp.bfloat16),
            "expert",
            split_axis=0,
            concat_axis=0,
            tiled=True,
        ),
        lax.all_to_all(
            own_route.astype(jnp.bfloat16), "expert", split_axis=0, concat_axis=0, tiled=True
        ),
    )
    input_grad = jnp.einsum(
        "ecr,ecf->rf", chosen_half, home[0], preferred_element_type=jnp.float32
    ).astype(jnp.bfloat16)
    per_expert = jnp.einsum("ecr,ec->re", chosen, home[1].astype(jnp.float32))
    route_grad = jnp.einsum("rke,re->rk", route_hits, per_expert).astype(jnp.bfloat16)
    return (input_grad, route_grad, grad_gate[None], grad_up[None], grad_down[None])


def solution(mesh):
    in_specs = (
        P(("dp", "expert"), "tensor"),
        P(("dp", "expert"), "tensor"),
        P(("dp", "expert"), None),
        P(("dp", "expert"), None),
        P(("dp", "expert")),
        P(),
        P(),
        P("expert", None, ("dp", "tensor")),
        P("expert", None, ("dp", "tensor")),
        P("expert", ("dp", "tensor"), None),
    )
    out_specs = (
        P(("dp", "expert"), "tensor"),
        P(("dp", "expert"), None),
        P("expert", None, ("dp", "tensor")),
        P("expert", None, ("dp", "tensor")),
        P("expert", ("dp", "tensor"), None),
    )
    return jax.shard_map(shards, mesh=mesh, in_specs=in_specs, out_specs=out_specs, check_vma=False)
```

profile of v0, /device:TPU:32, one launch (start us, length us, event | category | flops | bytes accessed | tf_op | source)
XLA Modules:
  0.0 505.4 jit_solution(11312434241959555918)
XLA Ops:
  7.2 0.0 copy-start
  7.2 0.0 all-gather.6.cloned.1.call-start
  7.3 0.9 convert_reduce_fusion
  8.2 0.3 convolution_convert_fusion
  8.6 0.3 copy.58
  8.9 36.5 %all_to_all.33 = bf16[16,5,3584]{2,1,0:T(8,128)(2,1)S(1)} all-to-all(bf16[16,5,3584]{2,1,0:T(8,128)(2,1)S(1)} %copy.58), channel_id=1, replica_groups=mesh['dp'=8,'expert'=16,'tensor'=2] {'expert'}, dimensions={0} | all-to-all | bytes 1146880 | tf_op jit(solution)/shard_map/all_to_all | solution.py:54
  45.4 1.0 reshape.75
  46.5 0.0 all-gather.6.cloned.1.call-update
  46.5 0.0 all-gather.4.cloned.1.call-start
  46.6 0.7 convert_element_type.94
  47.2 0.9 fusion.41
  48.2 1.0 fusion.34
  49.2 0.8 divide_subtract_fusion
  49.9 0.8 convolution_bitcast_fusion.2
  50.8 1.2 convolution_convert_fusion.1
  52.0 0.3 copy.54
  52.3 36.0 %all_to_all.34 = bf16[16,5,3584]{2,1,0:T(8,128)(2,1)S(1)} all-to-all(bf16[16,5,3584]{2,1,0:T(8,128)(2,1)S(1)} %copy.54), channel_id=1, replica_groups=mesh['dp'=8,'expert'=16,'tensor'=2] {'expert'}, dimensions={0} | all-to-all | bytes 1146880 | tf_op jit(solution)/shard_map/all_to_all | solution.py:55
  88.3 1.0 reshape.73
  89.3 0.0 all-gather.4.cloned.1.call-update
  89.4 0.2 fusion.51
  89.6 0.7 copy.52
  90.3 3.5 all-to-all-start
  93.8 0.0 reduce-scatter.2.cloned.1.call-start
  93.8 2.3 reshape_squeeze.3
  96.1 7.5 %all-to-all-done = bf16[16,1,5]{2,1,0:T(2,128)(2,1)S(1)} async-done(((bf16[16,1,5]{2,1,0:T(2,128)(2,1)}), bf16[16,1,5]{2,1,0:T(2,128)(2,1)S(1)}, u32[]{:S(2)}, u32[]{:S(2)}) %all-to-all-start) | async-done | bytes 192 | tf_op jit(solution)/shard_map/all_to_all | solution.py:56
  103.6 0.1 reshape.78
  103.7 27.9 %all-gather = bf16[16,1,80]{2,1,0:T(2,128)(2,1)S(1)} all-gather(bf16[1,1,80]{2,1,0:T(2,128)(2,1)S(1)} %reshape.78), channel_id=1, replica_groups=mesh['dp'=8,'expert'=16,'tensor'=2] {'dp','tensor'}, dimensions={0}, use_global_device_ids=true | all-gather | bytes 2720 | tf_op jit(solution)/shard_map/all_gather | solution.py:65
  131.7 0.1 reshape.72
  131.8 0.1 copy.53
  132.0 0.0 all-gather.6.cloned.1.call-done
  132.0 12.1 %copy.59 = bf16[16,80,3584]{2,0,1:T(8,128)(2,1)} copy(bf16[16,80,3584]{2,1,0:T(8,128)(2,1)} %all-gather.6.cloned.1.call-done) | data formatting | bytes 18350080 | tf_op jit(solution)/shard_map/all_gather | solution.py:59
  144.1 13.6 %reshape.76 = bf16[8,2,16,5,3584]{4,1,0,3,2:T(2,128)(2,1)} reshape(bf16[16,80,3584]{2,0,1:T(8,128)(2,1)} %copy.59) | data formatting | bytes 18350080 | tf_op jit(solution)/shard_map/reshape | solution.py:67
  157.7 29.4 %all-gather.4.cloned.1.call-done = bf16[16,80,3584]{2,1,0:T(8,128)(2,1)} async-done(((bf16[1,80,3584]{2,1,0:T(8,128)(2,1)}), bf16[16,80,3584]{2,1,0:T(8,128)(2,1)}) %all-gather.4.cloned.1.call-update) | async-done | bytes 9175056 | tf_op jit(solution)/shard_map/all_gather | solution.py:62
  187.2 12.1 %copy.55 = bf16[16,80,3584]{2,0,1:T(8,128)(2,1)} copy(bf16[16,80,3584]{2,1,0:T(8,128)(2,1)} %all-gather.4.cloned.1.call-done) | data formatting | bytes 18350080 | tf_op jit(solution)/shard_map/all_gather | solution.py:62
  199.3 13.9 %reshape.74 = bf16[8,2,16,5,3584]{4,1,0,3,2:T(2,128)(2,1)} reshape(bf16[16,80,3584]{2,0,1:T(8,128)(2,1)} %copy.55) | data formatting | bytes 18350080 | tf_op jit(solution)/shard_map/reshape | solution.py:68
  213.2 0.0 copy-start.4
  213.2 9.5 %fusion.23 = f32[8,16,5,256]{3,1,2,0:T(8,128)S(1)} fusion(bf16[2,3584,128]{2,1,0:T(8,128)(2,1)S(1)} %bitcast.121, bf16[2,3584,128]{2,1,0:T(8,128)(2,1)} %bitcast.123, bf16[8,2,16,5,3584]{4,1,0,3,2:T(2,128)(2,1)} %reshape.76), kind=kOutput, calls=%fused_computation.23 | convolution fusion | flops 2356150272 | bytes 13500416 | tf_op jit(solution)/shard_map/dtecf,tfk->deck/dot_general | solution.py:75
  222.7 0.0 copy-done.2
  222.7 0.0 copy-start.7
  222.7 5.1 %multiply_convert_fusion.2 = (bf16[8,16,5,128]{3,1,2,0:T(8,128)(2,1)S(1)}, bf16[8,16,5,128]{3,1,2,0:T(8,128)(2,1)S(1)}, bf16[8,16,5,128]{3,1,2,0:T(8,128)(2,1)S(1)}, f32[8,16,5,128]{3,1,2,0:T(8,128)S(1)}) fusion(f32[8,16,5,256]{3,1,2,0:T(8,128)S(1)} %fusion.23, f32[8,16,5]{1,2,0:T(8,128)S(1)} %copy.53, bf16[128,2,3584,1,1]{2,1,0,4,3:T(2,128)(2,1)S(1)} %bitcast.108, ...), kind=kOutput, calls=%fused_computation.39 | convolution fusion | flops 1175715840 | bytes 12487168 | tf_op jit(solution)/shard_map/dtecf,htf->dech/dot_general | solution.py:80
  227.8 3.0 convert_bitcast_fusion
  230.9 11.2 %copy.61 = bf16[8,2,16,5,3584]{4,3,2,1,0:T(8,128)(2,1)} copy(bf16[8,2,16,5,3584]{4,2,3,0,1:T(8,128)(2,1)S(1)} %convert_bitcast_fusion) | data formatting | bytes 18350080 | tf_op jit(solution)/shard_map/convert_element_type | solution.py:116
  242.1 14.9 %convert_element_type.102 = bf16[1280,3584]{1,0:T(8,128)(2,1)} reshape(bf16[8,2,16,5,3584]{4,3,2,1,0:T(8,128)(2,1)} %copy.61) | data formatting | bytes 18350080 | tf_op jit(solution)/shard_map/convert_element_type | solution.py:116
  257.0 0.0 reduce-scatter.2.cloned.1.call-update
  257.0 15.2 %reshape.104 = bf16[7168,5,8,16]{0,2,1,3:T(8,128)(2,1)} reshape(bf16[2,3584,5,8,16]{1,0,3,2,4:T(2,128)(2,1)} %bitcast.107) | data formatting | bytes 18350080 | tf_op jit(solution)/shard_map/dtecf,deck->tfk/dot_general | solution.py:98
  272.2 0.3 fusion.37
  272.5 57.4 %psum.7 = bf16[8,16,5]{1,2,0:T(8,128)(2,1)S(1)} all-reduce(f32[8,16,5]{1,2,0:T(8,128)S(1)} %get-tuple-element.11), channel_id=1, replica_groups=mesh['dp'=8,'expert'=16,'tensor'=2] {'dp','tensor'}, use_global_device_ids=true, to_apply=%region_5.6 | all-reduce | flops 640 | bytes 3840 | tf_op jit(solution)/shard_map/psum | solution.py:104
  329.8 0.7 copy.63
  330.5 8.8 %all-to-all-start.4 = ((bf16[16,1,5]{2,1,0:T(2,128)(2,1)}), bf16[16,1,5]{2,1,0:T(2,128)(2,1)S(1)}, u32[]{:S(2)}, u32[]{:S(2)}) async-start(bf16[16,1,5]{2,1,0:T(2,128)(2,1)} %copy.63), calls=%async_computation.5 | async-start | bytes 16384 | tf_op jit(solution)/shard_map/all_to_all | solution.py:126
  339.3 10.7 %fusion.7 = bf16[7168,256]{1,0:T(8,128)(2,1)S(1)} fusion(bf16[7168,5,8,16]{0,2,1,3:T(8,128)(2,1)} %reshape.104, bf16[8,16,5,128]{3,1,2,0:T(8,128)(2,1)S(1)} %get-tuple-element.8, bf16[8,16,5,128]{3,1,2,0:T(8,128)(2,1)S(1)} %get-tuple-element.7), kind=kOutput, calls=%fused_computation.9 | convolution fusion | flops 2351300608 | bytes 13172736 | tf_op jit(solution)/shard_map/dtecf,deck->tfk/dot_general | solution.py:98
  350.0 2.1 slice_bitcast_fusion
  352.1 15.2 %reshape.105 = bf16[7168,5,8,16]{0,2,1,3:T(8,128)(2,1)} reshape(bf16[2,3584,5,8,16]{1,0,3,2,4:T(2,128)(2,1)} %bitcast.106) | data formatting | bytes 18350080 | tf_op jit(solution)/shard_map/dech,dtecf->htf/dot_general | solution.py:94
  367.3 90.1 %reduce-scatter.2.cloned.1.call-done = bf16[80,3584]{1,0:T(8,128)(2,1)} async-done(((bf16[1280,3584]{1,0:T(8,128)(2,1)}), bf16[80,3584]{1,0:T(8,128)(2,1)}) %reduce-scatter.2.cloned.1.call-update) | async-done | bytes 573456 | tf_op jit(solution)/shard_map/reduce_scatter | solution.py:115
  457.5 2.2 convert_element_type.103
  459.7 0.0 all-to-all-done.4
  459.7 10.5 %all-to-all-start.3 = ((bf16[16,5,3584]{2,1,0:T(8,128)(2,1)}), bf16[16,5,3584]{2,1,0:T(8,128)(2,1)S(1)}, u32[]{:S(2)}, u32[]{:S(2)}) async-start(bf16[16,5,3584]{2,1,0:T(8,128)(2,1)} %convert_element_type.103), calls=%async_computation.4 | async-start | bytes 1835008 | tf_op jit(solution)/shard_map/all_to_all | solution.py:119
  470.2 10.6 %fusion.16 = bf16[1,128,7168]{2,1,0:T(8,128)(2,1)} fusion(bf16[7168,5,8,16]{0,2,1,3:T(8,128)(2,1)} %reshape.105, bf16[8,16,5,128]{3,1,2,0:T(8,128)(2,1)S(1)} %get-tuple-element.10), kind=kOutput, calls=%fused_computation.12 | convolution fusion | flops 1175322624 | bytes 11173888 | tf_op jit(solution)/shard_map/dech,dtecf->htf/dot_general | solution.py:94
  480.8 0.1 copy.98
  480.9 0.1 copy.86
  481.0 0.1 copy.87
  481.1 0.2 fusion.50
  481.3 0.6 convert_element_type.109
  481.9 15.8 %all-to-all-done.3 = bf16[16,5,3584]{2,1,0:T(8,128)(2,1)S(1)} async-done(((bf16[16,5,3584]{2,1,0:T(8,128)(2,1)}), bf16[16,5,3584]{2,1,0:T(8,128)(2,1)S(1)}, u32[]{:S(2)}, u32[]{:S(2)}) %all-to-all-start.3) | async-done | bytes 573472 | tf_op jit(solution)/shard_map/all_to_all | solution.py:119
  497.7 0.9 fusion.19
  (23 shorter events, 0.2 us)
Async XLA Ops:
  7.2 1.0 copy-start
  7.2 82.2 %copy-start.5 = (s32[8,8]{1,0:T(8,128)S(1)}, s32[8,8]{1,0:T(8,128)}, u32[]{:S(2)}) copy-start(s32[8,8]{1,0:T(8,128)} %param.13) | copy-start | bytes 772
  7.2 82.2 %copy-start.8 = (bf16[8,8]{1,0:T(8,128)(2,1)S(1)}, bf16[8,8]{1,0:T(8,128)(2,1)}, u32[]{:S(2)}) copy-start(bf16[8,8]{1,0:T(8,128)(2,1)} %param.12) | copy-start | bytes 388
  7.2 86.6 %copy-start.3 = (bf16[1,128,7168]{2,1,0:T(8,128)(2,1)S(1)}, bf16[1,128,7168]{2,1,0:T(8,128)(2,1)}, u32[]{:S(2)}) copy-start(bf16[1,128,7168]{2,1,0:T(8,128)(2,1)} %param.19) | copy-start | bytes 5505028
  7.2 124.7 %all-gather.6.cloned.1.call-start = ((), (), s32[]{:S(2)}) async-start(), calls=%async_computation.7 | async-start | bytes 9748480 | tf_op jit(solution)/shard_map/all_gather | solution.py:59
  46.5 140.7 %all-gather.4.cloned.1.call-start = ((), (), s32[]{:S(2)}) async-start(), calls=%async_computation.6 | async-start | bytes 9748480 | tf_op jit(solution)/shard_map/all_gather | solution.py:62
  90.3 13.3 %all-to-all-start = ((bf16[16,1,5]{2,1,0:T(2,128)(2,1)}), bf16[16,1,5]{2,1,0:T(2,128)(2,1)S(1)}, u32[]{:S(2)}, u32[]{:S(2)}) async-start(bf16[16,1,5]{2,1,0:T(2,128)(2,1)} %copy.52), calls=%async_computation | async-start | bytes 16384 | tf_op jit(solution)/shard_map/all_to_all | solution.py:56
  93.8 363.7 %reduce-scatter.2.cloned.1.call-start = ((), (), s32[]{:S(2)}) async-start(), calls=%async_computation.8 | async-start | bytes 9748480 | tf_op jit(solution)/shard_map/reduce_scatter | solution.py:115
  199.2 13.9 %copy-start.6 = (bf16[1,7168,128]{2,1,0:T(8,128)(2,1)S(1)}, bf16[1,7168,128]{2,1,0:T(8,128)(2,1)}, u32[]{:S(2)}) copy-start(bf16[1,7168,128]{2,1,0:T(8,128)(2,1)} %param.18) | copy-start | bytes 5505028
  213.1 9.6 %copy-start.2 = (bf16[8,2,16,5,3584]{4,1,0,3,2:T(2,128)(2,1)S(1)}, bf16[8,2,16,5,3584]{4,1,0,3,2:T(2,128)(2,1)}, u32[]{:S(2)}) copy-start(bf16[8,2,16,5,3584]{4,1,0,3,2:T(2,128)(2,1)} %reshape.74) | copy-start | bytes 27525124
  213.2 9.6 %copy-start.4 = (bf16[128,2,3584]{2,1,0:T(2,128)(2,1)S(1)}, bf16[128,2,3584]{2,1,0:T(2,128)(2,1)}, u32[]{:S(2)}) copy-start(bf16[128,2,3584]{2,1,0:T(2,128)(2,1)} %reshape_squeeze.3) | copy-start | bytes 5505028
  222.7 5.1 %copy-start.7 = (bf16[1,7168,128]{2,1,0:T(8,128)(2,1)S(1)}, bf16[1,7168,128]{2,1,0:T(8,128)(2,1)}, u32[]{:S(2)}) copy-start(bf16[1,7168,128]{2,1,0:T(8,128)(2,1)} %param.17) | copy-start | bytes 5505028
  330.5 129.1 %all-to-all-start.4 = ((bf16[16,1,5]{2,1,0:T(2,128)(2,1)}), bf16[16,1,5]{2,1,0:T(2,128)(2,1)S(1)}, u32[]{:S(2)}, u32[]{:S(2)}) async-start(bf16[16,1,5]{2,1,0:T(2,128)(2,1)} %copy.63), calls=%async_computation.5 | async-start | bytes 16384 | tf_op jit(solution)/shard_map/all_to_all | solution.py:126
  352.1 146.5 %copy-start.1 = (bf16[8,3584]{1,0:T(8,128)(2,1)S(1)}, bf16[8,3584]{1,0:T(8,128)(2,1)}, u32[]{:S(2)}) copy-start(bf16[8,3584]{1,0:T(8,128)(2,1)} %param.10) | copy-start | bytes 172036
  459.7 38.0 %all-to-all-start.3 = ((bf16[16,5,3584]{2,1,0:T(8,128)(2,1)}), bf16[16,5,3584]{2,1,0:T(8,128)(2,1)S(1)}, u32[]{:S(2)}, u32[]{:S(2)}) async-start(bf16[16,5,3584]{2,1,0:T(8,128)(2,1)} %convert_element_type.103), calls=%async_computation.4 | async-start | bytes 1835008 | tf_op jit(solution)/shard_map/all_to_all | solution.py:119
Sparse Core Ops, SparseCore 0:
  46.6 75.0 all-gather.5
  124.1 63.0 all-gather.3
  257.1 200.2 reduce-scatter.1
where the time goes:
time: 511 us; the launch traced here: 505 us
  blocking collectives  158 us (31%)
  waiting for transfers between devices  143 us (28%)
  local copies, waits for them, and re-layouts  120 us (23%)
  matrix products  43.7 us (9%)
  starting transfers between devices  22.9 us (4%)
  between operations  14.3 us (3%)
    reduce_scatter x1, waiting for transfers between devices, shards(): lax.psum_scatter(product.astype(jnp.bfloat16), ('dp', 'tensor'), scatter_...  90.1 us
    psum x1, blocking collectives, shards(): route_total = lax.psum(route_part, ('dp', 'tensor'))  57.4 us
    all_to_all x1, blocking collectives, shards(): lax.all_to_all(packed_rows, 'expert', split_axis=0, concat_axis=0, tiled=...  36.5 us
    all_to_all x1, blocking collectives, shards(): lax.all_to_all(packed_upstream, 'expert', split_axis=0, concat_axis=0, ti...  36 us
    all_gather x1, waiting for transfers between devices, shards(): lax.all_gather(arrived[1].reshape(1, slots, features), ('dp', 'tensor'),...  29.4 us
    all_gather x1, blocking collectives, shards(): lax.all_gather(arrived[2].reshape(1, slots), ('dp', 'tensor'), axis=0, ti...  27.9 us
    convert_element_type x2, local copies, waits for them, and re-layouts, shards(): product.astype(jnp.bfloat16)  26.1 us
    all_to_all x1, waiting for transfers between devices, shards(): lax.all_to_all(own_rows.reshape(experts, capacity, features).astype(jnp.b...  15.8 us
  transfers between devices with their start and end apart: 6, of which 4 were waited for; matrix products, arithmetic and copies ran while one was open for 19% of the time, Pallas kernels for 0%

commit v1 on v0

v1 whole, which is shorter than its diff:
```python
import jax
import jax.numpy as jnp
from jax import lax
from jax.sharding import PartitionSpec as P


def advantages(row_rollout, group_ids, rewards):
    same_group = (group_ids[:, None] == group_ids[None, :]).astype(jnp.float32)
    reward_values = rewards.astype(jnp.float32)
    group_total = jnp.dot(same_group, reward_values, precision=lax.Precision.HIGHEST)
    group_count = jnp.sum(same_group, axis=1)
    per_rollout = reward_values - group_total / group_count
    member = (
        row_rollout[:, None] == jnp.arange(per_rollout.shape[0], dtype=jnp.int32)[None, :]
    ).astype(jnp.float32)
    return jnp.dot(member, per_rollout, precision=lax.Precision.HIGHEST)


def selection(routing, probs, experts, capacity):
    route_hits = (
        routing[:, :, None] == jnp.arange(experts, dtype=jnp.int32)[None, None, :]
    ).astype(jnp.float32)
    occupied = jnp.sum(route_hits, axis=1)
    weight = jnp.einsum("rke,rk->re", route_hits, probs.astype(jnp.float32))
    before = jnp.cumsum(occupied, axis=0) - occupied
    slot_index = jnp.arange(capacity, dtype=jnp.float32)
    chosen = occupied.T[:, None, :] * (before.T[:, None, :] == slot_index[None, :, None]).astype(
        jnp.float32
    )
    return (route_hits, weight, chosen)


def shards(tokens, upstream, probs, routing, row_rollout, group_ids, rewards, w_gate, w_up, w_down):
    f32 = jnp.float32
    bf16 = jnp.bfloat16
    experts = lax.axis_size("expert")
    dp_size = lax.axis_size("dp")
    tensor_size = lax.axis_size("tensor")
    group_rows, features = tokens.shape
    routes_per_row = routing.shape[1]
    capacity = min(group_rows, 5 * group_rows * routes_per_row // (4 * experts))
    slots = experts * capacity
    all_slots = dp_size * slots

    advantage = advantages(row_rollout, group_ids, rewards)
    cotangent = (advantage[:, None] * upstream.astype(f32)).astype(bf16)
    route_hits, weight, chosen = selection(routing, probs, experts, capacity)
    chosen_half = chosen.astype(bf16)

    both = jnp.stack([tokens, cotangent])
    packed = jnp.einsum(
        "ecr,arf->aecf", chosen_half, both, preferred_element_type=f32
    ).astype(bf16)
    packed_prob = jnp.einsum("ecr,re->ec", chosen, weight).astype(bf16)
    prob_row = jnp.zeros((experts, 1, features), bf16).at[:, 0, :capacity].set(packed_prob)
    prob_rows = jnp.stack([jnp.zeros_like(prob_row), prob_row])
    packed = jnp.concatenate([packed, prob_rows], axis=2)
    arrived = lax.all_to_all(packed, "expert", split_axis=1, concat_axis=1, tiled=True)
    tok_rows = arrived[0, :, :capacity].reshape(slots, features)
    cot_rows = arrived[1, :, :capacity].reshape(slots, features)
    slot_prob_local = arrived[1, :, capacity, :capacity].reshape(slots)

    g_tok = lax.all_gather(tok_rows, ("tensor", "dp"), axis=0, tiled=True)
    g_tok = g_tok.reshape(tensor_size, all_slots, features)
    g_cot = lax.all_gather(cot_rows, ("tensor", "dp"), axis=0, tiled=True)
    g_cot = g_cot.reshape(tensor_size, all_slots, features)
    slot_prob = lax.all_gather(slot_prob_local, "dp", axis=0, tiled=True)

    wg = w_gate[0].reshape(tensor_size, features, -1)
    wu = w_up[0].reshape(tensor_size, features, -1)
    wd = w_down[0]
    hidden_width = wd.shape[0]
    wd = wd.reshape(hidden_width, tensor_size, features)

    gate = sum(
        jnp.dot(g_tok[t], wg[t], preferred_element_type=f32) for t in range(tensor_size)
    )
    up_part = sum(
        jnp.dot(g_tok[t], wu[t], preferred_element_type=f32) for t in range(tensor_size)
    )
    back_hidden = sum(
        jnp.einsum("sf,hf->sh", g_cot[t], wd[:, t], preferred_element_type=f32)
        for t in range(tensor_size)
    )

    sigmoid_gate = jax.nn.sigmoid(gate)
    active = gate * sigmoid_gate
    hidden = (active * up_part).astype(bf16)
    hidden_wide = lax.optimization_barrier(hidden).astype(f32)
    route_part = jnp.sum(hidden_wide * back_hidden, axis=-1)
    scale = slot_prob.astype(f32)[:, None]
    scaled = scale * back_hidden
    grad_g = (scaled * up_part * sigmoid_gate * (1.0 + gate * (1.0 - sigmoid_gate))).astype(bf16)
    grad_u = (scaled * active).astype(bf16)
    weighted = (scale * hidden_wide).astype(bf16)

    route_total = lax.psum(route_part, ("dp", "tensor"))
    route_total, grad_g_p, grad_u_p = lax.optimization_barrier((route_total, grad_g, grad_u))

    grad_down = jnp.concatenate(
        [
            jnp.dot(weighted.T, g_cot[t], preferred_element_type=f32).astype(bf16)
            for t in range(tensor_size)
        ],
        axis=1,
    )
    grad_gate = jnp.concatenate(
        [
            jnp.dot(g_tok[t].T, grad_g, preferred_element_type=f32).astype(bf16)
            for t in range(tensor_size)
        ],
        axis=0,
    )
    grad_up = jnp.concatenate(
        [
            jnp.dot(g_tok[t].T, grad_u, preferred_element_type=f32).astype(bf16)
            for t in range(tensor_size)
        ],
        axis=0,
    )

    product = jnp.stack(
        [
            (
                jnp.einsum("sk,fk->sf", grad_g_p, wg[t], preferred_element_type=f32)
                + jnp.einsum("sk,fk->sf", grad_u_p, wu[t], preferred_element_type=f32)
            ).astype(bf16)
            for t in range(tensor_size)
        ]
    ).reshape(tensor_size * all_slots, features)
    own_rows = lax.psum_scatter(product, ("tensor", "dp"), scatter_dimension=0, tiled=True)

    own_route = lax.dynamic_slice_in_dim(
        route_total, lax.axis_index("dp") * slots, slots, 0
    ).astype(bf16)
    route_row = jnp.zeros((experts, 1, features), bf16).at[:, 0, :capacity].set(
        own_route.reshape(experts, capacity)
    )
    back_pack = jnp.concatenate([own_rows.reshape(experts, capacity, features), route_row], axis=1)
    home = lax.all_to_all(back_pack, "expert", split_axis=0, concat_axis=0, tiled=True)
    input_grad = jnp.einsum(
        "ecr,ecf->rf", chosen_half, home[:, :capacity], preferred_element_type=f32
    ).astype(bf16)
    per_expert = jnp.einsum("ecr,ec->re", chosen, home[:, capacity, :capacity].astype(f32))
    route_grad = jnp.einsum("rke,re->rk", route_hits, per_expert).astype(bf16)
    return (input_grad, route_grad, grad_gate[None], grad_up[None], grad_down[None])


def solution(mesh):
    in_specs = (
        P(("dp", "expert"), "tensor"),
        P(("dp", "expert"), "tensor"),
        P(("dp", "expert"), None),
        P(("dp", "expert"), None),
        P(("dp", "expert")),
        P(),
        P(),
        P("expert", None, ("dp", "tensor")),
        P("expert", None, ("dp", "tensor")),
        P("expert", ("dp", "tensor"), None),
    )
    out_specs = (
        P(("dp", "expert"), "tensor"),
        P(("dp", "expert"), None),
        P("expert", None, ("dp", "tensor")),
        P("expert", None, ("dp", "tensor")),
        P("expert", ("dp", "tensor"), None),
    )
    return jax.shard_map(shards, mesh=mesh, in_specs=in_specs, out_specs=out_specs, check_vma=False)
```

time: 511 us -> 367 us (0.72)
  local copies, waits for them, and re-layouts: 120 us -> 16.8 us
  blocking collectives: 158 us -> 87.4 us
  waiting for transfers between devices: 143 us -> 164 us
  other arithmetic: 4.29 us -> 17.8 us
  starting transfers between devices: 22.9 us -> 9.69 us
  matrix products: 43.7 us -> 52.8 us
    all_gather x2, waiting for transfers between devices: 29.5 us -> 85.6 us  [the longest x1 50.1 us: shards(): g_cot = lax.all_gather(cot_rows, ('tensor', 'dp'), axis=0, tiled=True)]
    dot_general x3 -> x1, local copies, waits for them, and re-layouts: 30.5 us -> 0.08 us  [shards(): jnp.einsum('ecr,ec->re', chosen, home[:, capacity, :capacity].astype(f32))]
    convert_element_type x8 -> x0, local copies, waits for them, and re-layouts: 29.8 us -> none  [the longest x2 26.1 us: shards(): product.astype(jnp.bfloat16)]
    psum x1, blocking collectives: 57.4 us -> 28.3 us  [shards(): route_total = lax.psum(route_part, ('dp', 'tensor'))]
    reshape x5 -> x1, local copies, waits for them, and re-layouts: 29.7 us -> 1.29 us  [shards(): own_rows.reshape(experts, capacity, features)]
    reduce_scatter x1, waiting for transfers between devices: 90.1 us -> 62.1 us  [shards(): lax.psum_scatter(product, ('tensor', 'dp'), scatter_dimension=0, tiled=True)]
    all_gather x1 -> x0, blocking collectives: 27.9 us -> none  [shards(): lax.all_gather(arrived[2].reshape(1, slots), ('dp', 'tensor'), axis=0, ti...]
    all_to_all x2 -> x1, blocking collectives: 72.5 us -> 46.3 us  [shards(): lax.all_to_all(packed, 'expert', split_axis=1, concat_axis=1, tiled=True)]
  transfers between devices with their start and end apart: 6 -> 4, of which waited for: 4 -> 4; matrix products, arithmetic and copies ran while one was open for 19% -> 11% of each run, Pallas kernels for 0% -> 0%
where the time goes in v1:
time: 367 us; the launch traced here: 363 us
  waiting for transfers between devices  164 us (45%)
  blocking collectives  87.4 us (24%)
  matrix products  52.8 us (14%)
  other arithmetic  17.8 us (5%)
  local copies, waits for them, and re-layouts  16.8 us (5%)
  between operations  14.7 us (4%)
  starting transfers between devices  9.69 us (3%)
    reduce_scatter x1, waiting for transfers between devices, shards(): lax.psum_scatter(product, ('tensor', 'dp'), scatter_dimension=0, tiled=True)  62.1 us
    all_gather x1, waiting for transfers between devices, shards(): g_cot = lax.all_gather(cot_rows, ('tensor', 'dp'), axis=0, tiled=True)  50.1 us
    all_to_all x1, blocking collectives, shards(): lax.all_to_all(packed, 'expert', split_axis=1, concat_axis=1, tiled=True)  46.3 us
    all_gather x1, waiting for transfers between devices, shards(): g_tok = lax.all_gather(tok_rows, ('tensor', 'dp'), axis=0, tiled=True)  35.4 us
    psum x1, blocking collectives, shards(): route_total = lax.psum(route_part, ('dp', 'tensor'))  28.3 us
    all_to_all x1, waiting for transfers between devices, shards(): lax.all_to_all(back_pack, 'expert', split_axis=0, concat_axis=0, tiled=True)  16.4 us
    unnamed x1, blocking collectives  12.8 us
    all_to_all x1, starting transfers between devices, shards(): lax.all_to_all(back_pack, 'expert', split_axis=0, concat_axis=0, tiled=True)  9.57 us
  transfers between devices with their start and end apart: 4, of which 4 were waited for; matrix products, arithmetic and copies ran while one was open for 11% of the time, Pallas kernels for 0%

profile of v1, /device:TPU:32, one launch (start us, length us, event | category | flops | bytes accessed | tf_op | source)
XLA Modules:
  0.0 363.3 jit_solution(9495369176601378796)
XLA Ops:
  7.2 0.0 all-gather.3.cloned.1.call-start
  7.2 0.9 fusion.59
  8.2 0.7 convert_element_type.84
  8.8 1.0 fusion.54
  9.9 0.8 convert_reduce_fusion
  10.7 0.9 fusion.68
  11.6 0.1 copy.56
  11.7 0.7 divide_subtract_fusion
  12.4 0.8 convolution_bitcast_fusion.1
  13.3 0.9 fusion.66
  14.2 1.3 fusion.2
  15.5 0.1 fusion.24
  15.6 1.4 copy.57
  17.0 46.3 %all_to_all.10 = bf16[2,16,6,3584]{3,0,2,1:T(2,128)(2,1)S(1)} all-to-all(bf16[2,16,6,3584]{3,0,2,1:T(2,128)(2,1)S(1)} %copy.57), channel_id=1, replica_groups=mesh['dp'=8,'expert'=16,'tensor'=2] {'expert'}, dimensions={1} | all-to-all | bytes 2752512 | tf_op jit(solution)/shard_map/all_to_all | solution.py:58
  63.4 5.2 %slice_reduce_fusion.1 = (bf16[16,5,3584]{2,1,0:T(8,128)(2,1)S(1)}, bf16[16,5,3584]{2,1,0:T(8,128)(2,1)S(1)}) fusion(bf16[2,16,6,3584]{3,0,2,1:T(2,128)(2,1)S(1)} %all_to_all.10), kind=kLoop, calls=%fused_computation.45 | loop fusion | bytes 2293760 | tf_op jit(solution)/shard_map/slice | solution.py:59
  68.6 1.0 reshape_squeeze.14
  69.6 0.0 all-gather.3.cloned.1.call-update
  69.6 0.0 all-gather.5.cloned.1.call-start
  69.7 1.0 reshape_squeeze.15
  70.7 0.0 all-gather.5.cloned.1.call-update
  70.8 0.0 reduce-scatter.2.cloned.1.call-start
  70.8 4.0 %copy.58 = bf16[1,128,7168]{1,2,0:T(8,128)(2,1)} copy(bf16[1,128,7168]{2,1,0:T(8,128)(2,1)} %param.23) | data formatting | bytes 3670016 | tf_op args[9]
  74.8 0.6 dynamic-slice.13
  76.1 0.1 reshape.120
  76.2 0.2 dynamic-update-slice.7
  76.4 12.8 %all-reduce.3 = bf16[640]{0:T(1024)(128)(2,1)S(1)} all-reduce(bf16[640]{0:T(1024)(128)(2,1)S(1)} %dynamic-update-slice.7), channel_id=1, replica_groups=mesh['dp'=8,'expert'=16,'tensor'=2] {'dp'}, use_global_device_ids=true, to_apply=%add.3 | all-reduce | flops 640 | bytes 2560
  89.2 35.4 %all-gather.3.cloned.1.call-done = bf16[1280,3584]{1,0:T(8,128)(2,1)} async-done(((bf16[80,3584]{1,0:T(8,128)(2,1)}), bf16[1280,3584]{1,0:T(8,128)(2,1)}) %all-gather.3.cloned.1.call-update) | async-done | bytes 9175056 | tf_op jit(solution)/shard_map/all_gather | solution.py:63
  124.7 3.8 %fusion.12 = f32[640,128]{1,0:T(8,128)S(1)} fusion(bf16[1280,3584]{1,0:T(8,128)(2,1)} %all-gather.3.cloned.1.call-done, bf16[1,7168,128]{2,1,0:T(8,128)(2,1)S(1)} %copy-done.3), kind=kOutput, calls=%fused_computation.23 | convolution fusion | flops 587202560 | bytes 5832704 | tf_op jit(solution)/shard_map/dot_general | solution.py:79
  128.5 4.2 %fusion.14 = f32[640,128]{1,0:T(8,128)S(1)} fusion(bf16[1280,3584]{1,0:T(8,128)(2,1)} %all-gather.3.cloned.1.call-done, bf16[1,7168,128]{2,1,0:T(8,128)(2,1)S(1)} %copy-done.4), kind=kOutput, calls=%fused_computation.25 | convolution fusion | flops 587202560 | bytes 5832704 | tf_op jit(solution)/shard_map/dot_general | solution.py:76
  132.7 1.4 fusion.28
  134.1 2.1 fusion.25
  136.2 50.1 %all-gather.5.cloned.1.call-done = bf16[1280,3584]{1,0:T(8,128)(2,1)} async-done(((bf16[80,3584]{1,0:T(8,128)(2,1)}), bf16[1280,3584]{1,0:T(8,128)(2,1)}) %all-gather.5.cloned.1.call-update) | async-done | bytes 9175056 | tf_op jit(solution)/shard_map/all_gather | solution.py:65
  186.3 4.0 %fusion.5 = f32[640,128]{1,0:T(8,128)S(1)} fusion(bf16[1280,3584]{1,0:T(8,128)(2,1)} %all-gather.5.cloned.1.call-done, bf16[128,2,3584]{0,2,1:T(8,128)(2,1)} %bitcast.105), kind=kOutput, calls=%fused_computation.16 | convolution fusion | flops 587202560 | bytes 5832704 | tf_op jit(solution)/shard_map/sf,hf->sh/dot_general | solution.py:82
  190.4 1.2 copy-done.2
  191.6 2.6 multiply_convert_fusion
  194.2 0.2 fusion.56
  194.4 28.3 %psum.7 = bf16[640]{0:T(1024)(128)(2,1)S(1)} all-reduce(f32[640]{0:T(1024)S(1)} %fusion.56), channel_id=1, replica_groups=mesh['dp'=8,'expert'=16,'tensor'=2] {'dp','tensor'}, use_global_device_ids=true, to_apply=%region_4.5 | all-reduce | flops 640 | bytes 3840 | tf_op jit(solution)/shard_map/psum | solution.py:97
  222.7 2.7 fusion.39
  225.4 1.4 fusion.42
  226.8 3.6 fusion.1
  230.4 3.5 fusion
  233.8 8.1 %pad_maximum_fusion = bf16[2,640,3584]{2,1,0:T(8,128)(2,1)} fusion(bf16[1,640,3584]{2,1,0:T(8,128)(2,1)} %fusion.1, bf16[1,640,3584]{2,1,0:T(8,128)(2,1)} %fusion), kind=kLoop, calls=%fused_computation | loop fusion | flops 4587520 | bytes 18350080 | tf_op jit(solution)/shard_map/stack | solution.py:122
  242.0 0.0 reduce-scatter.2.cloned.1.call-update
  242.0 0.1 dynamic_slice.5
  242.1 0.1 reshape.140
  242.2 3.4 convolution_convert_fusion.1
  245.6 3.4 convolution_convert_fusion.2
  249.1 3.8 %convolution_convert_fusion.3 = bf16[3584,128]{1,0:T(8,128)(2,1)S(1)} fusion(bf16[640,128]{1,0:T(8,128)(2,1)S(1)} %get-tuple-element.33, bf16[1280,3584]{1,0:T(8,128)(2,1)} %all-gather.3.cloned.1.call-done), kind=kOutput, calls=%fused_computation.8 | convolution fusion | flops 587661312 | bytes 5668864 | tf_op jit(solution)/shard_map/dot_general | solution.py:116
  252.9 1.4 convolution_convert_fusion.4
  254.3 2.6 convolution_convert_fusion.5
  256.9 1.4 maximum_bitcast_fusion.2
  258.3 62.1 %reduce-scatter.2.cloned.1.call-done = bf16[80,3584]{1,0:T(8,128)(2,1)} async-done(((bf16[1280,3584]{1,0:T(8,128)(2,1)}), bf16[80,3584]{1,0:T(8,128)(2,1)}) %reduce-scatter.2.cloned.1.call-update) | async-done | bytes 573456 | tf_op jit(solution)/shard_map/reduce_scatter | solution.py:131
  320.4 1.3 reshape.118
  321.7 1.1 fusion.34
  322.8 9.6 %all-to-all-start.1 = ((bf16[16,6,3584]{2,1,0:T(8,128)(2,1)}), bf16[16,6,3584]{2,1,0:T(8,128)(2,1)S(1)}, u32[]{:S(2)}, u32[]{:S(2)}) async-start(bf16[16,6,3584]{2,1,0:T(8,128)(2,1)} %fusion.34), calls=%async_computation.2 | async-start | bytes 1835008 | tf_op jit(solution)/shard_map/all_to_all | solution.py:140
  332.4 3.8 %convolution_convert_fusion.6 = bf16[3584,128]{1,0:T(8,128)(2,1)S(1)} fusion(bf16[640,128]{1,0:T(8,128)(2,1)S(1)} %get-tuple-element.32, bf16[1280,3584]{1,0:T(8,128)(2,1)} %all-gather.3.cloned.1.call-done), kind=kOutput, calls=%fused_computation.11 | convolution fusion | flops 587661312 | bytes 5668864 | tf_op jit(solution)/shard_map/dot_general | solution.py:109
  336.2 2.1 maximum_bitcast_fusion
  338.3 16.4 %all-to-all-done.1 = bf16[16,6,3584]{2,1,0:T(8,128)(2,1)S(1)} async-done(((bf16[16,6,3584]{2,1,0:T(8,128)(2,1)}), bf16[16,6,3584]{2,1,0:T(8,128)(2,1)S(1)}, u32[]{:S(2)}, u32[]{:S(2)}) %all-to-all-start.1) | async-done | bytes 688160 | tf_op jit(solution)/shard_map/all_to_all | solution.py:140
  354.7 0.1 copy.91
  354.8 0.9 fusion.3
  355.8 0.1 copy.81
  355.9 0.1 copy.82
  356.0 0.2 fusion.67
  356.2 0.6 convert_element_type.100
  (42 shorter events, 0.2 us)
Async XLA Ops:
  7.2 3.6 copy-start
  7.2 117.5 %all-gather.3.cloned.1.call-start = ((), (), s32[]{:S(2)}) async-start(), calls=%async_computation.3 | async-start | bytes 9748480 | tf_op jit(solution)/shard_map/all_gather | solution.py:63
  68.6 6.3 %copy-start.8 = (u32[256]{0:T(256)S(1)}, u32[256]{0:T(256)}, u32[]{:S(2)}) copy-start(u32[256]{0:T(256)} %constant.88) | copy-start | bytes 3076
  69.6 116.7 %all-gather.5.cloned.1.call-start = ((), (), s32[]{:S(2)}) async-start(), calls=%async_computation.4 | async-start | bytes 9748480 | tf_op jit(solution)/shard_map/all_gather | solution.py:65
  70.7 54.0 %copy-start.3 = (bf16[1,7168,128]{2,1,0:T(8,128)(2,1)S(1)}, bf16[1,7168,128]{2,1,0:T(8,128)(2,1)}, u32[]{:S(2)}) copy-start(bf16[1,7168,128]{2,1,0:T(8,128)(2,1)} %param.22) | copy-start | bytes 5505028
  70.8 249.6 %reduce-scatter.2.cloned.1.call-start = ((), (), s32[]{:S(2)}) async-start(), calls=%async_computation.5 | async-start | bytes 9748480 | tf_op jit(solution)/shard_map/reduce_scatter | solution.py:131
  124.7 3.8 %copy-start.4 = (bf16[1,7168,128]{2,1,0:T(8,128)(2,1)S(1)}, bf16[1,7168,128]{2,1,0:T(8,128)(2,1)}, u32[]{:S(2)}) copy-start(bf16[1,7168,128]{2,1,0:T(8,128)(2,1)} %param.21) | copy-start | bytes 5505028
  124.7 8.0 %slice-start = ((s8[9175040]{0:T(1024)(128)(4,1)}), s8[4194304]{0:T(1024)(128)(4,1)S(1)}, s32[]{:S(2)}) async-start(s8[9175040]{0:T(1024)(128)(4,1)} %bitcast.120), calls=%async_computation.6 | async-start | bytes 8388608
  124.7 8.0 %slice-start.1 = ((s8[9175040]{0:T(1024)(128)(4,1)}), s8[4194304]{0:T(1024)(128)(4,1)S(1)}, s32[]{:S(2)}) async-start(s8[9175040]{0:T(1024)(128)(4,1)} %bitcast.120), calls=%async_computation.7 | async-start | bytes 8388608
  128.5 4.2 %slice-start.2 = ((s8[9175040]{0:T(1024)(128)(4,1)}), s8[786432]{0:T(1024)(128)(4,1)S(1)}, s32[]{:S(2)}) async-start(s8[9175040]{0:T(1024)(128)(4,1)} %bitcast.120), calls=%async_computation.8 | async-start | bytes 1572864
  186.3 5.3 %copy-start.2 = (bf16[1280,3584]{1,0:T(8,128)(2,1)S(1)}, bf16[1280,3584]{1,0:T(8,128)(2,1)}, u32[]{:S(2)}) copy-start(bf16[1280,3584]{1,0:T(8,128)(2,1)} %all-gather.5.cloned.1.call-done) | copy-start | bytes 27525124
  186.3 5.3 %copy-start.9 = (f32[640,128]{1,0:T(8,128)S(1)}, f32[640,128]{1,0:T(8,128)}, u32[]{:S(2)}) copy-start(f32[640,128]{1,0:T(8,128)} %fusion.25) | copy-start | bytes 983044
  222.7 2.7 copy-start.5
  242.2 10.7 %slice-start.3 = ((s8[9175040]{0:T(1024)(128)(4,1)}), s8[4194304]{0:T(1024)(128)(4,1)S(1)}, s32[]{:S(2)}) async-start(s8[9175040]{0:T(1024)(128)(4,1)} %bitcast.122), calls=%async_computation.9 | async-start | bytes 8388608
  245.6 7.3 %slice-start.4 = ((s8[9175040]{0:T(1024)(128)(4,1)}), s8[4194304]{0:T(1024)(128)(4,1)S(1)}, s32[]{:S(2)}) async-start(s8[9175040]{0:T(1024)(128)(4,1)} %bitcast.122), calls=%async_computation.10 | async-start | bytes 8388608
  249.1 3.8 %slice-start.5 = ((s8[9175040]{0:T(1024)(128)(4,1)}), s8[786432]{0:T(1024)(128)(4,1)S(1)}, s32[]{:S(2)}) async-start(s8[9175040]{0:T(1024)(128)(4,1)} %bitcast.122), calls=%async_computation.11 | async-start | bytes 1572864
  322.8 31.9 %all-to-all-start.1 = ((bf16[16,6,3584]{2,1,0:T(8,128)(2,1)}), bf16[16,6,3584]{2,1,0:T(8,128)(2,1)S(1)}, u32[]{:S(2)}, u32[]{:S(2)}) async-start(bf16[16,6,3584]{2,1,0:T(8,128)(2,1)} %fusion.34), calls=%async_computation.2 | async-start | bytes 1835008 | tf_op jit(solution)/shard_map/all_to_all | solution.py:140
  332.4 3.8 %copy-start.6 = (bf16[3584,128]{1,0:T(8,128)(2,1)S(1)}, bf16[3584,128]{1,0:T(8,128)(2,1)}, u32[]{:S(2)}) copy-start(bf16[3584,128]{1,0:T(8,128)(2,1)} %convolution_convert_fusion.5) | copy-start | bytes 2752516
  332.4 24.4 %copy-start.1 = (bf16[8,8]{1,0:T(8,128)(2,1)S(1)}, bf16[8,8]{1,0:T(8,128)(2,1)}, u32[]{:S(2)}) copy-start(bf16[8,8]{1,0:T(8,128)(2,1)} %param.16) | copy-start | bytes 388
  336.2 19.8 %copy-start.7 = (s32[8,8]{1,0:T(8,128)S(1)}, s32[8,8]{1,0:T(8,128)}, u32[]{:S(2)}) copy-start(s32[8,8]{1,0:T(8,128)} %param.17) | copy-start | bytes 772
Sparse Core Ops, SparseCore 0:
  69.8 54.8 all-gather.2
  127.1 59.1 all-gather.4
  242.1 78.2 reduce-scatter.1

commit v2 on v1

v2 whole, which is shorter than its diff:
```python
import jax
import jax.numpy as jnp
import numpy as np
from jax import lax
from jax.sharding import Mesh
from jax.sharding import PartitionSpec as P

CORES = 2
DP = ("x", "core")


def advantages(row_rollout, group_ids, rewards):
    same_group = (group_ids[:, None] == group_ids[None, :]).astype(jnp.float32)
    reward_values = rewards.astype(jnp.float32)
    group_total = jnp.dot(same_group, reward_values, precision=lax.Precision.HIGHEST)
    group_count = jnp.sum(same_group, axis=1)
    per_rollout = reward_values - group_total / group_count
    member = (
        row_rollout[:, None] == jnp.arange(per_rollout.shape[0], dtype=jnp.int32)[None, :]
    ).astype(jnp.float32)
    return jnp.dot(member, per_rollout, precision=lax.Precision.HIGHEST)


def selection(routing, probs, experts, capacity):
    route_hits = (
        routing[:, :, None] == jnp.arange(experts, dtype=jnp.int32)[None, None, :]
    ).astype(jnp.float32)
    occupied = jnp.sum(route_hits, axis=1)
    weight = jnp.einsum("rke,rk->re", route_hits, probs.astype(jnp.float32))
    before = jnp.cumsum(occupied, axis=0) - occupied
    slot_index = jnp.arange(capacity, dtype=jnp.float32)
    chosen = occupied.T[:, None, :] * (before.T[:, None, :] == slot_index[None, :, None]).astype(
        jnp.float32
    )
    return (route_hits, weight, chosen)


def shards(tokens, upstream, probs, routing, row_rollout, group_ids, rewards, w_gate, w_up, w_down):
    f32 = jnp.float32
    bf16 = jnp.bfloat16
    experts = lax.axis_size("expert")
    n_x = lax.axis_size("x")
    n_core = lax.axis_size("core")
    n_t = lax.axis_size("tensor")
    group_rows, features = tokens.shape
    routes_per_row = routing.shape[1]
    capacity = min(group_rows, 5 * group_rows * routes_per_row // (4 * experts))
    slots = experts * capacity
    chunk = slots + 8
    per_core = n_x * chunk

    advantage = advantages(row_rollout, group_ids, rewards)
    cotangent = (advantage[:, None] * upstream.astype(f32)).astype(bf16)
    route_hits, weight, chosen = selection(routing, probs, experts, capacity)
    chosen_half = chosen.astype(bf16)

    both = jnp.stack([tokens, cotangent])
    packed = jnp.einsum(
        "ecr,arf->aecf", chosen_half, both, preferred_element_type=f32
    ).astype(bf16)
    packed_prob = jnp.einsum("ecr,re->ec", chosen, weight).astype(bf16)
    prob_row = jnp.zeros((experts, 1, features), bf16).at[:, 0, :capacity].set(packed_prob)
    prob_rows = jnp.stack([jnp.zeros_like(prob_row), prob_row])
    packed = jnp.concatenate([packed, prob_rows], axis=2)
    arrived = lax.all_to_all(packed, "expert", split_axis=1, concat_axis=1, tiled=True)
    extra = jnp.zeros((chunk - slots, features), bf16)
    extra_prob = extra.at[0, :slots].set(arrived[1, :, capacity, :capacity].reshape(slots))
    tok_rows = jnp.concatenate([arrived[0, :, :capacity].reshape(slots, features), extra_prob])
    cot_rows = jnp.concatenate([arrived[1, :, :capacity].reshape(slots, features), extra])

    def gather(rows):
        g = lax.all_gather(rows, ("tensor", "x"), axis=0, tiled=True)
        g = lax.all_gather(g, "core", axis=0, tiled=True)
        return g.reshape(n_core, n_t, per_core, features)

    g_tok = gather(tok_rows)
    g_cot = gather(cot_rows)
    slot_prob = g_tok[:, 0].reshape(n_core, n_x, chunk, features)[:, :, slots, :chunk]
    slot_prob = slot_prob.reshape(n_core * per_core)

    wg = w_gate[0].reshape(n_t, features, -1)
    wu = w_up[0].reshape(n_t, features, -1)
    wd = w_down[0]
    hidden_width = wd.shape[0]
    wd = wd.reshape(hidden_width, n_t, features)

    def over_t(fn):
        return sum(fn(t) for t in range(n_t))

    gate = jnp.concatenate(
        [
            over_t(lambda t: jnp.dot(g_tok[c, t], wg[t], preferred_element_type=f32))
            for c in range(n_core)
        ]
    )
    up_part = jnp.concatenate(
        [
            over_t(lambda t: jnp.dot(g_tok[c, t], wu[t], preferred_element_type=f32))
            for c in range(n_core)
        ]
    )
    back_hidden = jnp.concatenate(
        [
            over_t(
                lambda t: jnp.einsum(
                    "sf,hf->sh", g_cot[c, t], wd[:, t], preferred_element_type=f32
                )
            )
            for c in range(n_core)
        ]
    )

    sigmoid_gate = jax.nn.sigmoid(gate)
    active = gate * sigmoid_gate
    hidden = (active * up_part).astype(bf16)
    hidden_wide = lax.optimization_barrier(hidden).astype(f32)
    route_part = jnp.sum(hidden_wide * back_hidden, axis=-1)
    scale = slot_prob.astype(f32)[:, None]
    scaled = scale * back_hidden
    grad_g = (scaled * up_part * sigmoid_gate * (1.0 + gate * (1.0 - sigmoid_gate))).astype(bf16)
    grad_u = (scaled * active).astype(bf16)
    weighted = (scale * hidden_wide).astype(bf16)

    def rows_of(a, c):
        return a[c * per_core:(c + 1) * per_core]

    grad_down = jnp.concatenate(
        [
            sum(
                jnp.dot(rows_of(weighted, c).T, g_cot[c, t], preferred_element_type=f32)
                for c in range(n_core)
            ).astype(bf16)
            for t in range(n_t)
        ],
        axis=1,
    )
    grad_gate = jnp.concatenate(
        [
            sum(
                jnp.dot(g_tok[c, t].T, rows_of(grad_g, c), preferred_element_type=f32)
                for c in range(n_core)
            ).astype(bf16)
            for t in range(n_t)
        ],
        axis=0,
    )
    grad_up = jnp.concatenate(
        [
            sum(
                jnp.dot(g_tok[c, t].T, rows_of(grad_u, c), preferred_element_type=f32)
                for c in range(n_core)
            ).astype(bf16)
            for t in range(n_t)
        ],
        axis=0,
    )

    route_hi = route_part.astype(bf16)
    route_lo = (route_part - route_hi.astype(f32)).astype(bf16)
    route_pair = jnp.stack([route_hi, route_lo]).reshape(2, n_core, n_x, chunk)
    row_id = lax.broadcasted_iota(jnp.int32, (n_x, chunk, features), 1)
    col_id = lax.broadcasted_iota(jnp.int32, (n_x, chunk, features), 2)
    pieces = []
    for c in range(n_core):
        gc = rows_of(grad_g, c)
        uc = rows_of(grad_u, c)
        pad = jnp.zeros((n_x, chunk, features - chunk), bf16)
        hi_rows = jnp.concatenate([route_pair[0, c][:, None, :].repeat(chunk, 1), pad], axis=2)
        lo_rows = jnp.concatenate([route_pair[1, c][:, None, :].repeat(chunk, 1), pad], axis=2)
        for t in range(n_t):
            term = (
                jnp.einsum("sk,fk->sf", gc, wg[t], preferred_element_type=f32)
                + jnp.einsum("sk,fk->sf", uc, wu[t], preferred_element_type=f32)
            ).astype(bf16).reshape(n_x, chunk, features)
            term = jnp.where(row_id == slots, hi_rows, term)
            term = jnp.where(row_id == slots + 1, lo_rows, term)
            pieces.append(term)
    product = jnp.stack(pieces).reshape(n_core * n_t * per_core, features)
    summed = lax.psum_scatter(product, "core", scatter_dimension=0, tiled=True)
    own_rows = lax.psum_scatter(summed, ("tensor", "x"), scatter_dimension=0, tiled=True)

    own_route = (
        own_rows[slots, :slots].astype(f32) + own_rows[slots + 1, :slots].astype(f32)
    ).astype(bf16)
    route_row = jnp.zeros((experts, 1, features), bf16).at[:, 0, :capacity].set(
        own_route.reshape(experts, capacity)
    )
    back_pack = jnp.concatenate(
        [own_rows[:slots].reshape(experts, capacity, features), route_row], axis=1
    )
    home = lax.all_to_all(back_pack, "expert", split_axis=0, concat_axis=0, tiled=True)
    input_grad = jnp.einsum(
        "ecr,ecf->rf", chosen_half, home[:, :capacity], preferred_element_type=f32
    ).astype(bf16)
    per_expert = jnp.einsum("ecr,ec->re", chosen, home[:, capacity, :capacity].astype(f32))
    route_grad = jnp.einsum("rke,re->rk", route_hits, per_expert).astype(bf16)
    return (input_grad, route_grad, grad_gate[None], grad_up[None], grad_down[None])


def solution(mesh):
    n_dp = mesh.shape["dp"]
    devices = np.asarray(mesh.devices).reshape(
        n_dp // CORES, CORES, mesh.shape["expert"], mesh.shape["tensor"]
    )
    split_mesh = Mesh(devices, ("x", "core", "expert", "tensor"))
    rows = DP + ("expert",)
    in_specs = (
        P(rows, "tensor"),
        P(rows, "tensor"),
        P(rows, None),
        P(rows, None),
        P(rows),
        P(),
        P(),
        P("expert", None, DP + ("tensor",)),
        P("expert", None, DP + ("tensor",)),
        P("expert", DP + ("tensor",), None),
    )
    out_specs = (
        P(rows, "tensor"),
        P(rows, None),
        P("expert", None, DP + ("tensor",)),
        P("expert", None, DP + ("tensor",)),
        P("expert", DP + ("tensor",), None),
    )
    return jax.shard_map(
        shards, mesh=split_mesh, in_specs=in_specs, out_specs=out_specs, check_vma=False
    )
```

time: 367 us -> 436 us (1.19)
  waiting for transfers between devices: 164 us -> 263 us
  blocking collectives: 87.4 us -> 46.3 us
  other arithmetic: 17.8 us -> 24.2 us
    all_gather x2 -> x4, waiting for transfers between devices: 85.6 us -> 170 us  [the longest x2 122 us: gather(): g = lax.all_gather(rows, ('tensor', 'x'), axis=0, tiled=True)]
    psum x1 -> x0, blocking collectives: 28.3 us -> none  [shards(): route_total = lax.psum(route_part, ('dp', 'tensor'))]
    unnamed x1 -> x0, blocking collectives: 12.8 us -> none
    reduce_scatter x1 -> x2, waiting for transfers between devices: 62.1 us -> 73.4 us  [the longest x1 48 us: shards(): lax.psum_scatter(summed, ('tensor', 'x'), scatter_dimension=0, tiled=True)]
    slice x2 -> x4, local copies, waits for them, and re-layouts: 5.22 us -> 9.13 us  [the longest x1 5.11 us: shards(): arrived[1, :, :capacity].reshape(slots, features)]
    dot_general x16 -> x32, matrix products: 47.6 us -> 51.5 us  [the longest x4 8.04 us: shards(): jnp.einsum('sk,fk->sf', uc, wu[t], preferred_element_type=f32)]
    another operation x1 -> x2, other arithmetic: 8.12 us -> 10.6 us  [shards(): product = jnp.stack(pieces).reshape(n_core * n_t * per_core, features)]
  transfers between devices with their start and end apart: 4 -> 7, of which waited for: 4 -> 7; matrix products, arithmetic and copies ran while one was open for 11% -> 9% of each run, Pallas kernels for 0% -> 0%
where the time goes in v2:
time: 436 us
  waiting for transfers between devices  263 us (60%)
  matrix products  56.7 us (13%)
  blocking collectives  46.3 us (11%)
  other arithmetic  24.2 us (6%)
  local copies, waits for them, and re-layouts  20.8 us (5%)
  between operations  14.6 us (3%)
  starting transfers between devices  9.79 us (2%)
    all_gather x2, waiting for transfers between devices, gather(): g = lax.all_gather(rows, ('tensor', 'x'), axis=0, tiled=True)  122 us
    all_gather x2, waiting for transfers between devices, gather(): g = lax.all_gather(g, 'core', axis=0, tiled=True)  48.4 us
    reduce_scatter x1, waiting for transfers between devices, shards(): lax.psum_scatter(summed, ('tensor', 'x'), scatter_dimension=0, tiled=True)  48 us
    all_to_all x1, blocking collectives, shards(): lax.all_to_all(packed, 'expert', split_axis=1, concat_axis=1, tiled=True)  46.3 us
    reduce_scatter x1, waiting for transfers between devices, shards(): summed = lax.psum_scatter(product, 'core', scatter_dimension=0, tiled=True)  25.4 us
    all_to_all x1, waiting for transfers between devices, shards(): lax.all_to_all(back_pack, 'expert', split_axis=0, concat_axis=0, tiled=True)  19.4 us
    another operation x2, other arithmetic, shards(): product = jnp.stack(pieces).reshape(n_core * n_t * per_core, features)  10.6 us
    all_to_all x1, starting transfers between devices, shards(): lax.all_to_all(back_pack, 'expert', split_axis=0, concat_axis=0, tiled=True)  9.55 us
  transfers between devices with their start and end apart: 7, of which 7 were waited for; matrix products, arithmetic and copies ran while one was open for 9% of the time, Pallas kernels for 0%

profile of v2, /device:TPU:32, one launch (start us, length us, event | category | flops | bytes accessed | tf_op | source)
XLA Modules:
  0.0 435.5 jit_solution(13245218322465069987)
XLA Ops:
  7.2 0.8 convert_reduce_fusion
  8.7 0.9 fusion.88
  9.7 1.0 fusion.86
  10.7 1.0 fusion.115
  12.4 0.8 convolution_bitcast_fusion.1
  13.3 0.9 fusion.113
  14.2 1.3 fusion.10
  15.6 1.4 copy.47
  17.0 46.3 %all_to_all.10 = bf16[2,16,6,3584]{3,0,2,1:T(2,128)(2,1)S(1)} all-to-all(bf16[2,16,6,3584]{3,0,2,1:T(2,128)(2,1)S(1)} %copy.47), channel_id=1, replica_groups=mesh['x'=4,'core'=2,'expert'=16,'tensor'=2] {'expert'}, dimensions={1} | all-to-all | bytes 2752512 | tf_op jit(solution)/shard_map/all_to_all | solution.py:65
  63.4 5.1 %slice_reduce_fusion = (bf16[16,5,3584]{2,1,0:T(8,128)(2,1)S(1)}, bf16[16,5,3584]{2,1,0:T(8,128)(2,1)S(1)}) fusion(bf16[2,16,6,3584]{3,0,2,1:T(2,128)(2,1)S(1)} %all_to_all.10), kind=kLoop, calls=%fused_computation.79 | loop fusion | bytes 2293760 | tf_op jit(solution)/shard_map/slice | solution.py:69
  68.5 1.0 reshape_squeeze.16
  69.7 1.9 fusion.65
  71.9 0.9 concatenate.53
  72.9 57.4 %all-gather.5.cloned.1.call-done = bf16[704,3584]{1,0:T(8,128)(2,1)} async-done(((bf16[88,3584]{1,0:T(8,128)(2,1)}), bf16[704,3584]{1,0:T(8,128)(2,1)}) %all-gather.5.cloned.1.call-update) | async-done | bytes 5046288 | tf_op jit(solution)/shard_map/all_gather | solution.py:72
  130.4 64.2 %all-gather.9.cloned.1.call-done = bf16[704,3584]{1,0:T(8,128)(2,1)} async-done(((bf16[88,3584]{1,0:T(8,128)(2,1)}), bf16[704,3584]{1,0:T(8,128)(2,1)}) %all-gather.9.cloned.1.call-update) | async-done | bytes 5046288 | tf_op jit(solution)/shard_map/all_gather | solution.py:72
  194.7 4.0 copy.48
  198.7 25.4 %all-gather.7.cloned.1.call-done = bf16[1408,3584]{1,0:T(8,128)(2,1)} async-done(((bf16[704,3584]{1,0:T(8,128)(2,1)}), bf16[1408,3584]{1,0:T(8,128)(2,1)}) %all-gather.7.cloned.1.call-update) | async-done | bytes 10092560 | tf_op jit(solution)/shard_map/all_gather | solution.py:73
  224.1 2.7 fusion.26
  226.8 3.3 fusion.32
  230.2 0.8 fusion.27
  231.1 0.8 fusion.33
  231.9 23.0 %all-gather.11.cloned.1.call-done = bf16[1408,3584]{1,0:T(8,128)(2,1)} async-done(((bf16[704,3584]{1,0:T(8,128)(2,1)}), bf16[1408,3584]{1,0:T(8,128)(2,1)}) %all-gather.11.cloned.1.call-update) | async-done | bytes 10092560 | tf_op jit(solution)/shard_map/all_gather | solution.py:73
  254.9 2.9 fusion.18
  257.8 2.7 fusion.21
  260.5 2.9 slice.261
  263.6 0.8 fusion.41
  264.5 0.8 fusion.39
  265.3 1.1 copy-done.6
  266.4 0.8 fusion.40
  267.2 1.5 fusion.38
  268.7 0.9 fusion.43
  269.6 0.9 fusion.42
  270.6 1.2 multiply_convert_fusion
  271.8 0.8 fusion.59
  272.6 0.8 fusion.53
  273.5 0.8 fusion.55
  274.3 0.8 fusion.61
  275.8 1.0 fusion.2
  276.8 2.4 fusion.3
  279.2 2.4 fusion.1
  281.5 2.3 fusion
  284.0 5.0 %fusion.13 = (bf16[1,4,88,3584]{3,2,1,0:T(8,128)(2,1)S(1)}, bf16[1,4,88,3584]{3,2,1,0:T(8,128)(2,1)S(1)}, bf16[1,4,88,3584]{3,2,1,0:T(8,128)(2,1)S(1)}, bf16[1,4,88,3584]{3,2,1,0:T(8,128)(2,1)S(1)}) fusion(bf16[4,88,88]{2,1,0:T(8,128)(2,1)S(1)} %reshape.247, bf16[4,88,3584]{2,1,0:T(8,128)(2,1)} %bitcast.209, bf16[4,88,88]{2,1,0:T(8,128)(2,1)S(1)} %reshape.248, ...), kind=kLoop, calls=%fused_computation.35 | loop fusion | flops 10092544 | bytes 20433072 | tf_op jit(solution)/shard_map/stack | solution.py:178
  289.0 5.6 %pad_maximum_fusion = bf16[4,4,88,3584]{3,2,1,0:T(8,128)(2,1)} fusion(bf16[1,4,88,3584]{3,2,1,0:T(8,128)(2,1)S(1)} %get-tuple-element.58, bf16[1,4,88,3584]{3,2,1,0:T(8,128)(2,1)S(1)} %get-tuple-element.59, bf16[1,4,88,3584]{3,2,1,0:T(8,128)(2,1)S(1)} %get-tuple-element.49, bf16[1,4,88,3584]{3,2,1,0:T(8,128)(2,1)S(1)} %get-tuple-element.48), kind=kLoop, calls=%fused_computation | loop fusion | flops 15138816 | bytes 20185088 | tf_op jit(solution)/shard_map/stack | solution.py:178
  294.7 25.4 %reduce-scatter.3.cloned.1.call-done = bf16[704,3584]{1,0:T(8,128)(2,1)} async-done(((bf16[1408,3584]{1,0:T(8,128)(2,1)}), bf16[704,3584]{1,0:T(8,128)(2,1)}) %reduce-scatter.3.cloned.1.call-update) | async-done | bytes 5046288 | tf_op jit(solution)/shard_map/reduce_scatter | solution.py:179
  320.1 2.5 fusion.17
  322.6 2.4 fusion.19
  325.0 2.8 fusion.25
  328.0 0.9 fusion.29
  328.9 0.9 fusion.24
  329.9 0.8 slice-done.10
  332.4 1.9 fusion.4
  334.3 1.9 fusion.5
  336.2 1.0 fusion.6
  337.2 1.4 maximum_bitcast_fusion.2
  338.6 48.0 %reduce-scatter.5.cloned.1.call-done = bf16[88,3584]{1,0:T(8,128)(2,1)} async-done(((bf16[704,3584]{1,0:T(8,128)(2,1)}), bf16[88,3584]{1,0:T(8,128)(2,1)}) %reduce-scatter.5.cloned.1.call-update) | async-done | bytes 630800 | tf_op jit(solution)/shard_map/reduce_scatter | solution.py:180
  386.6 1.1 slice.269
  388.0 0.8 fusion.134
  388.8 1.2 fusion.44
  390.0 9.5 %all-to-all-start.1 = ((bf16[16,6,3584]{2,1,0:T(8,128)(2,1)}), bf16[16,6,3584]{2,1,0:T(8,128)(2,1)S(1)}, u32[]{:S(2)}, u32[]{:S(2)}) async-start(bf16[16,6,3584]{2,1,0:T(8,128)(2,1)} %fusion.44), calls=%async_computation.3 | async-start | bytes 1835008 | tf_op jit(solution)/shard_map/all_to_all | solution.py:191
  399.6 2.7 fusion.28
  402.3 2.8 fusion.7
  405.1 2.1 maximum_bitcast_fusion
  407.2 19.4 %all-to-all-done.1 = bf16[16,6,3584]{2,1,0:T(8,128)(2,1)S(1)} async-done(((bf16[16,6,3584]{2,1,0:T(8,128)(2,1)}), bf16[16,6,3584]{2,1,0:T(8,128)(2,1)S(1)}, u32[]{:S(2)}, u32[]{:S(2)}) %all-to-all-start.1) | async-done | bytes 688160 | tf_op jit(solution)/shard_map/all_to_all | solution.py:191
  426.6 0.9 fusion.11
  (95 shorter events, 6.9 us)
Async XLA Ops:
  7.2 3.5 copy-start
  7.2 123.1 %all-gather.5.cloned.1.call-start = ((), (), s32[]{:S(2)}) async-start(), calls=%async_computation.4 | async-start | bytes 5677056 | tf_op jit(solution)/shard_map/all_gather | solution.py:72
  71.6 123.0 %all-gather.9.cloned.1.call-start = ((), (), s32[]{:S(2)}) async-start(), calls=%async_computation.6 | async-start | bytes 5677056 | tf_op jit(solution)/shard_map/all_gather | solution.py:72
  72.8 151.3 %all-gather.7.cloned.1.call-start = ((), (), s32[]{:S(2)}) async-start(), calls=%async_computation.5 | async-start | bytes 15138816 | tf_op jit(solution)/shard_map/all_gather | solution.py:73
  130.3 124.6 %all-gather.11.cloned.1.call-start = ((), (), s32[]{:S(2)}) async-start(), calls=%async_computation.7 | async-start | bytes 15138816 | tf_op jit(solution)/shard_map/all_gather | solution.py:73
  194.6 29.5 %copy-start.3 = (bf16[1,7168,128]{2,1,0:T(8,128)(2,1)S(1)}, bf16[1,7168,128]{2,1,0:T(8,128)(2,1)}, u32[]{:S(2)}) copy-start(bf16[1,7168,128]{2,1,0:T(8,128)(2,1)} %param.24) | copy-start | bytes 5505028
  194.6 125.4 %reduce-scatter.3.cloned.1.call-start = ((), (), s32[]{:S(2)}) async-start(), calls=%async_computation.8 | async-start | bytes 15138816 | tf_op jit(solution)/shard_map/reduce_scatter | solution.py:179
  224.1 6.0 %copy-start.2 = (bf16[1408,3584]{1,0:T(8,128)(2,1)S(1)}, bf16[1408,3584]{1,0:T(8,128)(2,1)}, u32[]{:S(2)}) copy-start(bf16[1408,3584]{1,0:T(8,128)(2,1)} %all-gather.7.cloned.1.call-done) | copy-start | bytes 30277636
  226.8 3.4 copy-start.5
  254.9 2.9 copy-start.10
  254.9 8.5 %slice-start = ((s8[10092544]{0:T(1024)(128)(4,1)}), s8[4194304]{0:T(1024)(128)(4,1)S(1)}, s32[]{:S(2)}) async-start(s8[10092544]{0:T(1024)(128)(4,1)} %bitcast.192), calls=%async_computation.10 | async-start | bytes 8388608
  257.8 5.6 %slice-start.1 = ((s8[10092544]{0:T(1024)(128)(4,1)}), s8[4194304]{0:T(1024)(128)(4,1)S(1)}, s32[]{:S(2)}) async-start(s8[10092544]{0:T(1024)(128)(4,1)} %bitcast.192), calls=%async_computation.11 | async-start | bytes 8388608
  260.5 3.1 slice-start.2
  263.6 5.1 %slice-start.6 = ((s8[10092544]{0:T(1024)(128)(4,1)}), s8[4194304]{0:T(1024)(128)(4,1)S(1)}, s32[]{:S(2)}) async-start(s8[10092544]{0:T(1024)(128)(4,1)} %bitcast.214), calls=%async_computation.16 | async-start | bytes 8388608
  264.4 1.9 copy-start.6
  264.5 4.2 slice-start.7
  266.4 2.3 slice-start.8
  269.6 2.2 copy-start.7
  274.3 1.5 copy-start.4
  294.6 92.0 %reduce-scatter.5.cloned.1.call-start = ((), (), s32[]{:S(2)}) async-start(), calls=%async_computation.9 | async-start | bytes 5677056 | tf_op jit(solution)/shard_map/reduce_scatter | solution.py:180
  320.1 7.8 %slice-start.3 = ((s8[10092544]{0:T(1024)(128)(4,1)}), s8[1703936]{0:T(1024)(128)(4,1)S(1)}, s32[]{:S(2)}) async-start(s8[10092544]{0:T(1024)(128)(4,1)} %bitcast.198), calls=%async_computation.13 | async-start | bytes 3407872
  320.1 7.8 %slice-start.4 = ((s8[10092544]{0:T(1024)(128)(4,1)}), s8[4194304]{0:T(1024)(128)(4,1)S(1)}, s32[]{:S(2)}) async-start(s8[10092544]{0:T(1024)(128)(4,1)} %bitcast.198), calls=%async_computation.14 | async-start | bytes 8388608
  325.0 3.0 slice-start.5
  325.0 4.8 %slice-start.9 = ((s8[10092544]{0:T(1024)(128)(4,1)}), s8[4194304]{0:T(1024)(128)(4,1)S(1)}, s32[]{:S(2)}) async-start(s8[10092544]{0:T(1024)(128)(4,1)} %bitcast.218), calls=%async_computation.19 | async-start | bytes 8388608
  328.0 2.7 slice-start.10
  328.9 2.2 slice-start.11
  390.0 36.6 %all-to-all-start.1 = ((bf16[16,6,3584]{2,1,0:T(8,128)(2,1)}), bf16[16,6,3584]{2,1,0:T(8,128)(2,1)S(1)}, u32[]{:S(2)}, u32[]{:S(2)}) async-start(bf16[16,6,3584]{2,1,0:T(8,128)(2,1)} %fusion.44), calls=%async_computation.3 | async-start | bytes 1835008 | tf_op jit(solution)/shard_map/all_to_all | solution.py:191
  402.2 2.9 copy-start.8
  402.2 2.9 copy-start.9
  402.3 26.4 %copy-start.1 = (bf16[8,8]{1,0:T(8,128)(2,1)S(1)}, bf16[8,8]{1,0:T(8,128)(2,1)}, u32[]{:S(2)}) copy-start(bf16[8,8]{1,0:T(8,128)(2,1)} %param.18) | copy-start | bytes 388
  405.1 22.8 %copy-start.11 = (s32[8,8]{1,0:T(8,128)S(1)}, s32[8,8]{1,0:T(8,128)}, u32[]{:S(2)}) copy-start(s32[8,8]{1,0:T(8,128)} %param.19) | copy-start | bytes 772
Sparse Core Ops, SparseCore 0:
  71.7 58.5 all-gather.4
  132.7 61.9 all-gather.8
  196.4 27.6 all-gather.6
  225.8 29.0 all-gather.10
  294.7 25.2 reduce-scatter.2
  322.7 63.9 reduce-scatter.4

commit v3 on v1

--- a/solution.py
+++ b/solution.py
@@ -40,7 +40,6 @@
     routes_per_row = routing.shape[1]
     capacity = min(group_rows, 5 * group_rows * routes_per_row // (4 * experts))
     slots = experts * capacity
-    all_slots = dp_size * slots
 
     advantage = advantages(row_rollout, group_ids, rewards)
     cotangent = (advantage[:, None] * upstream.astype(f32)).astype(bf16)
@@ -56,15 +55,18 @@
     prob_rows = jnp.stack([jnp.zeros_like(prob_row), prob_row])
     packed = jnp.concatenate([packed, prob_rows], axis=2)
     arrived = lax.all_to_all(packed, "expert", split_axis=1, concat_axis=1, tiled=True)
-    tok_rows = arrived[0, :, :capacity].reshape(slots, features)
-    cot_rows = arrived[1, :, :capacity].reshape(slots, features)
-    slot_prob_local = arrived[1, :, capacity, :capacity].reshape(slots)
+    chunk = slots + 8
+    all_rows = dp_size * chunk
+    extra = jnp.zeros((chunk - slots, features), bf16)
+    extra_prob = extra.at[0, :slots].set(arrived[1, :, capacity, :capacity].reshape(slots))
+    tok_rows = jnp.concatenate([arrived[0, :, :capacity].reshape(slots, features), extra_prob])
+    cot_rows = jnp.concatenate([arrived[1, :, :capacity].reshape(slots, features), extra])
 
     g_tok = lax.all_gather(tok_rows, ("tensor", "dp"), axis=0, tiled=True)
-    g_tok = g_tok.reshape(tensor_size, all_slots, features)
+    g_tok = g_tok.reshape(tensor_size, all_rows, features)
     g_cot = lax.all_gather(cot_rows, ("tensor", "dp"), axis=0, tiled=True)
-    g_cot = g_cot.reshape(tensor_size, all_slots, features)
-    slot_prob = lax.all_gather(slot_prob_local, "dp", axis=0, tiled=True)
+    g_cot = g_cot.reshape(tensor_size, all_rows, features)
+    slot_prob = g_tok[0].reshape(dp_size, chunk, features)[:, slots, :chunk].reshape(all_rows)
 
     wg = w_gate[0].reshape(tensor_size, features, -1)
     wu = w_up[0].reshape(tensor_size, features, -1)
@@ -72,12 +74,12 @@
     hidden_width = wd.shape[0]
     wd = wd.reshape(hidden_width, tensor_size, features)
 
-    gate = sum(
-        jnp.dot(g_tok[t], wg[t], preferred_element_type=f32) for t in range(tensor_size)
+    w_in = jnp.concatenate([wg, wu], axis=2)
+    gate_up = sum(
+        jnp.dot(g_tok[t], w_in[t], preferred_element_type=f32) for t in range(tensor_size)
     )
-    up_part = sum(
-        jnp.dot(g_tok[t], wu[t], preferred_element_type=f32) for t in range(tensor_size)
-    )
+    gate = gate_up[:, :hidden_width]
+    up_part = gate_up[:, hidden_width:]
     back_hidden = sum(
         jnp.einsum("sf,hf->sh", g_cot[t], wd[:, t], preferred_element_type=f32)
         for t in range(tensor_size)
@@ -93,9 +95,6 @@
     grad_g = (scaled * up_part * sigmoid_gate * (1.0 + gate * (1.0 - sigmoid_gate))).astype(bf16)
     grad_u = (scaled * active).astype(bf16)
     weighted = (scale * hidden_wide).astype(bf16)
-
-    route_total = lax.psum(route_part, ("dp", "tensor"))
-    route_total, grad_g_p, grad_u_p = lax.optimization_barrier((route_total, grad_g, grad_u))
 
     grad_down = jnp.concatenate(
         [
@@ -119,24 +118,35 @@
         axis=0,
     )
 
+    route_hi = route_part.astype(bf16).reshape(dp_size, chunk)
+    route_lo = (route_part.reshape(dp_size, chunk) - route_hi.astype(f32)).astype(bf16)
+    carry = jnp.zeros((dp_size, chunk, hidden_width), bf16)
+    carry = carry.at[:, slots, :chunk].set(route_hi).at[:, slots + 1, :chunk].set(route_lo)
+    lhs = jnp.concatenate([grad_g, grad_u, carry.reshape(all_rows, hidden_width)], axis=1)
+    eye = (
+        lax.broadcasted_iota(jnp.int32, (features, hidden_width), 0)
+        == lax.broadcasted_iota(jnp.int32, (features, hidden_width), 1)
+    ).astype(bf16)
+    w_out = jnp.concatenate([wg, wu, jnp.broadcast_to(eye, wg.shape)], axis=2)
     product = jnp.stack(
         [
-            (
-                jnp.einsum("sk,fk->sf", grad_g_p, wg[t], preferred_element_type=f32)
-                + jnp.einsum("sk,fk->sf", grad_u_p, wu[t], preferred_element_type=f32)
-            ).astype(bf16)
+            jnp.einsum("sk,fk->sf", lhs, w_out[t], preferred_element_type=f32).astype(bf16)
             for t in range(tensor_size)
         ]
-    ).reshape(tensor_size * all_slots, features)
+    ).reshape(tensor_size * all_rows, features)
     own_rows = lax.psum_scatter(product, ("tensor", "dp"), scatter_dimension=0, tiled=True)
 
-    own_route = lax.dynamic_slice_in_dim(
-        route_total, lax.axis_index("dp") * slots, slots, 0
+    own_route = (
+        own_rows[slots, :slots].astype(f32) + own_rows[slots + 1, :slots].astype(f32)
     ).astype(bf16)
+    partner = lax.ppermute(own_route, "tensor", [(i, i ^ 1) for i in range(tensor_size)])
+    own_route = jnp.where(lax.axis_index("tensor") == 0, own_route, partner)
     route_row = jnp.zeros((experts, 1, features), bf16).at[:, 0, :capacity].set(
         own_route.reshape(experts, capacity)
     )
-    back_pack = jnp.concatenate([own_rows.reshape(experts, capacity, features), route_row], axis=1)
+    back_pack = jnp.concatenate(
+        [own_rows[:slots].reshape(experts, capacity, features), route_row], axis=1
+    )
     home = lax.all_to_all(back_pack, "expert", split_axis=0, concat_axis=0, tiled=True)
     input_grad = jnp.einsum(
         "ecr,ecf->rf", chosen_half, home[:, :capacity], preferred_element_type=f32

time: 367 us -> 358 us (0.975)
  blocking collectives: 87.4 us -> 46.3 us
  waiting for transfers between devices: 164 us -> 184 us
  other arithmetic: 17.8 us -> 24.1 us
    psum x1 -> x0, blocking collectives: 28.3 us -> none  [shards(): route_total = lax.psum(route_part, ('dp', 'tensor'))]
    all_gather x1, waiting for transfers between devices: 35.4 us -> 49.8 us  [shards(): g_tok = lax.all_gather(tok_rows, ('tensor', 'dp'), axis=0, tiled=True)]
    unnamed x1 -> x0, blocking collectives: 12.8 us -> none
    concatenate x1 -> x3, other arithmetic: 1.15 us -> 6.17 us  [the longest x1 3.06 us: shards(): w_out = jnp.concatenate([wg, wu, jnp.broadcast_to(eye, wg.shape)], axis=2)]
    all_gather x1, waiting for transfers between devices: 50.1 us -> 54.5 us  [shards(): g_cot = lax.all_gather(cot_rows, ('tensor', 'dp'), axis=0, tiled=True)]
    dot_general x8 -> x4, matrix products: 22.5 us -> 18.2 us  [the longest x2 11.6 us: shards(): jnp.einsum('sk,fk->sf', lhs, w_out[t], preferred_element_type=f32)]
    slice x2 -> x6, local copies, waits for them, and re-layouts: 5.22 us -> 7.65 us  [the longest x1 5.18 us: shards(): arrived[0, :, :capacity].reshape(slots, features)]
  transfers between devices with their start and end apart: 4 -> 5, of which waited for: 4 -> 4; matrix products, arithmetic and copies ran while one was open for 11% -> 11% of each run, Pallas kernels for 0% -> 0%
where the time goes in v3:
time: 358 us; the launch traced here: 355 us
  waiting for transfers between devices  184 us (51%)
  matrix products  55.6 us (16%)
  blocking collectives  46.3 us (13%)
  other arithmetic  24.1 us (7%)
  local copies, waits for them, and re-layouts  19.7 us (6%)
  between operations  14.1 us (4%)
  starting transfers between devices  10.7 us (3%)
    reduce_scatter x1, waiting for transfers between devices, shards(): lax.psum_scatter(product, ('tensor', 'dp'), scatter_dimension=0, tiled=True)  64.6 us
    all_gather x1, waiting for transfers between devices, shards(): g_cot = lax.all_gather(cot_rows, ('tensor', 'dp'), axis=0, tiled=True)  54.5 us
    all_gather x1, waiting for transfers between devices, shards(): g_tok = lax.all_gather(tok_rows, ('tensor', 'dp'), axis=0, tiled=True)  49.8 us
    all_to_all x1, blocking collectives, shards(): lax.all_to_all(packed, 'expert', split_axis=1, concat_axis=1, tiled=True)  46.3 us
    all_to_all x1, waiting for transfers between devices, shards(): lax.all_to_all(back_pack, 'expert', split_axis=0, concat_axis=0, tiled=True)  15.4 us
    dot_general x2, matrix products, shards(): jnp.einsum('sk,fk->sf', lhs, w_out[t], preferred_element_type=f32)  11.6 us
    dot_general x2, matrix products, shards(): jnp.dot(g_tok[t].T, grad_g, preferred_element_type=f32).astype(bf16)  9.32 us
    dot_general x2, matrix products, shards(): jnp.einsum('sf,hf->sh', g_cot[t], wd[:, t], preferred_element_type=f32)  8.7 us
  transfers between devices with their start and end apart: 5, of which 4 were waited for; matrix products, arithmetic and copies ran while one was open for 11% of the time, Pallas kernels for 0%

profile of v3, /device:TPU:32, one launch (start us, length us, event | category | flops | bytes accessed | tf_op | source)
XLA Modules:
  0.0 354.9 jit_solution(5622345268903567653)
XLA Ops:
  7.2 0.8 convert_reduce_fusion
  8.0 0.7 convert_element_type.136
  8.7 0.9 fusion.42
  9.7 1.0 fusion.40
  10.7 1.0 fusion.51
  11.6 0.1 copy.46
  11.7 0.7 divide_subtract_fusion
  12.4 0.8 convolution_bitcast_fusion.1
  13.3 0.9 fusion.49
  14.2 1.3 fusion.2
  15.5 0.1 fusion.24
  15.6 1.4 copy.47
  17.0 46.3 %all_to_all.10 = bf16[2,16,6,3584]{3,0,2,1:T(2,128)(2,1)S(1)} all-to-all(bf16[2,16,6,3584]{3,0,2,1:T(2,128)(2,1)S(1)} %copy.47), channel_id=1, replica_groups=mesh['dp'=8,'expert'=16,'tensor'=2] {'expert'}, dimensions={1} | all-to-all | bytes 2752512 | tf_op jit(solution)/shard_map/all_to_all | solution.py:57
  63.4 5.2 %slice_reduce_fusion.1 = (bf16[16,5,3584]{2,1,0:T(8,128)(2,1)S(1)}, bf16[16,5,3584]{2,1,0:T(8,128)(2,1)S(1)}) fusion(bf16[2,16,6,3584]{3,0,2,1:T(2,128)(2,1)S(1)} %all_to_all.10), kind=kLoop, calls=%fused_computation.51 | loop fusion | bytes 2293760 | tf_op jit(solution)/shard_map/slice | solution.py:62
  68.5 1.0 reshape_squeeze.20
  69.6 0.1 reshape.250
  69.7 1.9 fusion.35
  71.7 0.2 reshape_squeeze.22
  72.0 0.9 concatenate.44
  72.9 0.2 reduce-scatter.2.cloned.1.call-start
  73.1 0.6 copy-done.4
  73.7 2.3 copy.48
  76.1 0.1 broadcast_in_dim.8
  76.2 1.3 copy-done.6
  77.5 0.6 copy-done.8
  78.0 3.1 pad_maximum_fusion.1
  81.1 49.8 %all-gather.3.cloned.1.call-done = bf16[1408,3584]{1,0:T(8,128)(2,1)} async-done(((bf16[88,3584]{1,0:T(8,128)(2,1)}), bf16[1408,3584]{1,0:T(8,128)(2,1)}) %all-gather.3.cloned.1.call-update) | async-done | bytes 10092560 | tf_op jit(solution)/shard_map/all_gather | solution.py:65
  130.9 2.4 slice-done.5
  133.5 4.3 %fusion.17 = f32[704,256]{1,0:T(8,128)S(1)} fusion(bf16[2,3584,128]{2,1,0:T(8,128)(2,1)} %bitcast.112, bf16[2,3584,128]{2,1,0:T(8,128)(2,1)S(1)} %bitcast.110, bf16[1408,3584]{1,0:T(8,128)(2,1)} %all-gather.3.cloned.1.call-done), kind=kOutput, calls=%fused_computation.34 | convolution fusion | flops 1295515648 | bytes 9437184 | tf_op jit(solution)/shard_map/dot_general | solution.py:79
  137.8 1.3 copy-done.2
  139.1 0.5 copy-done.7
  139.6 0.5 copy-done.9
  140.1 2.3 fusion.25
  142.4 54.5 %all-gather.5.cloned.1.call-done = bf16[1408,3584]{1,0:T(8,128)(2,1)} async-done(((bf16[88,3584]{1,0:T(8,128)(2,1)}), bf16[1408,3584]{1,0:T(8,128)(2,1)}) %all-gather.5.cloned.1.call-update) | async-done | bytes 10092560 | tf_op jit(solution)/shard_map/all_gather | solution.py:67
  196.9 4.0 %fusion.4 = f32[704,128]{1,0:T(8,128)S(1)} fusion(bf16[1408,3584]{1,0:T(8,128)(2,1)} %all-gather.5.cloned.1.call-done, bf16[128,2,3584]{0,2,1:T(8,128)(2,1)S(1)} %bitcast.107), kind=kOutput, calls=%fused_computation.16 | convolution fusion | flops 645922816 | bytes 6324224 | tf_op jit(solution)/shard_map/sf,hf->sh/dot_general | solution.py:84
  200.9 4.7 %multiply_convert_fusion.2 = (bf16[704,128]{1,0:T(8,128)(2,1)S(1)}, bf16[704,128]{1,0:T(8,128)(2,1)}, bf16[704,128]{1,0:T(8,128)(2,1)S(1)}, f32[704,128]{1,0:T(8,128)S(1)}) fusion(f32[704,256]{1,0:T(8,128)S(1)} %copy-done.13, f32[704]{0:T(1024)S(1)} %reshape.255, f32[704,128]{1,0:T(8,128)S(1)} %fusion.4, bf16[128,2,3584]{0,2,1:T(8,128)(2,1)S(1)} %bitcast.108, ...), kind=kOutput, calls=%fused_computation.65 | convolution fusion | flops 647454720 | bytes 7950336 | tf_op jit(solution)/shard_map/sf,hf->sh/dot_general | solution.py:84
  205.7 0.2 fusion.37
  205.9 0.1 reduce_sum.35
  206.0 0.2 scatter.21
  206.3 7.0 %fusion = bf16[1,704,3584]{2,1,0:T(8,128)(2,1)} fusion(bf16[2,3584,384]{2,1,0:T(8,128)(2,1)} %pad_maximum_fusion.1, bf16[704,128]{1,0:T(8,128)(2,1)S(1)} %bitcast.116, bf16[704,128]{1,0:T(8,128)(2,1)} %get-tuple-element.68, bf16[704,128]{1,0:T(8,128)(2,1)S(1)} %get-tuple-element.67), kind=kOutput, calls=%fused_computation.3 | convolution fusion | flops 1941913600 | bytes 8339456 | tf_op jit(solution)/shard_map/sk,fk->sf/dot_general | solution.py:133
  213.3 4.5 %fusion.1 = bf16[1,704,3584]{2,1,0:T(8,128)(2,1)} fusion(bf16[2,3584,384]{2,1,0:T(8,128)(2,1)S(1)} %bitcast.103, bf16[704,128]{1,0:T(8,128)(2,1)S(1)} %bitcast.117, bf16[704,128]{1,0:T(8,128)(2,1)S(1)} %copy-done.14, bf16[704,128]{1,0:T(8,128)(2,1)S(1)} %get-tuple-element.67), kind=kOutput, calls=%fused_computation.4 | convolution fusion | flops 1941913600 | bytes 8339456 | tf_op jit(solution)/shard_map/sk,fk->sf/dot_general | solution.py:133
  217.9 8.7 %pad_maximum_fusion = bf16[2,704,3584]{2,1,0:T(8,128)(2,1)} fusion(bf16[1,704,3584]{2,1,0:T(8,128)(2,1)} %fusion.1, bf16[1,704,3584]{2,1,0:T(8,128)(2,1)} %fusion), kind=kLoop, calls=%fused_computation | loop fusion | flops 5046272 | bytes 20185088 | tf_op jit(solution)/shard_map/stack | solution.py:131
  226.6 3.4 convolution_convert_fusion.3
  230.0 3.6 %convolution_convert_fusion.4 = bf16[128,3584]{1,0:T(8,128)(2,1)S(1)} fusion(bf16[1408,3584]{1,0:T(8,128)(2,1)} %all-gather.5.cloned.1.call-done, bf16[704,128]{1,0:T(8,128)(2,1)S(1)} %get-tuple-element.69, f32[704]{0:T(1024)S(1)} %reshape.255), kind=kOutput, calls=%fused_computation.8 | convolution fusion | flops 646651904 | bytes 6146816 | tf_op jit(solution)/shard_map/dot_general | solution.py:101
  233.6 4.5 %convolution_convert_fusion.5 = bf16[3584,128]{1,0:T(8,128)(2,1)S(1)} fusion(bf16[704,128]{1,0:T(8,128)(2,1)S(1)} %copy-done.14, bf16[1408,3584]{1,0:T(8,128)(2,1)} %all-gather.3.cloned.1.call-done), kind=kOutput, calls=%fused_computation.9 | convolution fusion | flops 646381568 | bytes 6144000 | tf_op jit(solution)/shard_map/dot_general | solution.py:115
  238.2 2.6 convolution_convert_fusion.6
  240.8 1.4 maximum_bitcast_fusion.2
  242.2 64.6 %reduce-scatter.2.cloned.1.call-done = bf16[88,3584]{1,0:T(8,128)(2,1)} async-done(((bf16[1408,3584]{1,0:T(8,128)(2,1)}), bf16[88,3584]{1,0:T(8,128)(2,1)}) %reduce-scatter.2.cloned.1.call-update) | async-done | bytes 630800 | tf_op jit(solution)/shard_map/reduce_scatter | solution.py:137
  306.8 0.8 fusion.70
  307.6 1.7 collective-permute-start
  309.3 5.1 %convolution_convert_fusion.7 = bf16[3584,128]{1,0:T(8,128)(2,1)} fusion(bf16[704,128]{1,0:T(8,128)(2,1)S(1)} %get-tuple-element.67, bf16[1408,3584]{1,0:T(8,128)(2,1)} %all-gather.3.cloned.1.call-done), kind=kOutput, calls=%fused_computation.11 | convolution fusion | flops 646381568 | bytes 6144000 | tf_op jit(solution)/shard_map/dot_general | solution.py:108
  314.3 0.2 reshape.253
  314.6 0.1 reshape.271
  314.7 1.2 fusion.34
  315.9 8.7 %all-to-all-start.1 = ((bf16[16,6,3584]{2,1,0:T(8,128)(2,1)}), bf16[16,6,3584]{2,1,0:T(8,128)(2,1)S(1)}, u32[]{:S(2)}, u32[]{:S(2)}) async-start(bf16[16,6,3584]{2,1,0:T(8,128)(2,1)} %fusion.34), calls=%async_computation.2 | async-start | bytes 1835008 | tf_op jit(solution)/shard_map/all_to_all | solution.py:150
  324.6 4.3 %convolution_convert_fusion.8 = bf16[3584,128]{1,0:T(8,128)(2,1)S(1)} fusion(bf16[704,128]{1,0:T(8,128)(2,1)S(1)} %get-tuple-element.67, bf16[1408,3584]{1,0:T(8,128)(2,1)} %all-gather.3.cloned.1.call-done), kind=kOutput, calls=%fused_computation.12 | convolution fusion | flops 646381568 | bytes 6144000 | tf_op jit(solution)/shard_map/dot_general | solution.py:108
  328.9 2.1 maximum_bitcast_fusion
  331.0 15.4 %all-to-all-done.1 = bf16[16,6,3584]{2,1,0:T(8,128)(2,1)S(1)} async-done(((bf16[16,6,3584]{2,1,0:T(8,128)(2,1)}), bf16[16,6,3584]{2,1,0:T(8,128)(2,1)S(1)}, u32[]{:S(2)}, u32[]{:S(2)}) %all-to-all-start.1) | async-done | bytes 688160 | tf_op jit(solution)/shard_map/all_to_all | solution.py:150
  346.4 0.9 fusion.9
  347.3 0.1 copy.77
  347.5 0.1 copy.67
  347.5 0.1 copy.68
  347.6 0.2 fusion.50
  347.8 0.6 convert_element_type.160
  (58 shorter events, 0.6 us)
Async XLA Ops:
  7.2 3.5 copy-start
  7.2 123.7 %all-gather.3.cloned.1.call-start = ((), (), s32[]{:S(2)}) async-start(), calls=%async_computation.3 | async-start | bytes 10723328 | tf_op jit(solution)/shard_map/all_gather | solution.py:65
  71.7 125.3 %all-gather.5.cloned.1.call-start = ((), (), s32[]{:S(2)}) async-start(), calls=%async_computation.4 | async-start | bytes 10723328 | tf_op jit(solution)/shard_map/all_gather | solution.py:67
  72.0 1.7 copy-start.4
  72.9 233.9 %reduce-scatter.2.cloned.1.call-start = ((), (), s32[]{:S(2)}) async-start(), calls=%async_computation.5 | async-start | bytes 10723328 | tf_op jit(solution)/shard_map/reduce_scatter | solution.py:137
  76.0 1.5 copy-start.6
  76.0 2.0 copy-start.8
  130.9 2.4 slice-start.5
  133.4 5.6 %copy-start.2 = (bf16[1408,3584]{1,0:T(8,128)(2,1)S(1)}, bf16[1408,3584]{1,0:T(8,128)(2,1)}, u32[]{:S(2)}) copy-start(bf16[1408,3584]{1,0:T(8,128)(2,1)} %all-gather.3.cloned.1.call-done) | copy-start | bytes 30277636
  133.5 6.1 %copy-start.7 = (bf16[1,7168,128]{2,1,0:T(8,128)(2,1)S(1)}, bf16[1,7168,128]{2,1,0:T(8,128)(2,1)}, u32[]{:S(2)}) copy-start(bf16[1,7168,128]{2,1,0:T(8,128)(2,1)} %param.28) | copy-start | bytes 5505028
  133.5 6.7 %copy-start.9 = (bf16[1,7168,128]{2,1,0:T(8,128)(2,1)S(1)}, bf16[1,7168,128]{2,1,0:T(8,128)(2,1)}, u32[]{:S(2)}) copy-start(bf16[1,7168,128]{2,1,0:T(8,128)(2,1)} %param.27) | copy-start | bytes 5505028
  140.1 56.8 %copy-start.5 = (bf16[1,128,7168]{1,2,0:T(8,128)(2,1)S(1)}, bf16[1,128,7168]{1,2,0:T(8,128)(2,1)}, u32[]{:S(2)}) copy-start(bf16[1,128,7168]{1,2,0:T(8,128)(2,1)} %copy.48) | copy-start | bytes 5505028
  196.9 4.0 %copy-start.13 = (f32[704,256]{1,0:T(8,128)S(1)}, f32[704,256]{1,0:T(8,128)}, u32[]{:S(2)}) copy-start(f32[704,256]{1,0:T(8,128)} %fusion.25) | copy-start | bytes 2162692
  200.9 12.4 %slice-start = ((s8[5505024]{0:T(1024)(128)(4,1)}), s8[1310720]{0:T(1024)(128)(4,1)S(1)}, s32[]{:S(2)}) async-start(s8[5505024]{0:T(1024)(128)(4,1)} %bitcast.102), calls=%async_computation.6 | async-start | bytes 2621440
  206.3 7.1 %slice-start.1 = ((s8[5505024]{0:T(1024)(128)(4,1)}), s8[4194304]{0:T(1024)(128)(4,1)S(1)}, s32[]{:S(2)}) async-start(s8[5505024]{0:T(1024)(128)(4,1)} %bitcast.102), calls=%async_computation.7 | async-start | bytes 8388608
  206.3 7.0 %copy-start.14 = (bf16[704,128]{1,0:T(8,128)(2,1)S(1)}, bf16[704,128]{1,0:T(8,128)(2,1)}, u32[]{:S(2)}) copy-start(bf16[704,128]{1,0:T(8,128)(2,1)} %get-tuple-element.68) | copy-start | bytes 540676
  230.0 8.1 %slice-start.2 = ((s8[10092544]{0:T(1024)(128)(4,1)}), s8[4194304]{0:T(1024)(128)(4,1)S(1)}, s32[]{:S(2)}) async-start(s8[10092544]{0:T(1024)(128)(4,1)} %bitcast.104), calls=%async_computation.8 | async-start | bytes 8388608
  230.0 8.1 %slice-start.3 = ((s8[10092544]{0:T(1024)(128)(4,1)}), s8[4194304]{0:T(1024)(128)(4,1)S(1)}, s32[]{:S(2)}) async-start(s8[10092544]{0:T(1024)(128)(4,1)} %bitcast.104), calls=%async_computation.9 | async-start | bytes 8388608
  233.6 4.5 %slice-start.4 = ((s8[10092544]{0:T(1024)(128)(4,1)}), s8[1703936]{0:T(1024)(128)(4,1)S(1)}, s32[]{:S(2)}) async-start(s8[10092544]{0:T(1024)(128)(4,1)} %bitcast.104), calls=%async_computation.10 | async-start | bytes 3407872
  307.6 6.8 %slice-start.6 = ((bf16[88,3584]{1,0:T(8,128)(2,1)}), bf16[80,3584]{1,0:T(8,128)(2,1)S(1)}, s32[]{:S(2)}) async-start(bf16[88,3584]{1,0:T(8,128)(2,1)} %reduce-scatter.2.cloned.1.call-done), calls=%async_computation.12 | async-start | bytes 1146880 | tf_op jit(solution)/shard_map/slice | solution.py:148
  307.6 7.0 %copy-start.3 = (bf16[88,3584]{1,0:T(8,128)(2,1)S(1)}, bf16[88,3584]{1,0:T(8,128)(2,1)}, u32[]{:S(2)}) copy-start(bf16[88,3584]{1,0:T(8,128)(2,1)} %reduce-scatter.2.cloned.1.call-done) | copy-start | bytes 1892356
  307.6 7.0 %collective-permute-start = (bf16[80]{0:T(256)(128)(2,1)S(1)}, bf16[80]{0:T(256)(128)(2,1)S(1)}, u32[]{:S(2)}, u32[]{:S(2)}) collective-permute-start(bf16[80]{0:T(256)(128)(2,1)S(1)} %fusion.70), channel_id=1, source_target_pairs={{0,1},{1,0},{2,3},{3,2},{4,5},{5,4},{6,7},{7,6},{8,9},{9,8},{10,11... | collective-permute-start | bytes 488 | tf_op jit(solution)/shard_map/ppermute | solution.py:142
  315.9 30.5 %all-to-all-start.1 = ((bf16[16,6,3584]{2,1,0:T(8,128)(2,1)}), bf16[16,6,3584]{2,1,0:T(8,128)(2,1)S(1)}, u32[]{:S(2)}, u32[]{:S(2)}) async-start(bf16[16,6,3584]{2,1,0:T(8,128)(2,1)} %fusion.34), calls=%async_computation.2 | async-start | bytes 1835008 | tf_op jit(solution)/shard_map/all_to_all | solution.py:150
  324.6 4.3 %copy-start.10 = (bf16[3584,128]{1,0:T(8,128)(2,1)S(1)}, bf16[3584,128]{1,0:T(8,128)(2,1)}, u32[]{:S(2)}) copy-start(bf16[3584,128]{1,0:T(8,128)(2,1)} %convolution_convert_fusion.6) | copy-start | bytes 2752516
  324.6 4.3 %copy-start.11 = (bf16[3584,128]{1,0:T(8,128)(2,1)S(1)}, bf16[3584,128]{1,0:T(8,128)(2,1)}, u32[]{:S(2)}) copy-start(bf16[3584,128]{1,0:T(8,128)(2,1)} %convolution_convert_fusion.7) | copy-start | bytes 2752516
  324.6 23.8 %copy-start.1 = (bf16[8,8]{1,0:T(8,128)(2,1)S(1)}, bf16[8,8]{1,0:T(8,128)(2,1)}, u32[]{:S(2)}) copy-start(bf16[8,8]{1,0:T(8,128)(2,1)} %param.22) | copy-start | bytes 388
  328.9 18.7 %copy-start.12 = (s32[8,8]{1,0:T(8,128)S(1)}, s32[8,8]{1,0:T(8,128)}, u32[]{:S(2)}) copy-start(s32[8,8]{1,0:T(8,128)} %param.23) | copy-start | bytes 772
Sparse Core Ops, SparseCore 0:
  71.8 59.0 all-gather.2
  133.3 63.5 all-gather.4
  226.7 80.0 reduce-scatter.1

commit v4 on v3

--- a/solution.py
+++ b/solution.py
@@ -128,12 +128,8 @@
         == lax.broadcasted_iota(jnp.int32, (features, hidden_width), 1)
     ).astype(bf16)
     w_out = jnp.concatenate([wg, wu, jnp.broadcast_to(eye, wg.shape)], axis=2)
-    product = jnp.stack(
-        [
-            jnp.einsum("sk,fk->sf", lhs, w_out[t], preferred_element_type=f32).astype(bf16)
-            for t in range(tensor_size)
-        ]
-    ).reshape(tensor_size * all_rows, features)
+    product = jnp.einsum("sk,tfk->tsf", lhs, w_out, preferred_element_type=f32).astype(bf16)
+    product = product.reshape(tensor_size * all_rows, features)
     own_rows = lax.psum_scatter(product, ("tensor", "dp"), scatter_dimension=0, tiled=True)
 
     own_route = (

time: 358 us -> 348 us (0.972)
  other arithmetic: 24.1 us -> 12.4 us
  waiting for transfers between devices: 184 us -> 188 us
    another operation x1 -> x0, other arithmetic: 8.7 us -> none  [shards(): jnp.stack([jnp.einsum('sk,fk->sf', lhs, w_out[t], preferred_element_type=...]
    all_gather x1, waiting for transfers between devices: 49.8 us -> 54.4 us  [shards(): g_tok = lax.all_gather(tok_rows, ('tensor', 'dp'), axis=0, tiled=True)]
    dot_general x2 -> x1, matrix products: 11.6 us -> 9.51 us  [shards(): jnp.einsum('sk,tfk->tsf', lhs, w_out, preferred_element_type=f32)]
where the time goes in v4:
time: 348 us; the launch traced here: 343 us
  waiting for transfers between devices  188 us (54%)
  matrix products  53 us (15%)
  blocking collectives  46.3 us (13%)
  local copies, waits for them, and re-layouts  19.1 us (5%)
  between operations  14.1 us (4%)
  other arithmetic  12.4 us (4%)
  starting transfers between devices  10.5 us (3%)
    reduce_scatter x1, waiting for transfers between devices, shards(): lax.psum_scatter(product, ('tensor', 'dp'), scatter_dimension=0, tiled=True)  64.5 us
    all_gather x1, waiting for transfers between devices, shards(): g_tok = lax.all_gather(tok_rows, ('tensor', 'dp'), axis=0, tiled=True)  54.4 us
    all_gather x1, waiting for transfers between devices, shards(): g_cot = lax.all_gather(cot_rows, ('tensor', 'dp'), axis=0, tiled=True)  54.3 us
    all_to_all x1, blocking collectives, shards(): lax.all_to_all(packed, 'expert', split_axis=1, concat_axis=1, tiled=True)  46.3 us
    all_to_all x1, waiting for transfers between devices, shards(): lax.all_to_all(back_pack, 'expert', split_axis=0, concat_axis=0, tiled=True)  14.2 us
    dot_general x1, matrix products, shards(): jnp.einsum('sk,tfk->tsf', lhs, w_out, preferred_element_type=f32)  9.51 us
    dot_general x2, matrix products, shards(): jnp.dot(g_tok[t].T, grad_g, preferred_element_type=f32).astype(bf16)  9.32 us
    all_to_all x1, starting transfers between devices, shards(): lax.all_to_all(back_pack, 'expert', split_axis=0, concat_axis=0, tiled=True)  8.58 us
  transfers between devices with their start and end apart: 5, of which 4 were waited for; matrix products, arithmetic and copies ran while one was open for 11% of the time, Pallas kernels for 0%

profile of v4, /device:TPU:32, one launch (start us, length us, event | category | flops | bytes accessed | tf_op | source)
XLA Modules:
  0.0 342.9 jit_solution(5663617773083369168)
XLA Ops:
  7.2 0.0 all-gather.3.cloned.1.call-start
  7.2 0.8 convert_reduce_fusion
  8.0 0.7 convert_element_type.137
  8.7 0.9 fusion.49
  9.7 1.0 fusion.47
  10.7 1.0 fusion.58
  11.6 0.1 copy.46
  11.7 0.7 divide_subtract_fusion
  12.4 0.8 convolution_bitcast_fusion.1
  13.3 0.9 fusion.56
  14.2 1.3 fusion.5
  15.5 0.1 fusion.27
  15.6 1.4 copy.47
  17.0 46.3 %all_to_all.10 = bf16[2,16,6,3584]{3,0,2,1:T(2,128)(2,1)S(1)} all-to-all(bf16[2,16,6,3584]{3,0,2,1:T(2,128)(2,1)S(1)} %copy.47), channel_id=1, replica_groups=mesh['dp'=8,'expert'=16,'tensor'=2] {'expert'}, dimensions={1} | all-to-all | bytes 2752512 | tf_op jit(solution)/shard_map/all_to_all | solution.py:57
  63.4 5.2 %slice_reduce_fusion.1 = (bf16[16,5,3584]{2,1,0:T(8,128)(2,1)S(1)}, bf16[16,5,3584]{2,1,0:T(8,128)(2,1)S(1)}) fusion(bf16[2,16,6,3584]{3,0,2,1:T(2,128)(2,1)S(1)} %all_to_all.10), kind=kLoop, calls=%fused_computation.49 | loop fusion | bytes 2293760 | tf_op jit(solution)/shard_map/slice | solution.py:62
  68.5 1.0 reshape_squeeze.22
  69.6 0.1 reshape.250
  69.7 1.9 fusion.38
  71.7 0.0 all-gather.5.cloned.1.call-start
  71.7 0.2 reshape_squeeze.24
  72.0 0.9 concatenate.45
  72.9 0.2 reduce-scatter.2.cloned.1.call-start
  73.1 3.3 copy.48
  76.4 0.1 fusion.25
  76.5 54.4 %all-gather.3.cloned.1.call-done = bf16[1408,3584]{1,0:T(8,128)(2,1)} async-done(((bf16[88,3584]{1,0:T(8,128)(2,1)}), bf16[1408,3584]{1,0:T(8,128)(2,1)}) %all-gather.3.cloned.1.call-update) | async-done | bytes 10092560 | tf_op jit(solution)/shard_map/all_gather | solution.py:65
  130.9 2.4 slice-done.3
  133.4 0.1 reshape.255
  133.5 4.5 %fusion.20 = f32[704,256]{1,0:T(8,128)S(1)} fusion(bf16[2,3584,128]{2,1,0:T(8,128)(2,1)} %bitcast.119, bf16[2,3584,128]{2,1,0:T(8,128)(2,1)} %bitcast.116, bf16[1408,3584]{1,0:T(8,128)(2,1)} %all-gather.3.cloned.1.call-done), kind=kOutput, calls=%fused_computation.32 | convolution fusion | flops 1295515648 | bytes 9437184 | tf_op jit(solution)/shard_map/dot_general | solution.py:79
  138.0 1.3 copy-done.2
  139.3 0.5 copy-done.7
  139.8 0.5 copy-done.8
  140.4 2.3 fusion.28
  142.7 54.3 %all-gather.5.cloned.1.call-done = bf16[1408,3584]{1,0:T(8,128)(2,1)} async-done(((bf16[88,3584]{1,0:T(8,128)(2,1)}), bf16[1408,3584]{1,0:T(8,128)(2,1)}) %all-gather.5.cloned.1.call-update) | async-done | bytes 10092560 | tf_op jit(solution)/shard_map/all_gather | solution.py:67
  196.9 4.0 %fusion.7 = f32[704,128]{1,0:T(8,128)S(1)} fusion(bf16[1408,3584]{1,0:T(8,128)(2,1)} %all-gather.5.cloned.1.call-done, bf16[128,2,3584]{0,2,1:T(8,128)(2,1)S(1)} %bitcast.100), kind=kOutput, calls=%fused_computation.16 | convolution fusion | flops 645922816 | bytes 6324224 | tf_op jit(solution)/shard_map/sf,hf->sh/dot_general | solution.py:84
  200.9 4.0 %multiply_convert_fusion.2 = (bf16[704,128]{1,0:T(8,128)(2,1)S(1)}, bf16[704,128]{1,0:T(8,128)(2,1)S(1)}, bf16[704,128]{1,0:T(8,128)(2,1)S(1)}, f32[704,128]{1,0:T(8,128)S(1)}) fusion(f32[704,256]{1,0:T(8,128)S(1)} %copy-done.9, f32[704]{0:T(1024)S(1)} %reshape.255, f32[704,128]{1,0:T(8,128)S(1)} %fusion.7, bf16[128,2,3584]{0,2,1:T(8,128)(2,1)S(1)} %bitcast.101, ...), kind=kOutput, calls=%fused_computation.67 | convolution fusion | flops 647454720 | bytes 7950336 | tf_op jit(solution)/shard_map/sf,hf->sh/dot_general | solution.py:84
  204.9 0.2 fusion.44
  205.1 0.1 reduce_sum.35
  205.2 0.2 scatter.21
  205.5 0.1 broadcast_in_dim.8
  205.6 9.5 %convolution_convert_fusion = bf16[2,3584,704]{1,2,0:T(8,128)(2,1)} fusion(bf16[2,3584,128]{2,1,0:T(8,128)(2,1)S(1)} %broadcast_in_dim.8, bf16[2,3584,128]{2,1,0:T(8,128)(2,1)} %bitcast.117, bf16[2,3584,128]{2,1,0:T(8,128)(2,1)} %bitcast.120, bf16[704,128]{1,0:T(8,128)(2,1)S(1)} %bitcast.103, bf16[704,128]{1,0:T(8,128)(2,1)S(1)} %get-tuple-element.68, ...), kind=kOutput, calls=%fused_computation | convolution fusion | flops 3898720256 | bytes 16138240 | tf_op jit(solution)/shard_map/sk,tfk->tsf/dot_general | solution.py:131
  215.1 0.0 reduce-scatter.2.cloned.1.call-update
  215.2 3.5 %convolution_convert_fusion.3 = bf16[128,3584]{1,0:T(8,128)(2,1)S(1)} fusion(bf16[1408,3584]{1,0:T(8,128)(2,1)} %all-gather.5.cloned.1.call-done, bf16[704,128]{1,0:T(8,128)(2,1)S(1)} %get-tuple-element.69, f32[704]{0:T(1024)S(1)} %reshape.255), kind=kOutput, calls=%fused_computation.8 | convolution fusion | flops 646651904 | bytes 6146816 | tf_op jit(solution)/shard_map/dot_general | solution.py:101
  218.7 3.6 %convolution_convert_fusion.2 = bf16[128,3584]{1,0:T(8,128)(2,1)S(1)} fusion(bf16[1408,3584]{1,0:T(8,128)(2,1)} %all-gather.5.cloned.1.call-done, bf16[704,128]{1,0:T(8,128)(2,1)S(1)} %get-tuple-element.69, f32[704]{0:T(1024)S(1)} %reshape.255), kind=kOutput, calls=%fused_computation.7 | convolution fusion | flops 646651904 | bytes 6146816 | tf_op jit(solution)/shard_map/dot_general | solution.py:101
  222.3 4.5 %convolution_convert_fusion.4 = bf16[3584,128]{1,0:T(8,128)(2,1)S(1)} fusion(bf16[704,128]{1,0:T(8,128)(2,1)S(1)} %copy-done.11, bf16[1408,3584]{1,0:T(8,128)(2,1)} %all-gather.3.cloned.1.call-done), kind=kOutput, calls=%fused_computation.9 | convolution fusion | flops 646381568 | bytes 6144000 | tf_op jit(solution)/shard_map/dot_general | solution.py:115
  226.8 2.6 convolution_convert_fusion.5
  229.4 1.4 maximum_bitcast_fusion.2
  230.8 64.5 %reduce-scatter.2.cloned.1.call-done = bf16[88,3584]{1,0:T(8,128)(2,1)} async-done(((bf16[1408,3584]{1,0:T(8,128)(2,1)}), bf16[88,3584]{1,0:T(8,128)(2,1)}) %reduce-scatter.2.cloned.1.call-update) | async-done | bytes 630800 | tf_op jit(solution)/shard_map/reduce_scatter | solution.py:133
  295.4 0.8 fusion.77
  296.1 1.6 collective-permute-start
  297.7 5.1 %convolution_convert_fusion.6 = bf16[3584,128]{1,0:T(8,128)(2,1)} fusion(bf16[704,128]{1,0:T(8,128)(2,1)S(1)} %get-tuple-element.67, bf16[1408,3584]{1,0:T(8,128)(2,1)} %all-gather.3.cloned.1.call-done), kind=kOutput, calls=%fused_computation.11 | convolution fusion | flops 646381568 | bytes 6144000 | tf_op jit(solution)/shard_map/dot_general | solution.py:108
  302.8 0.2 reshape.253
  303.0 0.8 copy-done.3
  303.9 0.1 reshape.272
  304.0 1.2 fusion.37
  305.1 8.6 %all-to-all-start.1 = ((bf16[16,6,3584]{2,1,0:T(8,128)(2,1)}), bf16[16,6,3584]{2,1,0:T(8,128)(2,1)S(1)}, u32[]{:S(2)}, u32[]{:S(2)}) async-start(bf16[16,6,3584]{2,1,0:T(8,128)(2,1)} %fusion.37), calls=%async_computation.2 | async-start | bytes 1835008 | tf_op jit(solution)/shard_map/all_to_all | solution.py:146
  313.8 4.3 %convolution_convert_fusion.7 = bf16[3584,128]{1,0:T(8,128)(2,1)S(1)} fusion(bf16[704,128]{1,0:T(8,128)(2,1)S(1)} %get-tuple-element.67, bf16[1408,3584]{1,0:T(8,128)(2,1)} %all-gather.3.cloned.1.call-done), kind=kOutput, calls=%fused_computation.12 | convolution fusion | flops 646381568 | bytes 6144000 | tf_op jit(solution)/shard_map/dot_general | solution.py:108
  318.1 2.1 maximum_bitcast_fusion
  320.1 14.2 %all-to-all-done.1 = bf16[16,6,3584]{2,1,0:T(8,128)(2,1)S(1)} async-done(((bf16[16,6,3584]{2,1,0:T(8,128)(2,1)}), bf16[16,6,3584]{2,1,0:T(8,128)(2,1)S(1)}, u32[]{:S(2)}, u32[]{:S(2)}) %all-to-all-start.1) | async-done | bytes 688160 | tf_op jit(solution)/shard_map/all_to_all | solution.py:146
  334.4 0.9 fusion.12
  335.3 0.1 copy.77
  335.5 0.1 copy.67
  335.5 0.1 copy.68
  335.6 0.2 fusion.57
  335.8 0.6 convert_element_type.160
  (44 shorter events, 0.3 us)
Async XLA Ops:
  7.2 3.5 %copy-start = (bf16[8,8]{1,0:T(8,128)(2,1)S(1)}, bf16[8,8]{1,0:T(8,128)(2,1)}, u32[]{:S(2)}) copy-start(bf16[8,8]{1,0:T(8,128)(2,1)} %param.22) | copy-start | bytes 388
  7.2 123.7 %all-gather.3.cloned.1.call-start = ((), (), s32[]{:S(2)}) async-start(), calls=%async_computation.3 | async-start | bytes 10723328 | tf_op jit(solution)/shard_map/all_gather | solution.py:65
  71.7 125.3 %all-gather.5.cloned.1.call-start = ((), (), s32[]{:S(2)}) async-start(), calls=%async_computation.4 | async-start | bytes 10723328 | tf_op jit(solution)/shard_map/all_gather | solution.py:67
  72.9 222.5 %reduce-scatter.2.cloned.1.call-start = ((), (), s32[]{:S(2)}) async-start(), calls=%async_computation.5 | async-start | bytes 10723328 | tf_op jit(solution)/shard_map/reduce_scatter | solution.py:133
  130.9 2.4 slice-start.3
  133.4 5.9 %copy-start.2 = (bf16[1408,3584]{1,0:T(8,128)(2,1)S(1)}, bf16[1408,3584]{1,0:T(8,128)(2,1)}, u32[]{:S(2)}) copy-start(bf16[1408,3584]{1,0:T(8,128)(2,1)} %all-gather.3.cloned.1.call-done) | copy-start | bytes 30277636
  133.5 6.4 %copy-start.7 = (bf16[1,7168,128]{2,1,0:T(8,128)(2,1)S(1)}, bf16[1,7168,128]{2,1,0:T(8,128)(2,1)}, u32[]{:S(2)}) copy-start(bf16[1,7168,128]{2,1,0:T(8,128)(2,1)} %param.28) | copy-start | bytes 5505028
  133.5 6.9 %copy-start.8 = (bf16[1,7168,128]{2,1,0:T(8,128)(2,1)S(1)}, bf16[1,7168,128]{2,1,0:T(8,128)(2,1)}, u32[]{:S(2)}) copy-start(bf16[1,7168,128]{2,1,0:T(8,128)(2,1)} %param.27) | copy-start | bytes 5505028
  196.9 4.0 %copy-start.9 = (f32[704,256]{1,0:T(8,128)S(1)}, f32[704,256]{1,0:T(8,128)}, u32[]{:S(2)}) copy-start(f32[704,256]{1,0:T(8,128)} %fusion.28) | copy-start | bytes 2162692
  204.9 10.2 %copy-start.10 = (bf16[704,128]{1,0:T(8,128)(2,1)}, bf16[704,128]{1,0:T(8,128)(2,1)S(1)}, u32[]{:S(2)}) copy-start(bf16[704,128]{1,0:T(8,128)(2,1)S(1)} %get-tuple-element.68) | copy-start | bytes 540676
  215.2 7.1 %copy-start.11 = (bf16[704,128]{1,0:T(8,128)(2,1)S(1)}, bf16[704,128]{1,0:T(8,128)(2,1)}, u32[]{:S(2)}) copy-start(bf16[704,128]{1,0:T(8,128)(2,1)} %copy-done.10) | copy-start | bytes 540676
  218.6 8.1 %slice-start = ((s8[10092544]{0:T(1024)(128)(4,1)}), s8[4194304]{0:T(1024)(128)(4,1)S(1)}, s32[]{:S(2)}) async-start(s8[10092544]{0:T(1024)(128)(4,1)} %bitcast.97), calls=%async_computation.6 | async-start | bytes 8388608
  218.6 8.1 %slice-start.1 = ((s8[10092544]{0:T(1024)(128)(4,1)}), s8[4194304]{0:T(1024)(128)(4,1)S(1)}, s32[]{:S(2)}) async-start(s8[10092544]{0:T(1024)(128)(4,1)} %bitcast.97), calls=%async_computation.7 | async-start | bytes 8388608
  222.2 4.5 %slice-start.2 = ((s8[10092544]{0:T(1024)(128)(4,1)}), s8[1703936]{0:T(1024)(128)(4,1)S(1)}, s32[]{:S(2)}) async-start(s8[10092544]{0:T(1024)(128)(4,1)} %bitcast.97), calls=%async_computation.8 | async-start | bytes 3407872
  296.1 6.7 %slice-start.4 = ((bf16[88,3584]{1,0:T(8,128)(2,1)}), bf16[80,3584]{1,0:T(8,128)(2,1)S(1)}, s32[]{:S(2)}) async-start(bf16[88,3584]{1,0:T(8,128)(2,1)} %reduce-scatter.2.cloned.1.call-done), calls=%async_computation.10 | async-start | bytes 1146880 | tf_op jit(solution)/shard_map/slice | solution.py:144
  296.1 6.9 %collective-permute-start = (bf16[80]{0:T(256)(128)(2,1)S(1)}, bf16[80]{0:T(256)(128)(2,1)S(1)}, u32[]{:S(2)}, u32[]{:S(2)}) collective-permute-start(bf16[80]{0:T(256)(128)(2,1)S(1)} %fusion.77), channel_id=1, source_target_pairs={{0,1},{1,0},{2,3},{3,2},{4,5},{5,4},{6,7},{7,6},{8,9},{9,8},{10,11... | collective-permute-start | bytes 488 | tf_op jit(solution)/shard_map/ppermute | solution.py:138
  302.8 1.1 copy-start.3
  305.1 29.2 %all-to-all-start.1 = ((bf16[16,6,3584]{2,1,0:T(8,128)(2,1)}), bf16[16,6,3584]{2,1,0:T(8,128)(2,1)S(1)}, u32[]{:S(2)}, u32[]{:S(2)}) async-start(bf16[16,6,3584]{2,1,0:T(8,128)(2,1)} %fusion.37), calls=%async_computation.2 | async-start | bytes 1835008 | tf_op jit(solution)/shard_map/all_to_all | solution.py:146
  313.7 4.3 %copy-start.4 = (bf16[3584,128]{1,0:T(8,128)(2,1)S(1)}, bf16[3584,128]{1,0:T(8,128)(2,1)}, u32[]{:S(2)}) copy-start(bf16[3584,128]{1,0:T(8,128)(2,1)} %convolution_convert_fusion.5) | copy-start | bytes 2752516
  313.7 4.3 %copy-start.5 = (bf16[3584,128]{1,0:T(8,128)(2,1)S(1)}, bf16[3584,128]{1,0:T(8,128)(2,1)}, u32[]{:S(2)}) copy-start(bf16[3584,128]{1,0:T(8,128)(2,1)} %convolution_convert_fusion.6) | copy-start | bytes 2752516
  318.0 17.6 %copy-start.6 = (s32[8,8]{1,0:T(8,128)S(1)}, s32[8,8]{1,0:T(8,128)}, u32[]{:S(2)}) copy-start(s32[8,8]{1,0:T(8,128)} %param.23) | copy-start | bytes 772
  318.1 18.4 %copy-start.1 = (bf16[8,8]{1,0:T(8,128)(2,1)S(1)}, bf16[8,8]{1,0:T(8,128)(2,1)}, u32[]{:S(2)}) copy-start(bf16[8,8]{1,0:T(8,128)(2,1)} %param.22) | copy-start | bytes 388
Sparse Core Ops, SparseCore 0:
  71.8 59.0 all-gather.2
  133.3 63.5 all-gather.4
  215.3 80.0 reduce-scatter.1

commit v5 on v4

--- a/solution.py
+++ b/solution.py
@@ -131,6 +131,9 @@
     product = jnp.einsum("sk,tfk->tsf", lhs, w_out, preferred_element_type=f32).astype(bf16)
     product = product.reshape(tensor_size * all_rows, features)
     own_rows = lax.psum_scatter(product, ("tensor", "dp"), scatter_dimension=0, tiled=True)
+    own_rows, grad_gate, grad_up, grad_down = lax.optimization_barrier(
+        (own_rows, grad_gate, grad_up, grad_down)
+    )
 
     own_route = (
         own_rows[slots, :slots].astype(f32) + own_rows[slots + 1, :slots].astype(f32)

time: 348 us -> 345 us (level)
  blocking collectives: 46.3 us -> 78.2 us
  waiting for transfers between devices: 188 us -> 170 us
  starting transfers between devices: 10.5 us -> 1.95 us
  matrix products: 53 us -> 46.1 us
    all_to_all x0 -> x1, blocking collectives: none -> 32.1 us  [shards(): lax.all_to_all(back_pack, 'expert', split_axis=0, concat_axis=0, tiled=True)]
    all_to_all x1 -> x0, waiting for transfers between devices: 14.2 us -> none  [shards(): lax.all_to_all(back_pack, 'expert', split_axis=0, concat_axis=0, tiled=True)]
    all_to_all x1 -> x0, starting transfers between devices: 8.58 us -> none  [shards(): lax.all_to_all(back_pack, 'expert', split_axis=0, concat_axis=0, tiled=True)]
    dot_general x2, matrix products: 9.32 us -> 3.39 us  [shards(): jnp.dot(g_tok[t].T, grad_g, preferred_element_type=f32).astype(bf16)]
    reduce_scatter x1, waiting for transfers between devices: 64.5 us -> 60.1 us  [shards(): lax.psum_scatter(product, ('tensor', 'dp'), scatter_dimension=0, tiled=True)]
    broadcast_in_dim x2 -> x0, other arithmetic: 3.48 us -> none  [the longest x1 2.07 us: shards(): grad_gate[None]]
    concatenate x0 -> x2, other arithmetic: none -> 3.48 us  [the longest x1 2.07 us: shards(): jnp.concatenate([jnp.dot(g_tok[t].T, grad_g, preferred_element_type=f32)....]
  transfers between devices with their start and end apart: 5 -> 4, of which waited for: 4 -> 4; matrix products, arithmetic and copies ran while one was open for 11% -> 10% of each run, Pallas kernels for 0% -> 0%
where the time goes in v5:
time: 345 us; the launch traced here: 341 us
  waiting for transfers between devices  170 us (49%)
  blocking collectives  78.2 us (23%)
  matrix products  46.1 us (13%)
  local copies, waits for them, and re-layouts  19.3 us (6%)
  between operations  14 us (4%)
  other arithmetic  12.1 us (4%)
    reduce_scatter x1, waiting for transfers between devices, shards(): lax.psum_scatter(product, ('tensor', 'dp'), scatter_dimension=0, tiled=True)  60.1 us
    all_gather x1, waiting for transfers between devices, shards(): g_tok = lax.all_gather(tok_rows, ('tensor', 'dp'), axis=0, tiled=True)  54.7 us
    all_gather x1, waiting for transfers between devices, shards(): g_cot = lax.all_gather(cot_rows, ('tensor', 'dp'), axis=0, tiled=True)  54.3 us
    all_to_all x1, blocking collectives, shards(): lax.all_to_all(packed, 'expert', split_axis=1, concat_axis=1, tiled=True)  46 us
    all_to_all x1, blocking collectives, shards(): lax.all_to_all(back_pack, 'expert', split_axis=0, concat_axis=0, tiled=True)  32.1 us
    dot_general x1, matrix products, shards(): jnp.einsum('sk,tfk->tsf', lhs, w_out, preferred_element_type=f32)  9.43 us
    dot_general x2, matrix products, shards(): jnp.einsum('sf,hf->sh', g_cot[t], wd[:, t], preferred_element_type=f32)  7.93 us
    dot_general x2, matrix products, shards(): jnp.dot(weighted.T, g_cot[t], preferred_element_type=f32).astype(bf16)  6.99 us
  transfers between devices with their start and end apart: 4, of which 4 were waited for; matrix products, arithmetic and copies ran while one was open for 10% of the time, Pallas kernels for 0%

profile of v5, /device:TPU:32, one launch (start us, length us, event | category | flops | bytes accessed | tf_op | source)
XLA Modules:
  0.0 341.3 jit_solution(1267415590380000024)
XLA Ops:
  7.2 0.0 all-gather.3.cloned.1.call-start
  7.2 0.8 convert_reduce_fusion
  8.0 0.7 convert_element_type.137
  8.7 0.9 fusion.49
  9.7 1.0 fusion.47
  10.7 1.0 fusion.58
  11.6 0.1 copy.46
  11.7 0.7 divide_subtract_fusion
  12.4 0.8 convolution_bitcast_fusion.1
  13.3 0.9 fusion.56
  14.2 1.3 fusion.5
  15.5 0.1 fusion.27
  15.6 1.4 copy.47
  17.0 46.0 %all_to_all.10 = bf16[2,16,6,3584]{3,0,2,1:T(2,128)(2,1)S(1)} all-to-all(bf16[2,16,6,3584]{3,0,2,1:T(2,128)(2,1)S(1)} %copy.47), channel_id=1, replica_groups=mesh['dp'=8,'expert'=16,'tensor'=2] {'expert'}, dimensions={1} | all-to-all | bytes 2752512 | tf_op jit(solution)/shard_map/all_to_all | solution.py:57
  63.1 5.2 %slice_reduce_fusion.1 = (bf16[16,5,3584]{2,1,0:T(8,128)(2,1)S(1)}, bf16[16,5,3584]{2,1,0:T(8,128)(2,1)S(1)}) fusion(bf16[2,16,6,3584]{3,0,2,1:T(2,128)(2,1)S(1)} %all_to_all.10), kind=kLoop, calls=%fused_computation.49 | loop fusion | bytes 2293760 | tf_op jit(solution)/shard_map/slice | solution.py:62
  68.2 1.0 reshape_squeeze.22
  69.3 0.1 reshape.250
  69.4 1.9 fusion.38
  71.4 0.0 all-gather.5.cloned.1.call-start
  71.4 0.2 reshape_squeeze.24
  71.7 0.9 concatenate.45
  72.6 0.2 reduce-scatter.2.cloned.1.call-start
  72.8 3.3 copy.48
  76.1 0.1 fusion.25
  76.2 54.7 %all-gather.3.cloned.1.call-done = bf16[1408,3584]{1,0:T(8,128)(2,1)} async-done(((bf16[88,3584]{1,0:T(8,128)(2,1)}), bf16[1408,3584]{1,0:T(8,128)(2,1)}) %all-gather.3.cloned.1.call-update) | async-done | bytes 10092560 | tf_op jit(solution)/shard_map/all_gather | solution.py:65
  130.9 2.4 slice-done.3
  133.4 0.1 reshape.255
  133.5 4.5 %fusion.20 = f32[704,256]{1,0:T(8,128)S(1)} fusion(bf16[2,3584,128]{2,1,0:T(8,128)(2,1)} %bitcast.119, bf16[2,3584,128]{2,1,0:T(8,128)(2,1)} %bitcast.116, bf16[1408,3584]{1,0:T(8,128)(2,1)} %all-gather.3.cloned.1.call-done), kind=kOutput, calls=%fused_computation.32 | convolution fusion | flops 1295515648 | bytes 9437184 | tf_op jit(solution)/shard_map/dot_general | solution.py:79
  138.0 1.3 copy-done.2
  139.3 0.5 copy-done.4
  139.8 0.5 copy-done.5
  140.3 2.3 fusion.28
  142.7 54.3 %all-gather.5.cloned.1.call-done = bf16[1408,3584]{1,0:T(8,128)(2,1)} async-done(((bf16[88,3584]{1,0:T(8,128)(2,1)}), bf16[1408,3584]{1,0:T(8,128)(2,1)}) %all-gather.5.cloned.1.call-update) | async-done | bytes 10092560 | tf_op jit(solution)/shard_map/all_gather | solution.py:67
  196.9 4.0 %fusion.7 = f32[704,128]{1,0:T(8,128)S(1)} fusion(bf16[1408,3584]{1,0:T(8,128)(2,1)} %all-gather.5.cloned.1.call-done, bf16[128,2,3584]{0,2,1:T(8,128)(2,1)S(1)} %bitcast.100), kind=kOutput, calls=%fused_computation.16 | convolution fusion | flops 645922816 | bytes 6324224 | tf_op jit(solution)/shard_map/sf,hf->sh/dot_general | solution.py:84
  200.9 4.0 %multiply_convert_fusion.2 = (bf16[704,128]{1,0:T(8,128)(2,1)S(1)}, bf16[704,128]{1,0:T(8,128)(2,1)S(1)}, bf16[704,128]{1,0:T(8,128)(2,1)S(1)}, f32[704,128]{1,0:T(8,128)S(1)}) fusion(f32[704,256]{1,0:T(8,128)S(1)} %copy-done.6, f32[704]{0:T(1024)S(1)} %reshape.255, f32[704,128]{1,0:T(8,128)S(1)} %fusion.7, bf16[128,2,3584]{0,2,1:T(8,128)(2,1)S(1)} %bitcast.101, ...), kind=kOutput, calls=%fused_computation.67 | convolution fusion | flops 647454720 | bytes 7950336 | tf_op jit(solution)/shard_map/sf,hf->sh/dot_general | solution.py:84
  204.9 0.2 fusion.44
  205.1 0.1 reduce_sum.35
  205.2 0.2 scatter.21
  205.5 0.1 broadcast_in_dim.8
  205.6 9.4 %convolution_convert_fusion = bf16[2,3584,704]{1,2,0:T(8,128)(2,1)} fusion(bf16[2,3584,128]{2,1,0:T(8,128)(2,1)S(1)} %broadcast_in_dim.8, bf16[2,3584,128]{2,1,0:T(8,128)(2,1)} %bitcast.117, bf16[2,3584,128]{2,1,0:T(8,128)(2,1)} %bitcast.120, bf16[704,128]{1,0:T(8,128)(2,1)S(1)} %bitcast.103, bf16[704,128]{1,0:T(8,128)(2,1)S(1)} %get-tuple-element.76, ...), kind=kOutput, calls=%fused_computation | convolution fusion | flops 3898720256 | bytes 16138240 | tf_op jit(solution)/shard_map/sk,tfk->tsf/dot_general | solution.py:131
  215.1 3.4 %convolution_convert_fusion.3 = bf16[128,3584]{1,0:T(8,128)(2,1)S(1)} fusion(bf16[1408,3584]{1,0:T(8,128)(2,1)} %all-gather.5.cloned.1.call-done, bf16[704,128]{1,0:T(8,128)(2,1)S(1)} %get-tuple-element.77, f32[704]{0:T(1024)S(1)} %reshape.255), kind=kOutput, calls=%fused_computation.8 | convolution fusion | flops 646651904 | bytes 6146816 | tf_op jit(solution)/shard_map/dot_general | solution.py:101
  218.5 3.6 %convolution_convert_fusion.2 = bf16[128,3584]{1,0:T(8,128)(2,1)S(1)} fusion(bf16[1408,3584]{1,0:T(8,128)(2,1)} %all-gather.5.cloned.1.call-done, bf16[704,128]{1,0:T(8,128)(2,1)S(1)} %get-tuple-element.77, f32[704]{0:T(1024)S(1)} %reshape.255), kind=kOutput, calls=%fused_computation.7 | convolution fusion | flops 646651904 | bytes 6146816 | tf_op jit(solution)/shard_map/dot_general | solution.py:101
  222.1 4.5 %convolution_convert_fusion.4 = bf16[3584,128]{1,0:T(8,128)(2,1)S(1)} fusion(bf16[704,128]{1,0:T(8,128)(2,1)S(1)} %get-tuple-element.76, bf16[1408,3584]{1,0:T(8,128)(2,1)} %all-gather.3.cloned.1.call-done), kind=kOutput, calls=%fused_computation.9 | convolution fusion | flops 646381568 | bytes 6144000 | tf_op jit(solution)/shard_map/dot_general | solution.py:115
  226.6 1.7 convolution_convert_fusion.5
  228.3 1.7 convolution_convert_fusion.6
  230.0 1.7 convolution_convert_fusion.7
  231.7 1.4 pad_maximum_fusion.3
  233.2 2.1 pad_maximum_fusion.1
  235.2 60.1 %reduce-scatter.2.cloned.1.call-done = bf16[88,3584]{1,0:T(8,128)(2,1)} async-done(((bf16[1408,3584]{1,0:T(8,128)(2,1)}), bf16[88,3584]{1,0:T(8,128)(2,1)}) %reduce-scatter.2.cloned.1.call-update) | async-done | bytes 630800 | tf_op jit(solution)/shard_map/reduce_scatter | solution.py:133
  295.3 0.7 convert_bitcast_fusion.1
  296.0 1.6 collective-permute-start
  297.6 1.1 slice.195
  298.7 0.2 reshape.253
  299.0 0.6 collective-permute-done
  299.5 0.7 broadcast_select_fusion
  300.3 0.1 reshape.272
  300.4 0.2 fusion.37
  300.6 32.1 %all_to_all.11 = bf16[16,6,3584]{2,1,0:T(8,128)(2,1)S(1)} all-to-all(bf16[16,6,3584]{2,1,0:T(8,128)(2,1)S(1)} %fusion.37), channel_id=1, replica_groups=mesh['dp'=8,'expert'=16,'tensor'=2] {'expert'}, dimensions={0} | all-to-all | bytes 1376256 | tf_op jit(solution)/shard_map/all_to_all | solution.py:149
  332.7 0.9 fusion.12
  333.7 0.1 copy.77
  333.8 0.1 copy.67
  333.9 0.1 copy.68
  334.0 0.2 fusion.57
  334.2 0.6 convert_element_type.167
  (32 shorter events, 0.3 us)
Async XLA Ops:
  7.2 3.5 %copy-start = (bf16[8,8]{1,0:T(8,128)(2,1)S(1)}, bf16[8,8]{1,0:T(8,128)(2,1)}, u32[]{:S(2)}) copy-start(bf16[8,8]{1,0:T(8,128)(2,1)} %param.22) | copy-start | bytes 388
  7.2 123.7 %all-gather.3.cloned.1.call-start = ((), (), s32[]{:S(2)}) async-start(), calls=%async_computation.3 | async-start | bytes 10723328 | tf_op jit(solution)/shard_map/all_gather | solution.py:65
  71.4 125.6 %all-gather.5.cloned.1.call-start = ((), (), s32[]{:S(2)}) async-start(), calls=%async_computation.4 | async-start | bytes 10723328 | tf_op jit(solution)/shard_map/all_gather | solution.py:67
  72.6 222.7 %reduce-scatter.2.cloned.1.call-start = ((), (), s32[]{:S(2)}) async-start(), calls=%async_computation.5 | async-start | bytes 10723328 | tf_op jit(solution)/shard_map/reduce_scatter | solution.py:133
  130.9 2.4 slice-start.3
  133.4 5.9 %copy-start.2 = (bf16[1408,3584]{1,0:T(8,128)(2,1)S(1)}, bf16[1408,3584]{1,0:T(8,128)(2,1)}, u32[]{:S(2)}) copy-start(bf16[1408,3584]{1,0:T(8,128)(2,1)} %all-gather.3.cloned.1.call-done) | copy-start | bytes 30277636
  133.4 6.4 %copy-start.4 = (bf16[1,7168,128]{2,1,0:T(8,128)(2,1)S(1)}, bf16[1,7168,128]{2,1,0:T(8,128)(2,1)}, u32[]{:S(2)}) copy-start(bf16[1,7168,128]{2,1,0:T(8,128)(2,1)} %param.28) | copy-start | bytes 5505028
  133.5 6.9 %copy-start.5 = (bf16[1,7168,128]{2,1,0:T(8,128)(2,1)S(1)}, bf16[1,7168,128]{2,1,0:T(8,128)(2,1)}, u32[]{:S(2)}) copy-start(bf16[1,7168,128]{2,1,0:T(8,128)(2,1)} %param.27) | copy-start | bytes 5505028
  196.9 4.0 %copy-start.6 = (f32[704,256]{1,0:T(8,128)S(1)}, f32[704,256]{1,0:T(8,128)}, u32[]{:S(2)}) copy-start(f32[704,256]{1,0:T(8,128)} %fusion.28) | copy-start | bytes 2162692
  218.5 8.1 %slice-start = ((s8[10092544]{0:T(1024)(128)(4,1)}), s8[4194304]{0:T(1024)(128)(4,1)S(1)}, s32[]{:S(2)}) async-start(s8[10092544]{0:T(1024)(128)(4,1)} %bitcast.94), calls=%async_computation.6 | async-start | bytes 8388608
  218.5 8.1 %slice-start.1 = ((s8[10092544]{0:T(1024)(128)(4,1)}), s8[4194304]{0:T(1024)(128)(4,1)S(1)}, s32[]{:S(2)}) async-start(s8[10092544]{0:T(1024)(128)(4,1)} %bitcast.94), calls=%async_computation.7 | async-start | bytes 8388608
  222.1 4.5 %slice-start.2 = ((s8[10092544]{0:T(1024)(128)(4,1)}), s8[1703936]{0:T(1024)(128)(4,1)S(1)}, s32[]{:S(2)}) async-start(s8[10092544]{0:T(1024)(128)(4,1)} %bitcast.94), calls=%async_computation.8 | async-start | bytes 3407872
  296.0 3.5 %collective-permute-start = (bf16[80]{0:T(256)(128)(2,1)S(1)}, bf16[80]{0:T(256)(128)(2,1)S(1)}, u32[]{:S(2)}, u32[]{:S(2)}) collective-permute-start(bf16[80]{0:T(256)(128)(2,1)S(1)} %convert_bitcast_fusion.1), channel_id=1, source_target_pairs={{0,1},{1,0},{2,3},{3,2},{4,5},{5,4},{6,7},{7,6},{8,9},{9,8},{10,11... | collective-permute-start | bytes 488 | tf_op jit(solution)/shard_map/ppermute | solution.py:141
  300.3 34.5 %copy-start.1 = (bf16[8,8]{1,0:T(8,128)(2,1)S(1)}, bf16[8,8]{1,0:T(8,128)(2,1)}, u32[]{:S(2)}) copy-start(bf16[8,8]{1,0:T(8,128)(2,1)} %param.22) | copy-start | bytes 388
  300.3 33.6 %copy-start.3 = (s32[8,8]{1,0:T(8,128)S(1)}, s32[8,8]{1,0:T(8,128)}, u32[]{:S(2)}) copy-start(s32[8,8]{1,0:T(8,128)} %param.23) | copy-start | bytes 772
Sparse Core Ops, SparseCore 0:
  71.5 59.3 all-gather.2
  133.3 63.5 all-gather.4
  215.2 80.0 reduce-scatter.1

commit v6 on v5

--- a/solution.py
+++ b/solution.py
@@ -52,15 +52,16 @@
     ).astype(bf16)
     packed_prob = jnp.einsum("ecr,re->ec", chosen, weight).astype(bf16)
     prob_row = jnp.zeros((experts, 1, features), bf16).at[:, 0, :capacity].set(packed_prob)
-    prob_rows = jnp.stack([jnp.zeros_like(prob_row), prob_row])
-    packed = jnp.concatenate([packed, prob_rows], axis=2)
-    arrived = lax.all_to_all(packed, "expert", split_axis=1, concat_axis=1, tiled=True)
     chunk = slots + 8
     all_rows = dp_size * chunk
     extra = jnp.zeros((chunk - slots, features), bf16)
-    extra_prob = extra.at[0, :slots].set(arrived[1, :, capacity, :capacity].reshape(slots))
-    tok_rows = jnp.concatenate([arrived[0, :, :capacity].reshape(slots, features), extra_prob])
-    cot_rows = jnp.concatenate([arrived[1, :, :capacity].reshape(slots, features), extra])
+    tok_pack = jnp.concatenate([packed[0], prob_row], axis=1)
+    arrived_tok = lax.all_to_all(tok_pack, "expert", split_axis=0, concat_axis=0, tiled=True)
+    extra_prob = extra.at[0, :slots].set(arrived_tok[:, capacity, :capacity].reshape(slots))
+    tok_rows = jnp.concatenate([arrived_tok[:, :capacity].reshape(slots, features), extra_prob])
+    tok_rows, cot_pack = lax.optimization_barrier((tok_rows, packed[1]))
+    arrived_cot = lax.all_to_all(cot_pack, "expert", split_axis=0, concat_axis=0, tiled=True)
+    cot_rows = jnp.concatenate([arrived_cot.reshape(slots, features), extra])
 
     g_tok = lax.all_gather(tok_rows, ("tensor", "dp"), axis=0, tiled=True)
     g_tok = g_tok.reshape(tensor_size, all_rows, features)

time: 345 us -> 342 us (level)
  blocking collectives: 78.2 us -> 109 us
  waiting for transfers between devices: 170 us -> 145 us
  local copies, waits for them, and re-layouts: 19.3 us -> 11.9 us
    all_to_all x1 -> x2, blocking collectives: 46 us -> 77 us  [the longest x1 40.3 us: shards(): lax.all_to_all(cot_pack, 'expert', split_axis=0, concat_axis=0, tiled=True)]
    all_gather x1, waiting for transfers between devices: 54.7 us -> 29.5 us  [shards(): g_tok = lax.all_gather(tok_rows, ('tensor', 'dp'), axis=0, tiled=True)]
    slice x2 -> x1, local copies, waits for them, and re-layouts: 5.22 us -> 0.04 us  [shards(): arrived_tok[:, capacity, :capacity].reshape(slots)]
  transfers between devices with their start and end apart: 4 -> 4, of which waited for: 4 -> 4; matrix products, arithmetic and copies ran while one was open for 10% -> 9% of each run, Pallas kernels for 0% -> 0%
where the time goes in v6:
time: 342 us; the launch traced here: 338 us
  waiting for transfers between devices  145 us (42%)
  blocking collectives  109 us (32%)
  matrix products  45.7 us (13%)
  between operations  14.1 us (4%)
  local copies, waits for them, and re-layouts  11.9 us (3%)
  other arithmetic  11.1 us (3%)
    reduce_scatter x1, waiting for transfers between devices, shards(): lax.psum_scatter(product, ('tensor', 'dp'), scatter_dimension=0, tiled=True)  60 us
    all_gather x1, waiting for transfers between devices, shards(): g_cot = lax.all_gather(cot_rows, ('tensor', 'dp'), axis=0, tiled=True)  54.6 us
    all_to_all x1, blocking collectives, shards(): lax.all_to_all(cot_pack, 'expert', split_axis=0, concat_axis=0, tiled=True)  40.3 us
    all_to_all x1, blocking collectives, shards(): lax.all_to_all(tok_pack, 'expert', split_axis=0, concat_axis=0, tiled=True)  36.7 us
    all_to_all x1, blocking collectives, shards(): lax.all_to_all(back_pack, 'expert', split_axis=0, concat_axis=0, tiled=True)  32.1 us
    all_gather x1, waiting for transfers between devices, shards(): g_tok = lax.all_gather(tok_rows, ('tensor', 'dp'), axis=0, tiled=True)  29.5 us
    dot_general x1, matrix products, shards(): jnp.einsum('sk,tfk->tsf', lhs, w_out, preferred_element_type=f32)  9.4 us
    dot_general x2, matrix products, shards(): jnp.einsum('sf,hf->sh', g_cot[t], wd[:, t], preferred_element_type=f32)  8.61 us
  transfers between devices with their start and end apart: 4, of which 4 were waited for; matrix products, arithmetic and copies ran while one was open for 9% of the time, Pallas kernels for 0%

profile of v6, /device:TPU:32, one launch (start us, length us, event | category | flops | bytes accessed | tf_op | source)
XLA Modules:
  0.0 338.4 jit_solution(15306360421438200320)
XLA Ops:
  7.2 0.8 convert_reduce_fusion
  8.1 0.7 convert_element_type.137
  8.7 0.9 fusion.49
  9.7 1.0 fusion.47
  10.7 0.8 divide_subtract_fusion
  11.4 0.8 convolution_bitcast_fusion.1
  12.3 0.9 fusion.56
  13.2 1.3 fusion.5
  14.5 0.1 slice_bitcast_fusion.4
  14.6 0.2 fusion.58
  14.8 0.1 copy.39
  14.9 0.1 fusion.37
  15.0 0.4 copy.40
  15.4 36.7 %all_to_all.15 = bf16[16,6,3584]{2,1,0:T(8,128)(2,1)S(1)} all-to-all(bf16[16,6,3584]{2,1,0:T(8,128)(2,1)S(1)} %copy.40), channel_id=1, replica_groups=mesh['dp'=8,'expert'=16,'tensor'=2] {'expert'}, dimensions={0} | all-to-all | bytes 1376256 | tf_op jit(solution)/shard_map/all_to_all | solution.py:59
  52.1 0.2 reshape.256
  52.4 0.1 reshape.257
  52.5 0.9 fusion.38
  53.4 0.3 copy.41
  53.8 40.3 %all_to_all.16 = bf16[16,5,3584]{2,1,0:T(8,128)(2,1)S(1)} all-to-all(bf16[16,5,3584]{2,1,0:T(8,128)(2,1)S(1)} %copy.41), channel_id=1, replica_groups=mesh['dp'=8,'expert'=16,'tensor'=2] {'expert'}, dimensions={0} | all-to-all | bytes 1146880 | tf_op jit(solution)/shard_map/all_to_all | solution.py:63
  94.0 0.2 reshape.258
  94.3 0.9 concatenate.45
  95.2 2.3 copy.42
  97.5 0.1 fusion.24
  97.6 29.5 %all-gather.3.cloned.1.call-done = bf16[1408,3584]{1,0:T(8,128)(2,1)} async-done(((bf16[88,3584]{1,0:T(8,128)(2,1)}), bf16[1408,3584]{1,0:T(8,128)(2,1)}) %all-gather.3.cloned.1.call-update) | async-done | bytes 10092560 | tf_op jit(solution)/shard_map/all_gather | solution.py:66
  127.1 2.4 slice-done.3
  129.5 0.1 reshape.263
  129.7 4.3 %fusion.19 = f32[704,256]{1,0:T(8,128)S(1)} fusion(bf16[2,3584,128]{2,1,0:T(8,128)(2,1)} %bitcast.125, bf16[2,3584,128]{2,1,0:T(8,128)(2,1)S(1)} %bitcast.123, bf16[1408,3584]{1,0:T(8,128)(2,1)} %all-gather.3.cloned.1.call-done), kind=kOutput, calls=%fused_computation.30 | convolution fusion | flops 1295515648 | bytes 9437184 | tf_op jit(solution)/shard_map/dot_general | solution.py:80
  134.0 1.3 copy-done.2
  135.3 0.5 copy-done.7
  135.8 0.5 copy-done.8
  136.3 2.3 fusion.27
  138.6 54.6 %all-gather.5.cloned.1.call-done = bf16[1408,3584]{1,0:T(8,128)(2,1)} async-done(((bf16[88,3584]{1,0:T(8,128)(2,1)}), bf16[1408,3584]{1,0:T(8,128)(2,1)}) %all-gather.5.cloned.1.call-update) | async-done | bytes 10092560 | tf_op jit(solution)/shard_map/all_gather | solution.py:68
  193.2 4.0 %fusion.7 = f32[704,128]{1,0:T(8,128)S(1)} fusion(bf16[1408,3584]{1,0:T(8,128)(2,1)} %all-gather.5.cloned.1.call-done, bf16[128,2,3584]{0,2,1:T(8,128)(2,1)S(1)} %bitcast.106), kind=kOutput, calls=%fused_computation.16 | convolution fusion | flops 645922816 | bytes 6324224 | tf_op jit(solution)/shard_map/sf,hf->sh/dot_general | solution.py:85
  197.2 4.6 %multiply_convert_fusion.2 = (bf16[704,128]{1,0:T(8,128)(2,1)S(1)}, bf16[704,128]{1,0:T(8,128)(2,1)}, bf16[704,128]{1,0:T(8,128)(2,1)S(1)}, f32[704,128]{1,0:T(8,128)S(1)}) fusion(f32[704,256]{1,0:T(8,128)S(1)} %copy-done.9, f32[704]{0:T(1024)S(1)} %reshape.263, f32[704,128]{1,0:T(8,128)S(1)} %fusion.7, bf16[128,2,3584]{0,2,1:T(8,128)(2,1)S(1)} %bitcast.107, ...), kind=kOutput, calls=%fused_computation.67 | convolution fusion | flops 647454720 | bytes 7950336 | tf_op jit(solution)/shard_map/sf,hf->sh/dot_general | solution.py:85
  201.8 0.2 fusion.44
  202.0 0.1 reduce_sum.35
  202.2 0.2 scatter.21
  202.4 0.1 broadcast_in_dim.8
  202.5 0.2 copy-done.10
  202.8 9.4 %convolution_convert_fusion = bf16[2,3584,704]{1,2,0:T(8,128)(2,1)} fusion(bf16[2,3584,128]{2,1,0:T(8,128)(2,1)S(1)} %broadcast_in_dim.8, bf16[2,3584,128]{2,1,0:T(8,128)(2,1)} %bitcast.122, bf16[2,3584,128]{2,1,0:T(8,128)(2,1)} %bitcast.126, bf16[704,128]{1,0:T(8,128)(2,1)S(1)} %bitcast.109, bf16[704,128]{1,0:T(8,128)(2,1)S(1)} %copy-done.10, ...), kind=kOutput, calls=%fused_computation | convolution fusion | flops 3898720256 | bytes 16138240 | tf_op jit(solution)/shard_map/sk,tfk->tsf/dot_general | solution.py:132
  212.2 3.4 %convolution_convert_fusion.3 = bf16[128,3584]{1,0:T(8,128)(2,1)S(1)} fusion(bf16[1408,3584]{1,0:T(8,128)(2,1)} %all-gather.5.cloned.1.call-done, bf16[704,128]{1,0:T(8,128)(2,1)S(1)} %get-tuple-element.81, f32[704]{0:T(1024)S(1)} %reshape.263), kind=kOutput, calls=%fused_computation.8 | convolution fusion | flops 646651904 | bytes 6146816 | tf_op jit(solution)/shard_map/dot_general | solution.py:102
  215.6 3.6 %convolution_convert_fusion.2 = bf16[128,3584]{1,0:T(8,128)(2,1)S(1)} fusion(bf16[1408,3584]{1,0:T(8,128)(2,1)} %all-gather.5.cloned.1.call-done, bf16[704,128]{1,0:T(8,128)(2,1)S(1)} %get-tuple-element.81, f32[704]{0:T(1024)S(1)} %reshape.263), kind=kOutput, calls=%fused_computation.7 | convolution fusion | flops 646651904 | bytes 6146816 | tf_op jit(solution)/shard_map/dot_general | solution.py:102
  219.2 4.5 %convolution_convert_fusion.4 = bf16[3584,128]{1,0:T(8,128)(2,1)S(1)} fusion(bf16[704,128]{1,0:T(8,128)(2,1)S(1)} %copy-done.10, bf16[1408,3584]{1,0:T(8,128)(2,1)} %all-gather.3.cloned.1.call-done), kind=kOutput, calls=%fused_computation.9 | convolution fusion | flops 646381568 | bytes 6144000 | tf_op jit(solution)/shard_map/dot_general | solution.py:116
  223.7 1.7 convolution_convert_fusion.5
  225.4 1.7 convolution_convert_fusion.6
  227.1 1.7 convolution_convert_fusion.7
  228.8 1.4 pad_maximum_fusion.3
  230.3 2.1 pad_maximum_fusion.1
  232.3 60.0 %reduce-scatter.2.cloned.1.call-done = bf16[88,3584]{1,0:T(8,128)(2,1)} async-done(((bf16[1408,3584]{1,0:T(8,128)(2,1)}), bf16[88,3584]{1,0:T(8,128)(2,1)}) %reduce-scatter.2.cloned.1.call-update) | async-done | bytes 630800 | tf_op jit(solution)/shard_map/reduce_scatter | solution.py:134
  292.4 0.7 convert_bitcast_fusion.1
  293.1 1.6 collective-permute-start
  294.7 1.1 slice.199
  295.8 0.2 reshape.261
  296.1 0.6 collective-permute-done
  296.6 0.7 broadcast_select_fusion
  297.4 0.1 reshape.280
  297.5 0.2 fusion.36
  297.7 32.1 %all_to_all.17 = bf16[16,6,3584]{2,1,0:T(8,128)(2,1)S(1)} all-to-all(bf16[16,6,3584]{2,1,0:T(8,128)(2,1)S(1)} %fusion.36), channel_id=1, replica_groups=mesh['dp'=8,'expert'=16,'tensor'=2] {'expert'}, dimensions={0} | all-to-all | bytes 1376256 | tf_op jit(solution)/shard_map/all_to_all | solution.py:150
  329.8 0.9 fusion.12
  330.8 0.1 copy.69
  330.9 0.1 copy.61
  331.0 0.1 copy.62
  331.1 0.2 fusion.57
  331.3 0.6 convert_element_type.167
  (42 shorter events, 0.4 us)
Async XLA Ops:
  7.2 7.4 %copy-start = (bf16[8,8]{1,0:T(8,128)(2,1)S(1)}, bf16[8,8]{1,0:T(8,128)(2,1)}, u32[]{:S(2)}) copy-start(bf16[8,8]{1,0:T(8,128)(2,1)} %param.22) | copy-start | bytes 388
  7.2 7.4 %copy-start.5 = (s32[8,8]{1,0:T(8,128)S(1)}, s32[8,8]{1,0:T(8,128)}, u32[]{:S(2)}) copy-start(s32[8,8]{1,0:T(8,128)} %param.23) | copy-start | bytes 772
  7.2 119.9 %all-gather.3.cloned.1.call-start = ((), (), s32[]{:S(2)}) async-start(), calls=%async_computation.4 | async-start | bytes 10723328 | tf_op jit(solution)/shard_map/all_gather | solution.py:66
  53.4 139.8 %all-gather.5.cloned.1.call-start = ((), (), s32[]{:S(2)}) async-start(), calls=%async_computation.5 | async-start | bytes 10723328 | tf_op jit(solution)/shard_map/all_gather | solution.py:68
  53.7 41.5 %copy-start.3 = (bf16[1,128,7168]{2,1,0:T(8,128)(2,1)S(1)}, bf16[1,128,7168]{2,1,0:T(8,128)(2,1)}, u32[]{:S(2)}) copy-start(bf16[1,128,7168]{2,1,0:T(8,128)(2,1)} %param.29) | copy-start | bytes 5505028
  95.2 197.2 %reduce-scatter.2.cloned.1.call-start = ((), (), s32[]{:S(2)}) async-start(), calls=%async_computation.6 | async-start | bytes 10723328 | tf_op jit(solution)/shard_map/reduce_scatter | solution.py:134
  97.6 32.0 %copy-start.6 = (bf16[1,7168,128]{2,1,0:T(8,128)(2,1)S(1)}, bf16[1,7168,128]{2,1,0:T(8,128)(2,1)}, u32[]{:S(2)}) copy-start(bf16[1,7168,128]{2,1,0:T(8,128)(2,1)} %param.28) | copy-start | bytes 5505028
  127.1 2.4 slice-start.3
  129.6 5.6 %copy-start.2 = (bf16[1408,3584]{1,0:T(8,128)(2,1)S(1)}, bf16[1408,3584]{1,0:T(8,128)(2,1)}, u32[]{:S(2)}) copy-start(bf16[1408,3584]{1,0:T(8,128)(2,1)} %all-gather.3.cloned.1.call-done) | copy-start | bytes 30277636
  129.6 6.1 %copy-start.7 = (bf16[1,7168,128]{2,1,0:T(8,128)(2,1)S(1)}, bf16[1,7168,128]{2,1,0:T(8,128)(2,1)}, u32[]{:S(2)}) copy-start(bf16[1,7168,128]{2,1,0:T(8,128)(2,1)} %param.28) | copy-start | bytes 5505028
  129.6 6.6 %copy-start.8 = (bf16[1,7168,128]{2,1,0:T(8,128)(2,1)S(1)}, bf16[1,7168,128]{2,1,0:T(8,128)(2,1)}, u32[]{:S(2)}) copy-start(bf16[1,7168,128]{2,1,0:T(8,128)(2,1)} %param.27) | copy-start | bytes 5505028
  136.3 56.9 %copy-start.4 = (bf16[1,128,7168]{1,2,0:T(8,128)(2,1)S(1)}, bf16[1,128,7168]{1,2,0:T(8,128)(2,1)}, u32[]{:S(2)}) copy-start(bf16[1,128,7168]{1,2,0:T(8,128)(2,1)} %copy.42) | copy-start | bytes 5505028
  193.2 4.0 %copy-start.9 = (f32[704,256]{1,0:T(8,128)S(1)}, f32[704,256]{1,0:T(8,128)}, u32[]{:S(2)}) copy-start(f32[704,256]{1,0:T(8,128)} %fusion.27) | copy-start | bytes 2162692
  201.8 0.9 copy-start.10
  215.6 8.1 %slice-start = ((s8[10092544]{0:T(1024)(128)(4,1)}), s8[4194304]{0:T(1024)(128)(4,1)S(1)}, s32[]{:S(2)}) async-start(s8[10092544]{0:T(1024)(128)(4,1)} %bitcast.99), calls=%async_computation.7 | async-start | bytes 8388608
  215.6 8.1 %slice-start.1 = ((s8[10092544]{0:T(1024)(128)(4,1)}), s8[4194304]{0:T(1024)(128)(4,1)S(1)}, s32[]{:S(2)}) async-start(s8[10092544]{0:T(1024)(128)(4,1)} %bitcast.99), calls=%async_computation.8 | async-start | bytes 8388608
  219.2 4.5 %slice-start.2 = ((s8[10092544]{0:T(1024)(128)(4,1)}), s8[1703936]{0:T(1024)(128)(4,1)S(1)}, s32[]{:S(2)}) async-start(s8[10092544]{0:T(1024)(128)(4,1)} %bitcast.99), calls=%async_computation.9 | async-start | bytes 3407872
  293.1 3.5 %collective-permute-start = (bf16[80]{0:T(256)(128)(2,1)S(1)}, bf16[80]{0:T(256)(128)(2,1)S(1)}, u32[]{:S(2)}, u32[]{:S(2)}) collective-permute-start(bf16[80]{0:T(256)(128)(2,1)S(1)} %convert_bitcast_fusion.1), channel_id=1, source_target_pairs={{0,1},{1,0},{2,3},{3,2},{4,5},{5,4},{6,7},{7,6},{8,9},{9,8},{10,11... | collective-permute-start | bytes 488 | tf_op jit(solution)/shard_map/ppermute | solution.py:142
  295.8 36.0 %copy-start.1 = (bf16[8,8]{1,0:T(8,128)(2,1)S(1)}, bf16[8,8]{1,0:T(8,128)(2,1)}, u32[]{:S(2)}) copy-start(bf16[8,8]{1,0:T(8,128)(2,1)} %param.22) | copy-start | bytes 388
Sparse Core Ops, SparseCore 0:
  53.5 73.5 all-gather.2
  129.5 63.6 all-gather.4
  212.3 80.0 reduce-scatter.1

commit v7 on v6

--- a/solution.py
+++ b/solution.py
@@ -139,8 +139,6 @@
     own_route = (
         own_rows[slots, :slots].astype(f32) + own_rows[slots + 1, :slots].astype(f32)
     ).astype(bf16)
-    partner = lax.ppermute(own_route, "tensor", [(i, i ^ 1) for i in range(tensor_size)])
-    own_route = jnp.where(lax.axis_index("tensor") == 0, own_route, partner)
     route_row = jnp.zeros((experts, 1, features), bf16).at[:, 0, :capacity].set(
         own_route.reshape(experts, capacity)
     )
@@ -153,6 +151,8 @@
     ).astype(bf16)
     per_expert = jnp.einsum("ecr,ec->re", chosen, home[:, capacity, :capacity].astype(f32))
     route_grad = jnp.einsum("rke,re->rk", route_hits, per_expert).astype(bf16)
+    partner = lax.ppermute(route_grad, "tensor", [(i, i ^ 1) for i in range(tensor_size)])
+    route_grad = jnp.where(lax.axis_index("tensor") == 0, route_grad, partner)
     return (input_grad, route_grad, grad_gate[None], grad_up[None], grad_down[None])
 
 

time: 342 us -> 341 us (level)
  blocking collectives: 109 us -> 77 us
  waiting for transfers between devices: 145 us -> 171 us
  starting transfers between devices: 1.74 us -> 9.89 us
    all_to_all x1 -> x0, blocking collectives: 32.1 us -> none  [shards(): lax.all_to_all(back_pack, 'expert', split_axis=0, concat_axis=0, tiled=True)]
    all_to_all x0 -> x1, waiting for transfers between devices: none -> 24.1 us  [shards(): lax.all_to_all(back_pack, 'expert', split_axis=0, concat_axis=0, tiled=True)]
    all_to_all x0 -> x1, starting transfers between devices: none -> 9.68 us  [shards(): lax.all_to_all(back_pack, 'expert', split_axis=0, concat_axis=0, tiled=True)]
  transfers between devices with their start and end apart: 4 -> 5, of which waited for: 4 -> 5; matrix products, arithmetic and copies ran while one was open for 9% -> 9% of each run, Pallas kernels for 0% -> 0%
where the time goes in v7:
time: 341 us
  waiting for transfers between devices  171 us (50%)
  blocking collectives  77 us (23%)
  matrix products  45.7 us (13%)
  between operations  14.1 us (4%)
  local copies, waits for them, and re-layouts  11.9 us (3%)
  other arithmetic  11.3 us (3%)
  starting transfers between devices  9.89 us (3%)
    reduce_scatter x1, waiting for transfers between devices, shards(): lax.psum_scatter(product, ('tensor', 'dp'), scatter_dimension=0, tiled=True)  60 us
    all_gather x1, waiting for transfers between devices, shards(): g_cot = lax.all_gather(cot_rows, ('tensor', 'dp'), axis=0, tiled=True)  54.6 us
    all_to_all x1, blocking collectives, shards(): lax.all_to_all(cot_pack, 'expert', split_axis=0, concat_axis=0, tiled=True)  40.3 us
    all_to_all x1, blocking collectives, shards(): lax.all_to_all(tok_pack, 'expert', split_axis=0, concat_axis=0, tiled=True)  36.7 us
    all_gather x1, waiting for transfers between devices, shards(): g_tok = lax.all_gather(tok_rows, ('tensor', 'dp'), axis=0, tiled=True)  29.5 us
    all_to_all x1, waiting for transfers between devices, shards(): lax.all_to_all(back_pack, 'expert', split_axis=0, concat_axis=0, tiled=True)  24.1 us
    all_to_all x1, starting transfers between devices, shards(): lax.all_to_all(back_pack, 'expert', split_axis=0, concat_axis=0, tiled=True)  9.68 us
    dot_general x1, matrix products, shards(): jnp.einsum('sk,tfk->tsf', lhs, w_out, preferred_element_type=f32)  9.4 us
  transfers between devices with their start and end apart: 5, of which 5 were waited for; matrix products, arithmetic and copies ran while one was open for 9% of the time, Pallas kernels for 0%

profile of v7, /device:TPU:32, one launch (start us, length us, event | category | flops | bytes accessed | tf_op | source)
XLA Modules:
  0.0 340.8 jit_solution(9094497950849691241)
XLA Ops:
  7.2 0.8 convert_reduce_fusion
  8.1 0.7 convert_element_type.161
  8.7 0.9 fusion.49
  9.7 1.0 fusion.47
  10.7 0.8 divide_subtract_fusion
  11.4 0.8 convolution_bitcast_fusion.1
  12.3 0.9 fusion.56
  13.2 1.3 fusion.5
  14.5 0.1 slice_bitcast_fusion.4
  14.6 0.2 fusion.58
  14.8 0.1 copy.39
  14.9 0.1 fusion.37
  15.0 0.4 copy.40
  15.4 36.7 %all_to_all.15 = bf16[16,6,3584]{2,1,0:T(8,128)(2,1)S(1)} all-to-all(bf16[16,6,3584]{2,1,0:T(8,128)(2,1)S(1)} %copy.40), channel_id=1, replica_groups=mesh['dp'=8,'expert'=16,'tensor'=2] {'expert'}, dimensions={0} | all-to-all | bytes 1376256 | tf_op jit(solution)/shard_map/all_to_all | solution.py:59
  52.1 0.2 reshape.281
  52.4 0.1 reshape.282
  52.5 0.9 fusion.38
  53.4 0.3 copy.41
  53.8 40.3 %all_to_all.16 = bf16[16,5,3584]{2,1,0:T(8,128)(2,1)S(1)} all-to-all(bf16[16,5,3584]{2,1,0:T(8,128)(2,1)S(1)} %copy.41), channel_id=1, replica_groups=mesh['dp'=8,'expert'=16,'tensor'=2] {'expert'}, dimensions={0} | all-to-all | bytes 1146880 | tf_op jit(solution)/shard_map/all_to_all | solution.py:63
  94.0 0.2 reshape.283
  94.3 0.9 concatenate.45
  95.2 2.3 copy.42
  97.5 0.1 fusion.24
  97.6 29.5 %all-gather.3.cloned.1.call-done = bf16[1408,3584]{1,0:T(8,128)(2,1)} async-done(((bf16[88,3584]{1,0:T(8,128)(2,1)}), bf16[1408,3584]{1,0:T(8,128)(2,1)}) %all-gather.3.cloned.1.call-update) | async-done | bytes 10092560 | tf_op jit(solution)/shard_map/all_gather | solution.py:66
  127.1 2.4 slice-done.3
  129.5 0.1 reshape.287
  129.7 4.3 %fusion.19 = f32[704,256]{1,0:T(8,128)S(1)} fusion(bf16[2,3584,128]{2,1,0:T(8,128)(2,1)} %bitcast.122, bf16[2,3584,128]{2,1,0:T(8,128)(2,1)S(1)} %bitcast.120, bf16[1408,3584]{1,0:T(8,128)(2,1)} %all-gather.3.cloned.1.call-done), kind=kOutput, calls=%fused_computation.30 | convolution fusion | flops 1295515648 | bytes 9437184 | tf_op jit(solution)/shard_map/dot_general | solution.py:80
  134.0 1.3 copy-done.2
  135.3 0.5 copy-done.7
  135.8 0.5 copy-done.8
  136.3 2.3 fusion.27
  138.6 54.6 %all-gather.5.cloned.1.call-done = bf16[1408,3584]{1,0:T(8,128)(2,1)} async-done(((bf16[88,3584]{1,0:T(8,128)(2,1)}), bf16[1408,3584]{1,0:T(8,128)(2,1)}) %all-gather.5.cloned.1.call-update) | async-done | bytes 10092560 | tf_op jit(solution)/shard_map/all_gather | solution.py:68
  193.2 4.0 %fusion.7 = f32[704,128]{1,0:T(8,128)S(1)} fusion(bf16[1408,3584]{1,0:T(8,128)(2,1)} %all-gather.5.cloned.1.call-done, bf16[128,2,3584]{0,2,1:T(8,128)(2,1)S(1)} %bitcast.102), kind=kOutput, calls=%fused_computation.16 | convolution fusion | flops 645922816 | bytes 6324224 | tf_op jit(solution)/shard_map/sf,hf->sh/dot_general | solution.py:85
  197.2 4.6 %multiply_convert_fusion.2 = (bf16[704,128]{1,0:T(8,128)(2,1)S(1)}, bf16[704,128]{1,0:T(8,128)(2,1)}, bf16[704,128]{1,0:T(8,128)(2,1)S(1)}, f32[704,128]{1,0:T(8,128)S(1)}) fusion(f32[704,256]{1,0:T(8,128)S(1)} %copy-done.9, f32[704]{0:T(1024)S(1)} %reshape.287, f32[704,128]{1,0:T(8,128)S(1)} %fusion.7, bf16[128,2,3584]{0,2,1:T(8,128)(2,1)S(1)} %bitcast.103, ...), kind=kOutput, calls=%fused_computation.67 | convolution fusion | flops 647454720 | bytes 7950336 | tf_op jit(solution)/shard_map/sf,hf->sh/dot_general | solution.py:85
  201.8 0.2 fusion.44
  202.0 0.1 reduce_sum.35
  202.2 0.2 scatter.21
  202.4 0.1 broadcast_in_dim.8
  202.5 0.2 copy-done.10
  202.8 9.4 %convolution_convert_fusion = bf16[2,3584,704]{1,2,0:T(8,128)(2,1)} fusion(bf16[2,3584,128]{2,1,0:T(8,128)(2,1)S(1)} %broadcast_in_dim.8, bf16[2,3584,128]{2,1,0:T(8,128)(2,1)} %bitcast.119, bf16[2,3584,128]{2,1,0:T(8,128)(2,1)} %bitcast.123, bf16[704,128]{1,0:T(8,128)(2,1)S(1)} %bitcast.105, bf16[704,128]{1,0:T(8,128)(2,1)S(1)} %copy-done.10, ...), kind=kOutput, calls=%fused_computation | convolution fusion | flops 3898720256 | bytes 16138240 | tf_op jit(solution)/shard_map/sk,tfk->tsf/dot_general | solution.py:132
  212.2 3.4 %convolution_convert_fusion.3 = bf16[128,3584]{1,0:T(8,128)(2,1)S(1)} fusion(bf16[1408,3584]{1,0:T(8,128)(2,1)} %all-gather.5.cloned.1.call-done, bf16[704,128]{1,0:T(8,128)(2,1)S(1)} %get-tuple-element.81, f32[704]{0:T(1024)S(1)} %reshape.287), kind=kOutput, calls=%fused_computation.8 | convolution fusion | flops 646651904 | bytes 6146816 | tf_op jit(solution)/shard_map/dot_general | solution.py:102
  215.6 3.6 %convolution_convert_fusion.2 = bf16[128,3584]{1,0:T(8,128)(2,1)S(1)} fusion(bf16[1408,3584]{1,0:T(8,128)(2,1)} %all-gather.5.cloned.1.call-done, bf16[704,128]{1,0:T(8,128)(2,1)S(1)} %get-tuple-element.81, f32[704]{0:T(1024)S(1)} %reshape.287), kind=kOutput, calls=%fused_computation.7 | convolution fusion | flops 646651904 | bytes 6146816 | tf_op jit(solution)/shard_map/dot_general | solution.py:102
  219.2 4.5 %convolution_convert_fusion.4 = bf16[3584,128]{1,0:T(8,128)(2,1)S(1)} fusion(bf16[704,128]{1,0:T(8,128)(2,1)S(1)} %copy-done.10, bf16[1408,3584]{1,0:T(8,128)(2,1)} %all-gather.3.cloned.1.call-done), kind=kOutput, calls=%fused_computation.9 | convolution fusion | flops 646381568 | bytes 6144000 | tf_op jit(solution)/shard_map/dot_general | solution.py:116
  223.7 1.7 convolution_convert_fusion.5
  225.4 1.7 convolution_convert_fusion.6
  227.1 1.7 convolution_convert_fusion.7
  228.8 1.4 pad_maximum_fusion.3
  230.3 2.1 pad_maximum_fusion.1
  232.3 60.0 %reduce-scatter.2.cloned.1.call-done = bf16[88,3584]{1,0:T(8,128)(2,1)} async-done(((bf16[1408,3584]{1,0:T(8,128)(2,1)}), bf16[88,3584]{1,0:T(8,128)(2,1)}) %reduce-scatter.2.cloned.1.call-update) | async-done | bytes 630800 | tf_op jit(solution)/shard_map/reduce_scatter | solution.py:134
  292.4 1.1 slice.199
  293.5 0.8 convert_reduce_fusion.1
  294.2 0.2 reshape.286
  294.5 0.1 convert_element_type.193
  294.6 1.2 fusion.36
  295.7 9.7 %all-to-all-start.2 = ((bf16[16,6,3584]{2,1,0:T(8,128)(2,1)}), bf16[16,6,3584]{2,1,0:T(8,128)(2,1)S(1)}, u32[]{:S(2)}, u32[]{:S(2)}) async-start(bf16[16,6,3584]{2,1,0:T(8,128)(2,1)} %fusion.36), calls=%async_computation.3 | async-start | bytes 1835008 | tf_op jit(solution)/shard_map/all_to_all | solution.py:148
  305.4 24.1 %all-to-all-done.2 = bf16[16,6,3584]{2,1,0:T(8,128)(2,1)S(1)} async-done(((bf16[16,6,3584]{2,1,0:T(8,128)(2,1)}), bf16[16,6,3584]{2,1,0:T(8,128)(2,1)S(1)}, u32[]{:S(2)}, u32[]{:S(2)}) %all-to-all-start.2) | async-done | bytes 688160 | tf_op jit(solution)/shard_map/all_to_all | solution.py:148
  329.5 0.1 copy.69
  329.6 0.1 copy.61
  329.7 0.1 copy.62
  329.8 0.2 fusion.57
  330.0 0.1 collective-permute-start
  330.1 0.9 fusion.12
  331.1 2.6 collective-permute-done
  333.7 0.6 broadcast_select_fusion
  (43 shorter events, 0.4 us)
Async XLA Ops:
  7.2 7.4 %copy-start = (bf16[8,8]{1,0:T(8,128)(2,1)S(1)}, bf16[8,8]{1,0:T(8,128)(2,1)}, u32[]{:S(2)}) copy-start(bf16[8,8]{1,0:T(8,128)(2,1)} %param.22) | copy-start | bytes 388
  7.2 7.4 %copy-start.5 = (s32[8,8]{1,0:T(8,128)S(1)}, s32[8,8]{1,0:T(8,128)}, u32[]{:S(2)}) copy-start(s32[8,8]{1,0:T(8,128)} %param.23) | copy-start | bytes 772
  7.2 119.9 %all-gather.3.cloned.1.call-start = ((), (), s32[]{:S(2)}) async-start(), calls=%async_computation.4 | async-start | bytes 10723328 | tf_op jit(solution)/shard_map/all_gather | solution.py:66
  53.4 139.8 %all-gather.5.cloned.1.call-start = ((), (), s32[]{:S(2)}) async-start(), calls=%async_computation.5 | async-start | bytes 10723328 | tf_op jit(solution)/shard_map/all_gather | solution.py:68
  53.7 41.5 %copy-start.3 = (bf16[1,128,7168]{2,1,0:T(8,128)(2,1)S(1)}, bf16[1,128,7168]{2,1,0:T(8,128)(2,1)}, u32[]{:S(2)}) copy-start(bf16[1,128,7168]{2,1,0:T(8,128)(2,1)} %param.29) | copy-start | bytes 5505028
  95.2 197.2 %reduce-scatter.2.cloned.1.call-start = ((), (), s32[]{:S(2)}) async-start(), calls=%async_computation.6 | async-start | bytes 10723328 | tf_op jit(solution)/shard_map/reduce_scatter | solution.py:134
  97.6 32.0 %copy-start.6 = (bf16[1,7168,128]{2,1,0:T(8,128)(2,1)S(1)}, bf16[1,7168,128]{2,1,0:T(8,128)(2,1)}, u32[]{:S(2)}) copy-start(bf16[1,7168,128]{2,1,0:T(8,128)(2,1)} %param.28) | copy-start | bytes 5505028
  127.1 2.4 slice-start.3
  129.6 5.6 %copy-start.2 = (bf16[1408,3584]{1,0:T(8,128)(2,1)S(1)}, bf16[1408,3584]{1,0:T(8,128)(2,1)}, u32[]{:S(2)}) copy-start(bf16[1408,3584]{1,0:T(8,128)(2,1)} %all-gather.3.cloned.1.call-done) | copy-start | bytes 30277636
  129.6 6.1 %copy-start.7 = (bf16[1,7168,128]{2,1,0:T(8,128)(2,1)S(1)}, bf16[1,7168,128]{2,1,0:T(8,128)(2,1)}, u32[]{:S(2)}) copy-start(bf16[1,7168,128]{2,1,0:T(8,128)(2,1)} %param.28) | copy-start | bytes 5505028
  129.6 6.6 %copy-start.8 = (bf16[1,7168,128]{2,1,0:T(8,128)(2,1)S(1)}, bf16[1,7168,128]{2,1,0:T(8,128)(2,1)}, u32[]{:S(2)}) copy-start(bf16[1,7168,128]{2,1,0:T(8,128)(2,1)} %param.27) | copy-start | bytes 5505028
  136.3 56.9 %copy-start.4 = (bf16[1,128,7168]{1,2,0:T(8,128)(2,1)S(1)}, bf16[1,128,7168]{1,2,0:T(8,128)(2,1)}, u32[]{:S(2)}) copy-start(bf16[1,128,7168]{1,2,0:T(8,128)(2,1)} %copy.42) | copy-start | bytes 5505028
  193.2 4.0 %copy-start.9 = (f32[704,256]{1,0:T(8,128)S(1)}, f32[704,256]{1,0:T(8,128)}, u32[]{:S(2)}) copy-start(f32[704,256]{1,0:T(8,128)} %fusion.27) | copy-start | bytes 2162692
  201.8 0.9 copy-start.10
  215.6 8.1 %slice-start = ((s8[10092544]{0:T(1024)(128)(4,1)}), s8[4194304]{0:T(1024)(128)(4,1)S(1)}, s32[]{:S(2)}) async-start(s8[10092544]{0:T(1024)(128)(4,1)} %bitcast.95), calls=%async_computation.7 | async-start | bytes 8388608
  215.6 8.1 %slice-start.1 = ((s8[10092544]{0:T(1024)(128)(4,1)}), s8[4194304]{0:T(1024)(128)(4,1)S(1)}, s32[]{:S(2)}) async-start(s8[10092544]{0:T(1024)(128)(4,1)} %bitcast.95), calls=%async_computation.8 | async-start | bytes 8388608
  219.2 4.5 %slice-start.2 = ((s8[10092544]{0:T(1024)(128)(4,1)}), s8[1703936]{0:T(1024)(128)(4,1)S(1)}, s32[]{:S(2)}) async-start(s8[10092544]{0:T(1024)(128)(4,1)} %bitcast.95), calls=%async_computation.9 | async-start | bytes 3407872
  294.2 40.0 %copy-start.1 = (bf16[8,8]{1,0:T(8,128)(2,1)S(1)}, bf16[8,8]{1,0:T(8,128)(2,1)}, u32[]{:S(2)}) copy-start(bf16[8,8]{1,0:T(8,128)(2,1)} %param.22) | copy-start | bytes 388
  295.7 33.7 %all-to-all-start.2 = ((bf16[16,6,3584]{2,1,0:T(8,128)(2,1)}), bf16[16,6,3584]{2,1,0:T(8,128)(2,1)S(1)}, u32[]{:S(2)}, u32[]{:S(2)}) async-start(bf16[16,6,3584]{2,1,0:T(8,128)(2,1)} %fusion.36), calls=%async_computation.3 | async-start | bytes 1835008 | tf_op jit(solution)/shard_map/all_to_all | solution.py:148
  330.0 3.7 %collective-permute-start = (bf16[8,8]{1,0:T(8,128)(2,1)S(1)}, bf16[8,8]{1,0:T(8,128)(2,1)S(1)}, u32[]{:S(2)}, u32[]{:S(2)}) collective-permute-start(bf16[8,8]{1,0:T(8,128)(2,1)S(1)} %convert_element_type.191), channel_id=1, source_target_pairs={{0,1},{1,0},{2,3},{3,2},{4,5},{5,4},{6,7},{7,6},{8,9},{9,8},{10,11... | collective-permute-start | bytes 392 | tf_op jit(solution)/shard_map/ppermute | solution.py:154
Sparse Core Ops, SparseCore 0:
  53.5 73.5 all-gather.2
  129.5 63.6 all-gather.4
  212.3 80.0 reduce-scatter.1

commit v8 on v6

--- a/solution.py
+++ b/solution.py
@@ -81,10 +81,7 @@
     )
     gate = gate_up[:, :hidden_width]
     up_part = gate_up[:, hidden_width:]
-    back_hidden = sum(
-        jnp.einsum("sf,hf->sh", g_cot[t], wd[:, t], preferred_element_type=f32)
-        for t in range(tensor_size)
-    )
+    back_hidden = jnp.einsum("tsf,htf->sh", g_cot, wd, preferred_element_type=f32)
 
     sigmoid_gate = jax.nn.sigmoid(gate)
     active = gate * sigmoid_gate

time: 342 us -> 340 us (level)
    dot_general x2 -> x1, matrix products: 8.61 us -> 6.77 us  [shards(): jnp.einsum('tsf,htf->sh', g_cot, wd, preferred_element_type=f32)]
where the time goes in v8:
time: 340 us; the launch traced here: 337 us
  waiting for transfers between devices  145 us (43%)
  blocking collectives  109 us (32%)
  matrix products  43.9 us (13%)
  between operations  14.1 us (4%)
  local copies, waits for them, and re-layouts  12.2 us (4%)
  other arithmetic  11.1 us (3%)
    reduce_scatter x1, waiting for transfers between devices, shards(): lax.psum_scatter(product, ('tensor', 'dp'), scatter_dimension=0, tiled=True)  60.2 us
    all_gather x1, waiting for transfers between devices, shards(): g_cot = lax.all_gather(cot_rows, ('tensor', 'dp'), axis=0, tiled=True)  54.6 us
    all_to_all x1, blocking collectives, shards(): lax.all_to_all(cot_pack, 'expert', split_axis=0, concat_axis=0, tiled=True)  40.3 us
    all_to_all x1, blocking collectives, shards(): lax.all_to_all(tok_pack, 'expert', split_axis=0, concat_axis=0, tiled=True)  36.5 us
    all_to_all x1, blocking collectives, shards(): lax.all_to_all(back_pack, 'expert', split_axis=0, concat_axis=0, tiled=True)  32.3 us
    all_gather x1, waiting for transfers between devices, shards(): g_tok = lax.all_gather(tok_rows, ('tensor', 'dp'), axis=0, tiled=True)  29 us
    dot_general x1, matrix products, shards(): jnp.einsum('sk,tfk->tsf', lhs, w_out, preferred_element_type=f32)  9.44 us
    dot_general x2, matrix products, shards(): jnp.dot(weighted.T, g_cot[t], preferred_element_type=f32).astype(bf16)  7 us
  transfers between devices with their start and end apart: 4, of which 4 were waited for; matrix products, arithmetic and copies ran while one was open for 9% of the time, Pallas kernels for 0%

profile of v8, /device:TPU:32, one launch (start us, length us, event | category | flops | bytes accessed | tf_op | source)
XLA Modules:
  0.0 336.5 jit_solution(15449962634105801400)
XLA Ops:
  7.2 0.8 convert_reduce_fusion
  8.0 0.7 convert_element_type.137
  8.7 0.9 fusion.55
  9.7 1.0 fusion.53
  10.7 0.8 divide_subtract_fusion
  11.4 0.8 convolution_bitcast_fusion.1
  12.3 0.9 fusion.62
  13.2 1.3 fusion.15
  14.5 0.1 slice_bitcast_fusion
  14.6 0.2 fusion.64
  14.8 0.1 copy.31
  14.9 0.1 fusion.43
  15.0 0.4 copy.32
  15.4 36.5 %all_to_all.15 = bf16[16,6,3584]{2,1,0:T(8,128)(2,1)S(1)} all-to-all(bf16[16,6,3584]{2,1,0:T(8,128)(2,1)S(1)} %copy.32), channel_id=1, replica_groups=mesh['dp'=8,'expert'=16,'tensor'=2] {'expert'}, dimensions={0} | all-to-all | bytes 1376256 | tf_op jit(solution)/shard_map/all_to_all | solution.py:59
  51.9 0.2 reshape.258
  52.2 0.1 reshape.259
  52.3 0.9 fusion.44
  53.2 0.3 copy.33
  53.6 40.3 %all_to_all.16 = bf16[16,5,3584]{2,1,0:T(8,128)(2,1)S(1)} all-to-all(bf16[16,5,3584]{2,1,0:T(8,128)(2,1)S(1)} %copy.33), channel_id=1, replica_groups=mesh['dp'=8,'expert'=16,'tensor'=2] {'expert'}, dimensions={0} | all-to-all | bytes 1146880 | tf_op jit(solution)/shard_map/all_to_all | solution.py:63
  93.8 0.2 reshape.260
  94.1 0.9 concatenate.45
  95.0 0.0 reduce-scatter.2.cloned.1.call-start
  95.0 0.6 copy-done.3
  95.6 2.3 reshape_squeeze.17
  97.8 0.1 fusion.30
  97.9 29.0 %all-gather.3.cloned.1.call-done = bf16[1408,3584]{1,0:T(8,128)(2,1)} async-done(((bf16[88,3584]{1,0:T(8,128)(2,1)}), bf16[1408,3584]{1,0:T(8,128)(2,1)}) %all-gather.3.cloned.1.call-update) | async-done | bytes 10092560 | tf_op jit(solution)/shard_map/all_gather | solution.py:66
  126.9 2.4 slice-done.3
  129.4 0.1 reshape.266
  129.5 4.3 %fusion.23 = f32[704,256]{1,0:T(8,128)S(1)} fusion(bf16[2,3584,128]{2,1,0:T(8,128)(2,1)} %bitcast.117, bf16[2,3584,128]{2,1,0:T(8,128)(2,1)S(1)} %bitcast.115, bf16[1408,3584]{1,0:T(8,128)(2,1)} %all-gather.3.cloned.1.call-done), kind=kOutput, calls=%fused_computation.28 | convolution fusion | flops 1295515648 | bytes 9437184 | tf_op jit(solution)/shard_map/dot_general | solution.py:80
  133.8 1.3 copy-done.2
  135.1 0.5 copy-done.7
  135.6 0.5 copy-done.8
  136.1 2.3 fusion.33
  138.5 54.6 %all-gather.5.cloned.1.call-done = bf16[1408,3584]{1,0:T(8,128)(2,1)} async-done(((bf16[88,3584]{1,0:T(8,128)(2,1)}), bf16[1408,3584]{1,0:T(8,128)(2,1)}) %all-gather.5.cloned.1.call-update) | async-done | bytes 10092560 | tf_op jit(solution)/shard_map/all_gather | solution.py:68
  193.0 6.8 %multiply_convert_fusion.2 = (bf16[704,128]{1,0:T(8,128)(2,1)S(1)}, bf16[704,128]{1,0:T(8,128)(2,1)S(1)}, bf16[704,128]{1,0:T(8,128)(2,1)S(1)}, f32[704,128]{1,0:T(8,128)S(1)}) fusion(f32[704,256]{1,0:T(8,128)} %fusion.33, f32[704]{0:T(1024)S(1)} %reshape.266, bf16[2,704,3584]{2,1,0:T(8,128)(2,1)} %bitcast.92, bf16[128,2,3584]{2,1,0:T(2,128)(2,1)S(1)} %copy-done.4), kind=kOutput, calls=%fused_computation.65 | convolution fusion | flops 1293287424 | bytes 13552384 | tf_op jit(solution)/shard_map/tsf,htf->sh/dot_general | solution.py:84
  199.8 0.2 fusion.50
  200.0 0.1 reduce_sum.35
  200.2 0.2 scatter.21
  200.4 0.1 broadcast_in_dim.8
  200.5 9.4 %convolution_convert_fusion = bf16[2,3584,704]{1,2,0:T(8,128)(2,1)} fusion(bf16[2,3584,128]{2,1,0:T(8,128)(2,1)S(1)} %broadcast_in_dim.8, bf16[2,3584,128]{2,1,0:T(8,128)(2,1)} %bitcast.114, bf16[2,3584,128]{2,1,0:T(8,128)(2,1)} %bitcast.118, bf16[704,128]{1,0:T(8,128)(2,1)S(1)} %bitcast.101, bf16[704,128]{1,0:T(8,128)(2,1)S(1)} %get-tuple-element.80, ...), kind=kOutput, calls=%fused_computation | convolution fusion | flops 3898720256 | bytes 16138240 | tf_op jit(solution)/shard_map/sk,tfk->tsf/dot_general | solution.py:129
  210.0 3.4 %fusion.9 = bf16[128,3584]{1,0:T(8,128)(2,1)S(1)} fusion(bf16[1408,3584]{1,0:T(8,128)(2,1)} %all-gather.5.cloned.1.call-done, bf16[704,128]{1,0:T(8,128)(2,1)S(1)} %get-tuple-element.81, f32[704]{0:T(1024)S(1)} %reshape.266), kind=kOutput, calls=%fused_computation.11 | convolution fusion | flops 646651904 | bytes 6146816 | tf_op jit(solution)/shard_map/dot_general | solution.py:99
  213.4 3.6 %fusion.12 = bf16[128,3584]{1,0:T(8,128)(2,1)S(1)} fusion(bf16[1408,3584]{1,0:T(8,128)(2,1)} %all-gather.5.cloned.1.call-done, bf16[704,128]{1,0:T(8,128)(2,1)S(1)} %get-tuple-element.81, f32[704]{0:T(1024)S(1)} %reshape.266), kind=kOutput, calls=%fused_computation.12 | convolution fusion | flops 646651904 | bytes 6146816 | tf_op jit(solution)/shard_map/dot_general | solution.py:99
  217.0 4.5 %convolution_convert_fusion.2 = bf16[3584,128]{1,0:T(8,128)(2,1)S(1)} fusion(bf16[704,128]{1,0:T(8,128)(2,1)S(1)} %get-tuple-element.80, bf16[1408,3584]{1,0:T(8,128)(2,1)} %all-gather.3.cloned.1.call-done), kind=kOutput, calls=%fused_computation.13 | convolution fusion | flops 646381568 | bytes 6144000 | tf_op jit(solution)/shard_map/dot_general | solution.py:113
  221.6 1.7 convolution_convert_fusion.3
  223.3 1.7 convolution_convert_fusion.4
  225.0 1.7 convolution_convert_fusion.5
  226.7 1.4 pad_maximum_fusion.3
  228.1 2.1 pad_maximum_fusion.1
  230.2 60.2 %reduce-scatter.2.cloned.1.call-done = bf16[88,3584]{1,0:T(8,128)(2,1)} async-done(((bf16[1408,3584]{1,0:T(8,128)(2,1)}), bf16[88,3584]{1,0:T(8,128)(2,1)}) %reduce-scatter.2.cloned.1.call-update) | async-done | bytes 630800 | tf_op jit(solution)/shard_map/reduce_scatter | solution.py:131
  290.3 0.7 convert_bitcast_fusion.1
  291.1 1.5 collective-permute-start
  292.6 1.1 slice.189
  293.7 0.2 reshape.264
  293.9 0.7 collective-permute-done
  294.6 0.7 broadcast_select_fusion
  295.4 0.1 reshape.284
  295.5 0.2 fusion.42
  295.7 32.3 %all_to_all.17 = bf16[16,6,3584]{2,1,0:T(8,128)(2,1)S(1)} all-to-all(bf16[16,6,3584]{2,1,0:T(8,128)(2,1)S(1)} %fusion.42), channel_id=1, replica_groups=mesh['dp'=8,'expert'=16,'tensor'=2] {'expert'}, dimensions={0} | all-to-all | bytes 1376256 | tf_op jit(solution)/shard_map/all_to_all | solution.py:147
  328.0 0.9 fusion.16
  328.9 0.1 copy.59
  329.0 0.1 copy.51
  329.1 0.1 copy.52
  329.2 0.2 fusion.63
  329.4 0.6 convert_element_type.167
  (37 shorter events, 0.4 us)
Async XLA Ops:
  7.2 7.4 %copy-start = (bf16[8,8]{1,0:T(8,128)(2,1)S(1)}, bf16[8,8]{1,0:T(8,128)(2,1)}, u32[]{:S(2)}) copy-start(bf16[8,8]{1,0:T(8,128)(2,1)} %param.22) | copy-start | bytes 388
  7.2 119.8 %all-gather.3.cloned.1.call-start = ((), (), s32[]{:S(2)}) async-start(), calls=%async_computation.4 | async-start | bytes 10723328 | tf_op jit(solution)/shard_map/all_gather | solution.py:66
  12.3 2.3 copy-start.5
  53.2 139.9 %all-gather.5.cloned.1.call-start = ((), (), s32[]{:S(2)}) async-start(), calls=%async_computation.5 | async-start | bytes 10723328 | tf_op jit(solution)/shard_map/all_gather | solution.py:68
  93.8 1.8 copy-start.3
  95.0 195.4 %reduce-scatter.2.cloned.1.call-start = ((), (), s32[]{:S(2)}) async-start(), calls=%async_computation.6 | async-start | bytes 10723328 | tf_op jit(solution)/shard_map/reduce_scatter | solution.py:131
  97.9 31.6 %copy-start.6 = (bf16[1,7168,128]{2,1,0:T(8,128)(2,1)S(1)}, bf16[1,7168,128]{2,1,0:T(8,128)(2,1)}, u32[]{:S(2)}) copy-start(bf16[1,7168,128]{2,1,0:T(8,128)(2,1)} %param.28) | copy-start | bytes 5505028
  126.9 2.4 slice-start.3
  129.5 5.6 %copy-start.2 = (bf16[1408,3584]{1,0:T(8,128)(2,1)S(1)}, bf16[1408,3584]{1,0:T(8,128)(2,1)}, u32[]{:S(2)}) copy-start(bf16[1408,3584]{1,0:T(8,128)(2,1)} %all-gather.3.cloned.1.call-done) | copy-start | bytes 30277636
  129.5 6.1 %copy-start.7 = (bf16[1,7168,128]{2,1,0:T(8,128)(2,1)S(1)}, bf16[1,7168,128]{2,1,0:T(8,128)(2,1)}, u32[]{:S(2)}) copy-start(bf16[1,7168,128]{2,1,0:T(8,128)(2,1)} %param.28) | copy-start | bytes 5505028
  129.5 6.6 %copy-start.8 = (bf16[1,7168,128]{2,1,0:T(8,128)(2,1)S(1)}, bf16[1,7168,128]{2,1,0:T(8,128)(2,1)}, u32[]{:S(2)}) copy-start(bf16[1,7168,128]{2,1,0:T(8,128)(2,1)} %param.27) | copy-start | bytes 5505028
  136.1 56.9 %copy-start.4 = (bf16[128,2,3584]{2,1,0:T(2,128)(2,1)S(1)}, bf16[128,2,3584]{2,1,0:T(2,128)(2,1)}, u32[]{:S(2)}) copy-start(bf16[128,2,3584]{2,1,0:T(2,128)(2,1)} %reshape_squeeze.17) | copy-start | bytes 5505028
  213.4 8.1 %slice-start = ((s8[10092544]{0:T(1024)(128)(4,1)}), s8[4194304]{0:T(1024)(128)(4,1)S(1)}, s32[]{:S(2)}) async-start(s8[10092544]{0:T(1024)(128)(4,1)} %bitcast.93), calls=%async_computation.7 | async-start | bytes 8388608
  213.4 8.1 %slice-start.1 = ((s8[10092544]{0:T(1024)(128)(4,1)}), s8[4194304]{0:T(1024)(128)(4,1)S(1)}, s32[]{:S(2)}) async-start(s8[10092544]{0:T(1024)(128)(4,1)} %bitcast.93), calls=%async_computation.8 | async-start | bytes 8388608
  217.0 4.5 %slice-start.2 = ((s8[10092544]{0:T(1024)(128)(4,1)}), s8[1703936]{0:T(1024)(128)(4,1)S(1)}, s32[]{:S(2)}) async-start(s8[10092544]{0:T(1024)(128)(4,1)} %bitcast.93), calls=%async_computation.9 | async-start | bytes 3407872
  291.1 3.5 %collective-permute-start = (bf16[80]{0:T(256)(128)(2,1)S(1)}, bf16[80]{0:T(256)(128)(2,1)S(1)}, u32[]{:S(2)}, u32[]{:S(2)}) collective-permute-start(bf16[80]{0:T(256)(128)(2,1)S(1)} %convert_bitcast_fusion.1), channel_id=1, source_target_pairs={{0,1},{1,0},{2,3},{3,2},{4,5},{5,4},{6,7},{7,6},{8,9},{9,8},{10,11... | collective-permute-start | bytes 488 | tf_op jit(solution)/shard_map/ppermute | solution.py:139
  295.4 34.6 %copy-start.1 = (bf16[8,8]{1,0:T(8,128)(2,1)S(1)}, bf16[8,8]{1,0:T(8,128)(2,1)}, u32[]{:S(2)}) copy-start(bf16[8,8]{1,0:T(8,128)(2,1)} %param.22) | copy-start | bytes 388
Sparse Core Ops, SparseCore 0:
  53.3 73.5 all-gather.2
  129.4 63.6 all-gather.4
  210.1 80.1 reduce-scatter.1
